TPU v7x, 512 devices: a whole 4x8x8 slice. The times are simulated.
512 devices in a mesh: ep: 128 (over y, z, core), dp: 4 (over x).
Axes of the slice: x: 4, y: 8, z: 8, core: 2. Of those that a mesh axis runs over, the one named last changes fastest.
Arguments:
- tokens: bfloat16 [2, 2048, 3584], P(None, ('ep', 'dp')), may hold values from -6 to 6
- routing: int32 [2, 2048, 8], P(None, 'ep'), may hold values from 0 to 127, all different within a row; in each aligned block of 16 rows (0 to 15, 16 to 31, ..., all dimensions but the last counted through in order) at most 2 rows name the same one
- gate_values: float32 [2, 2048, 8], P(None, 'ep'), may hold values from 0.05 to 0.5
- held_weight: bfloat16 [128, 3584, 1024], P('ep', None, 'dp'), may hold values from -0.09375 to 0.09375
- scale_table: float32 [128, 28, 8], P(None, None, 'dp'), may hold values from 0.25 to 4
- old_expert: int32 [128], replicated, may hold values from 0 to 127, as said below
- new_expert: int32 [128], replicated, may hold values from 0 to 127, as said below
Outputs:
- combined: bfloat16 [2, 2048, 1024], P(None, 'ep', 'dp')
- moved_weight: bfloat16 [128, 3584, 1024], P('ep', None, 'dp')
Inputs may be any that keep to these rules, and one draw needn't show every extreme that they name: `routing`: each row names 8 different experts; in each aligned block of 16 token rows of a step no expert is named by more than 2 rows. `old_expert`: A permutation of the experts over the slots. `new_expert`: A permutation of the experts over the slots; it equals old_expert except at exactly 32 slots, whose experts are permuted among themselves so that each of them changes.
All inputs are finite; a program needn't handle non-finite values.
Results may differ from a plain program's by a relative error of at most 0.0039.
Values may be sent and summed in bfloat16 or wider, within the bound.
No kernel may reach another device: no remote copies, remote signals or barrier semaphores. Data moves between devices by JAX's collectives and lax.ppermute only.
A program may use at most 64 MiB of HBM per device.

v0:
```python
import jax
import jax.numpy as jnp
from jax import lax
from jax.sharding import PartitionSpec as P


def inverse_place(expert_at):
    count = expert_at.shape[0]
    labels = jnp.arange(count, dtype=jnp.int32)
    match = expert_at[None, :] == labels[:, None]
    return jnp.sum(jnp.where(match, labels[None, :], 0), axis=1)


def source_slots(old_expert, new_expert):
    labels = jnp.arange(old_expert.shape[0], dtype=jnp.int32)
    match = old_expert[None, :] == new_expert[:, None]
    return jnp.sum(jnp.where(match, labels[None, :], 0), axis=1)


def scaled_product(token_rows, weight_block, scales):
    row_blocks = scales.shape[0]
    block_rows = weight_block.shape[0] // row_blocks
    partial_value = jnp.einsum(
        "rbi,bif->rbf",
        token_rows.reshape(token_rows.shape[0], row_blocks, block_rows),
        weight_block.reshape(row_blocks, block_rows, weight_block.shape[1]),
        preferred_element_type=jnp.float32,
    )
    widened = jnp.repeat(scales, weight_block.shape[1] // scales.shape[1], axis=1)
    return jnp.sum(partial_value * widened[None, :, :], axis=1)


def expert_service(weight_block, scales):

    def serve_rows(arrived):

        def one_slot(slot_rows):
            return jax.nn.silu(scaled_product(slot_rows, weight_block, scales)).astype(jnp.bfloat16)

        activated = lax.map(one_slot, arrived)
        return lax.all_to_all(activated, "ep", split_axis=1, concat_axis=1, tiled=True)

    return serve_rows


def route_pairs(routing, expert_at, peers):
    pair_ids = routing.reshape(-1)
    labels = jnp.arange(peers, dtype=jnp.int32)
    onehot = (pair_ids[:, None] == labels[None, :]).astype(jnp.int32)
    before = jnp.cumsum(onehot, axis=0) - onehot
    slot_rank = jnp.sum(before * onehot, axis=1)
    owners = jnp.sum(onehot * inverse_place(expert_at)[None, :], axis=1)
    return slot_rank * peers + owners


def shards(tokens, routing, gate_values, held_weight, scale_table, old_expert, new_expert):
    peers = lax.axis_size("ep")
    my_slot = lax.axis_index("ep")
    group_size = routing.shape[1]
    top_count = routing.shape[2]
    capacity = min(group_size, max(2, 2 * group_size * top_count // peers))
    hidden_width = held_weight.shape[2]
    old_block = held_weight[0]
    sources = source_slots(old_expert, new_expert)
    pieces = old_block.reshape(peers, old_block.shape[0] // peers, hidden_width)
    new_block = lax.all_to_all(
        jnp.take(
            lax.all_to_all(pieces, "ep", split_axis=0, concat_axis=0, tiled=True), sources, axis=0
        ),
        "ep",
        split_axis=0,
        concat_axis=0,
        tiled=True,
    ).reshape(old_block.shape)
    first_serve = (new_block, new_expert)
    serve_plans = [first_serve] + [(new_block, new_expert)] * (tokens.shape[0] - 1)
    grouped = lax.all_gather(tokens, "dp", axis=1, tiled=True)
    columns = grouped.shape[2]
    combined_steps = []
    for decode_step in range(tokens.shape[0]):
        weight_block, expert_at = serve_plans[decode_step]
        scales = scale_table[expert_at[my_slot]]
        target = route_pairs(routing[decode_step], expert_at, peers)
        repeated = jnp.repeat(grouped[decode_step], top_count, axis=0)
        send_buffer = jnp.zeros((capacity * peers, columns), grouped.dtype).at[target].set(repeated)
        send_buffer = send_buffer.reshape(capacity, peers, columns)
        serve_rows = expert_service(weight_block, scales)
        returned = serve_rows(
            lax.all_to_all(send_buffer, "ep", split_axis=1, concat_axis=1, tiled=True)
        )
        activated = returned.reshape(capacity * peers, hidden_width)[target].astype(jnp.float32)
        activated = activated.reshape(group_size, top_count, hidden_width)
        weighted = jnp.sum(gate_values[decode_step][:, :, None] * activated, axis=1)
        combined_steps.append(weighted.astype(jnp.bfloat16))
    return (jnp.stack(combined_steps), new_block[None])


def solution(mesh):
    placed = (
        P(None, ("ep", "dp"), None),
        P(None, "ep", None),
        P(None, "ep", None),
        P("ep", None, "dp"),
        P(None, None, "dp"),
        P(),
        P(),
    )
    return jax.shard_map(
        shards,
        mesh=mesh,
        in_specs=placed,
        out_specs=(P(None, "ep", "dp"), P("ep", None, "dp")),
        check_vma=False,
    )
```

profile of v0, /device:TPU:1, one launch (start us, length us, event | category | flops | bytes accessed | tf_op | source)
XLA Modules:
  0.0 315.5 jit_solution(4355905081281846887)
XLA Ops:
  0.6 0.7 fusion.26
  2.2 0.9 copy.58
  3.1 10.5 %all_gather.3 = bf16[2,16,3584]{2,0,1:T(2,128)(2,1)S(1)} all-gather(bf16[2,4,3584]{2,0,1:T(2,128)(2,1)S(1)} %copy.58), channel_id=1, replica_groups=mesh['ep'=128,'dp'=4] {'dp'}, dimensions={1}, use_global_device_ids=true | all-gather | bytes 286720 | tf_op jit(solution)/shard_map/all_gather | solution.py:77
  13.6 0.3 fusion.25
  13.9 0.9 select_reduce_fusion.2
  15.1 2.5 scatter_custom_fusion
  17.5 3.1 copy.60
  20.7 20.5 %all-to-all-start = ((bf16[2,128,3584]{2,0,1:T(2,128)(2,1)}), bf16[2,128,3584]{2,0,1:T(2,128)(2,1)S(1)}, u32[]{:S(2)}, u32[]{:S(2)}) async-start(bf16[2,128,3584]{2,0,1:T(2,128)(2,1)} %copy.60), calls=%async_computation | async-start | bytes 3670016 | tf_op jit(solution)/shard_map/all_to_all | solution.py:89
  41.1 3.7 %reshape_squeeze.3 = bf16[128,28,256]{2,1,0:T(8,128)(2,1)} reshape(bf16[1,3584,256]{2,1,0:T(8,128)(2,1)} %param.14) | data formatting | bytes 3670016 | tf_op jit(solution)/shard_map/reshape;squeeze | solution.py:65
  44.9 42.7 %all-to-all-done = bf16[2,128,3584]{2,0,1:T(2,128)(2,1)S(1)} async-done(((bf16[2,128,3584]{2,0,1:T(2,128)(2,1)}), bf16[2,128,3584]{2,0,1:T(2,128)(2,1)S(1)}, u32[]{:S(2)}, u32[]{:S(2)}) %all-to-all-start) | async-done | bytes 1835040 | tf_op jit(solution)/shard_map/all_to_all | solution.py:89
  87.6 1.3 copy-done.3
  88.9 7.8 %all-to-all-start.1 = ((bf16[128,28,256]{2,1,0:T(8,128)(2,1)}), bf16[128,28,256]{2,1,0:T(8,128)(2,1)S(1)}, u32[]{:S(2)}, u32[]{:S(2)}) async-start(bf16[128,28,256]{2,1,0:T(8,128)(2,1)} %reshape_squeeze.3), calls=%async_computation.1 | async-start | bytes 4194304 | tf_op jit(solution)/shard_map/all_to_all | solution.py:68
  96.7 3.3 %scatter_custom_fusion.1 = bf16[256,3584]{1,0:T(8,128)(2,1)} fusion(s32[128]{0:T(128)S(1)} %get-tuple-element.141, bf16[]{:T(256)} %constant.58.clone.1, bf16[16,3584]{1,0:T(8,128)(2,1)S(1)} %get-tuple-element.142), kind=kCustom, calls=%fused_computation.24 | custom fusion | bytes 1949698 | tf_op jit(solution)/shard_map/scatter | solution.py:85
  100.0 4.6 %copy.69 = bf16[2,128,3584]{2,0,1:T(2,128)(2,1)} copy(bf16[2,128,3584]{2,1,0:T(8,128)(2,1)} %bitcast.125) | data formatting | bytes 3670016 | tf_op jit(solution)/shard_map/reshape | solution.py:86
  104.6 44.2 %all-to-all-done.1 = bf16[128,28,256]{2,1,0:T(8,128)(2,1)S(1)} async-done(((bf16[128,28,256]{2,1,0:T(8,128)(2,1)}), bf16[128,28,256]{2,1,0:T(8,128)(2,1)S(1)}, u32[]{:S(2)}, u32[]{:S(2)}) %all-to-all-start.1) | async-done | bytes 1835040 | tf_op jit(solution)/shard_map/all_to_all | solution.py:68
  148.8 8.1 %all-to-all-start.4 = ((bf16[2,128,3584]{2,0,1:T(2,128)(2,1)}), bf16[2,128,3584]{2,0,1:T(2,128)(2,1)}, u32[]{:S(2)}, u32[]{:S(2)}) async-start(bf16[2,128,3584]{2,0,1:T(2,128)(2,1)} %copy.69), calls=%async_computation.4 | async-start | bytes 3670016 | tf_op jit(solution)/shard_map/all_to_all | solution.py:89
  157.0 2.0 gather_fusion
  159.0 3.2 %broadcast_select_fusion = bf16[128,28,256]{2,1,0:T(8,128)(2,1)} fusion(bf16[128,28,256]{2,1,0:T(8,128)(2,1)} %gather_fusion, pred[128]{0:T(512)(128)(4,1)S(1)} %compare_and_fusion), kind=kLoop, calls=%fused_computation.23 | loop fusion | flops 917504 | bytes 3670144 | tf_op jit(solution)/shard_map/jit(_take)/select_n | solution.py:67
  162.2 40.9 %all-to-all-done.4 = bf16[2,128,3584]{2,0,1:T(2,128)(2,1)} async-done(((bf16[2,128,3584]{2,0,1:T(2,128)(2,1)}), bf16[2,128,3584]{2,0,1:T(2,128)(2,1)}, u32[]{:S(2)}, u32[]{:S(2)}) %all-to-all-start.4) | async-done | bytes 1835040 | tf_op jit(solution)/shard_map/all_to_all | solution.py:89
  203.1 7.8 %all-to-all-start.2 = ((bf16[128,28,256]{2,1,0:T(8,128)(2,1)}), bf16[128,28,256]{2,1,0:T(8,128)(2,1)S(1)}, u32[]{:S(2)}, u32[]{:S(2)}) async-start(bf16[128,28,256]{2,1,0:T(8,128)(2,1)} %broadcast_select_fusion), calls=%async_computation.2 | async-start | bytes 4194304 | tf_op jit(solution)/shard_map/all_to_all | solution.py:66
  210.9 0.6 dynamic_slice.15
  213.8 5.6 %copy.62 = bf16[2,128,3584]{1,2,0:T(8,128)(2,1)} copy(bf16[2,128,3584]{2,0,1:T(2,128)(2,1)} %copy-done.3) | data formatting | bytes 3670016 | tf_op jit(solution)/shard_map/while | solution.py:40
  219.3 5.5 %copy.70 = bf16[2,128,3584]{1,2,0:T(8,128)(2,1)} copy(bf16[2,128,3584]{2,0,1:T(2,128)(2,1)} %all-to-all-done.4) | data formatting | bytes 3670016 | tf_op jit(solution)/shard_map/while | solution.py:40
  224.9 38.2 %all-to-all-done.2 = bf16[128,28,256]{2,1,0:T(8,128)(2,1)S(1)} async-done(((bf16[128,28,256]{2,1,0:T(8,128)(2,1)}), bf16[128,28,256]{2,1,0:T(8,128)(2,1)S(1)}, u32[]{:S(2)}, u32[]{:S(2)}) %all-to-all-start.2) | async-done | bytes 1835040 | tf_op jit(solution)/shard_map/all_to_all | solution.py:66
  263.1 1.5 reshape_reshape.6
  264.6 0.4 copy-done.1
  265.0 5.2 %while.22 = (s32[]{:T(128)}, bf16[2,128,256]{2,1,0:T(8,128)(2,1)S(1)}, bf16[2,128,3584]{1,2,0:T(8,128)(2,1)}, bf16[128,28,256]{2,1,0:T(8,128)(2,1)}, f32[28,2]{1...) while((s32[]{:T(128)}, bf16[2,128,256]{2,1,0:T(8,128)(2,1)S(1)}, ...), condition=%wide.wide.region_8.9_spmd, body=%wide.wide.region_6.8_spmd.sunk | while | flops 236847104 | bytes 12439901 | solution.py:40
  265.0 1.4 constant_dynamic-slice_fusion.7
  266.5 0.3 copy-done.5
  266.8 0.7 multiply_reduce_fusion.6
  267.6 1.4 constant_dynamic-slice_fusion.7
  269.4 0.7 multiply_reduce_fusion.6
  270.2 0.8 copy.64
  270.9 7.7 %all-to-all-start.3 = ((bf16[2,128,256]{2,0,1:T(2,128)(2,1)}), bf16[2,128,256]{2,0,1:T(2,128)(2,1)S(1)}, u32[]{:S(2)}, u32[]{:S(2)}) async-start(bf16[2,128,256]{2,0,1:T(2,128)(2,1)} %copy.64), calls=%async_computation.3 | async-start | bytes 262144 | tf_op jit(solution)/shard_map/all_to_all | solution.py:41
  278.7 3.9 %reshape_reshape.8 = bf16[28,128,256]{2,1,0:T(8,128)(2,1)} reshape(bf16[128,28,256]{2,1,0:T(8,128)(2,1)} %get-tuple-element.307) | data formatting | bytes 3670016 | tf_op jit(solution)/shard_map/while/body/eval_jaxpr/reshape;reshape | solution.py:26
  282.6 4.6 %while.23 = (s32[]{:T(128)}, bf16[2,128,256]{2,1,0:T(8,128)(2,1)S(1)}, bf16[2,128,3584]{1,2,0:T(8,128)(2,1)S(1)}, bf16[128,28,256]{2,1,0:T(8,128)(2,1)}, f32[28,...) while((s32[]{:T(128)}, bf16[2,128,256]{2,1,0:T(8,128)(2,1)S(1)}, ...), condition=%wide.wide.region_16.17_spmd, body=%wide.wide.region_14.16_spmd.sunk | while | flops 236847104 | bytes 12439901 | solution.py:40
  282.8 1.3 copy-done.4
  284.1 0.7 multiply_reduce_fusion.7
  285.1 1.3 copy-done.4
  286.4 0.7 multiply_reduce_fusion.7
  287.2 0.8 copy.72
  288.0 3.0 all-to-all-done.3
  290.9 10.8 %all-to-all-start.5 = ((bf16[2,128,256]{2,0,1:T(2,128)(2,1)}), bf16[2,128,256]{2,0,1:T(2,128)(2,1)S(1)}, u32[]{:S(2)}, u32[]{:S(2)}) async-start(bf16[2,128,256]{2,0,1:T(2,128)(2,1)} %copy.72), calls=%async_computation.5 | async-start | bytes 262144 | tf_op jit(solution)/shard_map/all_to_all | solution.py:41
  301.9 3.7 %broadcast_in_dim_reshape.3 = bf16[1,3584,256]{2,1,0:T(8,128)(2,1)} reshape(bf16[128,28,256]{2,1,0:T(8,128)(2,1)} %get-tuple-element.308) | data formatting | bytes 3670016 | tf_op jit(solution)/shard_map/broadcast_in_dim;reshape | solution.py:95
  305.6 0.8 gather_fusion.1
  306.6 7.3 %all-to-all-done.5 = bf16[2,128,256]{2,0,1:T(2,128)(2,1)S(1)} async-done(((bf16[2,128,256]{2,0,1:T(2,128)(2,1)}), bf16[2,128,256]{2,0,1:T(2,128)(2,1)S(1)}, u32[]{:S(2)}, u32[]{:S(2)}) %all-to-all-start.5) | async-done | bytes 131104 | tf_op jit(solution)/shard_map/all_to_all | solution.py:41
  313.9 0.8 gather_fusion.2
  314.9 0.6 pad_maximum_fusion
  (61 shorter events, 2.9 us)
Async XLA Ops:
  0.6 212.8 %copy-start = (f32[128,28,2]{0,2,1:T(2,128)S(1)}, f32[128,28,2]{0,2,1:T(2,128)}, u32[]{:S(2)}) copy-start(f32[128,28,2]{0,2,1:T(2,128)} %param.15) | copy-start | bytes 86020
  20.7 67.0 %all-to-all-start = ((bf16[2,128,3584]{2,0,1:T(2,128)(2,1)}), bf16[2,128,3584]{2,0,1:T(2,128)(2,1)S(1)}, u32[]{:S(2)}, u32[]{:S(2)}) async-start(bf16[2,128,3584]{2,0,1:T(2,128)(2,1)} %copy.60), calls=%async_computation | async-start | bytes 3670016 | tf_op jit(solution)/shard_map/all_to_all | solution.py:89
  87.6 1.3 copy-start.3
  88.9 59.9 %all-to-all-start.1 = ((bf16[128,28,256]{2,1,0:T(8,128)(2,1)}), bf16[128,28,256]{2,1,0:T(8,128)(2,1)S(1)}, u32[]{:S(2)}, u32[]{:S(2)}) async-start(bf16[128,28,256]{2,1,0:T(8,128)(2,1)} %reshape_squeeze.3), calls=%async_computation.1 | async-start | bytes 4194304 | tf_op jit(solution)/shard_map/all_to_all | solution.py:68
  148.8 54.3 %all-to-all-start.4 = ((bf16[2,128,3584]{2,0,1:T(2,128)(2,1)}), bf16[2,128,3584]{2,0,1:T(2,128)(2,1)}, u32[]{:S(2)}, u32[]{:S(2)}) async-start(bf16[2,128,3584]{2,0,1:T(2,128)(2,1)} %copy.69), calls=%async_computation.4 | async-start | bytes 3670016 | tf_op jit(solution)/shard_map/all_to_all | solution.py:89
  162.2 48.7 %copy-start.7 = (s32[128]{0:T(128)S(1)}, s32[128]{0:T(128)}, u32[]{:S(2)}) copy-start(s32[128]{0:T(128)} %param.17) | copy-start | bytes 1540
  162.2 51.5 %copy-start.6 = (f32[2,16,8]{1,2,0:T(8,128)S(1)}, f32[2,16,8]{1,2,0:T(8,128)}, u32[]{:S(2)}) copy-start(f32[2,16,8]{1,2,0:T(8,128)} %param.13) | copy-start | bytes 3076
  203.1 59.9 %all-to-all-start.2 = ((bf16[128,28,256]{2,1,0:T(8,128)(2,1)}), bf16[128,28,256]{2,1,0:T(8,128)(2,1)S(1)}, u32[]{:S(2)}, u32[]{:S(2)}) async-start(bf16[128,28,256]{2,1,0:T(8,128)(2,1)} %broadcast_select_fusion), calls=%async_computation.2 | async-start | bytes 4194304 | tf_op jit(solution)/shard_map/all_to_all | solution.py:66
  263.1 1.9 copy-start.1
  265.0 1.8 copy-start.5
  267.6 1.8 copy-start.5
  270.9 20.0 %all-to-all-start.3 = ((bf16[2,128,256]{2,0,1:T(2,128)(2,1)}), bf16[2,128,256]{2,0,1:T(2,128)(2,1)S(1)}, u32[]{:S(2)}, u32[]{:S(2)}) async-start(bf16[2,128,256]{2,0,1:T(2,128)(2,1)} %copy.64), calls=%async_computation.3 | async-start | bytes 262144 | tf_op jit(solution)/shard_map/all_to_all | solution.py:41
  278.7 3.9 %copy-start.2 = (bf16[2,128,3584]{1,2,0:T(8,128)(2,1)S(1)}, bf16[2,128,3584]{1,2,0:T(8,128)(2,1)}, u32[]{:S(2)}) copy-start(bf16[2,128,3584]{1,2,0:T(8,128)(2,1)} %copy.70) | copy-start | bytes 5505028
  282.6 1.5 copy-start.4
  284.9 1.5 copy-start.4
  290.9 22.9 %all-to-all-start.5 = ((bf16[2,128,256]{2,0,1:T(2,128)(2,1)}), bf16[2,128,256]{2,0,1:T(2,128)(2,1)S(1)}, u32[]{:S(2)}, u32[]{:S(2)}) async-start(bf16[2,128,256]{2,0,1:T(2,128)(2,1)} %copy.72), calls=%async_computation.5 | async-start | bytes 262144 | tf_op jit(solution)/shard_map/all_to_all | solution.py:41
where the time goes:
time: 317 us; the launch traced here: 315 us
  waiting for transfers between devices  176 us (56%)
  starting transfers between devices  62.7 us (20%)
  local copies, waits for them, and re-layouts  54.2 us (17%)
  blocking collectives  10.5 us (3%)
  other arithmetic  5.92 us (2%)
    all_to_all x2, waiting for transfers between devices, shards(): lax.all_to_all(send_buffer, 'ep', split_axis=1, concat_axis=1, tiled=True)  83.6 us
    all_to_all x1, waiting for transfers between devices, shards(): lax.all_to_all(pieces, 'ep', split_axis=0, concat_axis=0, tiled=True)  44.2 us
    all_to_all x1, waiting for transfers between devices, shards(): lax.all_to_all(jnp.take(lax.all_to_all(pieces, 'ep', split_axis=0, concat...  38.2 us
    all_to_all x2, starting transfers between devices, shards(): lax.all_to_all(send_buffer, 'ep', split_axis=1, concat_axis=1, tiled=True)  28.6 us
    all_to_all x2, starting transfers between devices, serve_rows(): lax.all_to_all(activated, 'ep', split_axis=1, concat_axis=1, tiled=True)  18.5 us
    while x5, local copies, waits for them, and re-layouts, serve_rows(): activated = lax.map(one_slot, arrived)  12.7 us
    all_gather x1, blocking collectives, shards(): grouped = lax.all_gather(tokens, 'dp', axis=1, tiled=True)  10.5 us
    all_to_all x2, waiting for transfers between devices, serve_rows(): lax.all_to_all(activated, 'ep', split_axis=1, concat_axis=1, tiled=True)  10.3 us
  transfers between devices with their start and end apart: 6, of which 6 were waited for; matrix products, arithmetic and copies ran while one was open for 13% of the time, Pallas kernels for 0%

commit v1 on v0

v1 whole, which is shorter than its diff:
```python
import jax
import jax.numpy as jnp
from jax import lax
from jax.sharding import PartitionSpec as P


def inverse_place(expert_at):
    count = expert_at.shape[0]
    labels = jnp.arange(count, dtype=jnp.int32)
    match = expert_at[None, :] == labels[:, None]
    return jnp.sum(jnp.where(match, labels[None, :], 0), axis=1)


def source_slots(old_expert, new_expert):
    labels = jnp.arange(old_expert.shape[0], dtype=jnp.int32)
    match = old_expert[None, :] == new_expert[:, None]
    return jnp.sum(jnp.where(match, labels[None, :], 0), axis=1)


def route_targets(routing, owners, peers, capacity):
    steps, group_size, top_count = routing.shape
    labels = jnp.arange(peers, dtype=jnp.int32)
    pair_ids = routing.reshape(steps, group_size * top_count)
    onehot = (pair_ids[:, :, None] == labels[None, None, :]).astype(jnp.int32)
    before = jnp.cumsum(onehot, axis=1) - onehot
    rank = jnp.sum(before * onehot, axis=2)
    slot = owners[pair_ids]
    step = jnp.arange(steps, dtype=jnp.int32)[:, None]
    return (slot * steps + step) * capacity + rank


def shards(tokens, routing, gate_values, held_weight, scale_table, old_expert, new_expert):
    peers = lax.axis_size("ep")
    n_dp = lax.axis_size("dp")
    my_slot = lax.axis_index("ep")
    my_dp = lax.axis_index("dp")
    steps, group_size, top_count = routing.shape
    capacity = 2
    old_block = held_weight[0]
    rows, cols = old_block.shape
    row_part = rows // n_dp
    blk = rows // scale_table.shape[1]
    owners = inverse_place(old_expert)
    sources = source_slots(old_expert, new_expert)

    w_rows = lax.all_to_all(old_block, "dp", split_axis=0, concat_axis=1, tiled=True)
    my_scales = lax.all_gather(scale_table[old_expert[my_slot]], "dp", axis=1, tiled=True)
    row_blocks = row_part // blk
    my_scales = lax.dynamic_slice_in_dim(my_scales, my_dp * row_blocks, row_blocks, axis=0)
    widened = jnp.repeat(jnp.repeat(my_scales, blk, axis=0), blk, axis=1)
    w32 = w_rows.astype(jnp.float32) * widened
    w_hi = w32.astype(jnp.bfloat16)
    w_lo = (w32 - w_hi.astype(jnp.float32)).astype(jnp.bfloat16)

    feats = lax.all_to_all(tokens, "dp", split_axis=2, concat_axis=1, tiled=True)

    target = route_targets(routing, owners, peers, capacity)
    token_of = jnp.broadcast_to(
        jnp.arange(group_size, dtype=jnp.int32)[None, :, None], (steps, group_size, top_count)
    ).reshape(steps, -1)
    step_of = jnp.broadcast_to(jnp.arange(steps, dtype=jnp.int32)[:, None], token_of.shape)
    pick = jnp.zeros((peers * steps * capacity,), jnp.int32).at[target.reshape(-1)].set(
        (step_of * group_size + token_of).reshape(-1)
    )
    send_tokens = feats.reshape(steps * group_size, row_part)[pick]
    send_tokens = send_tokens.reshape(peers, steps * capacity * row_part)

    pieces = old_block.reshape(peers, (rows // peers) * cols)
    first = lax.all_to_all(
        jnp.concatenate([pieces, send_tokens], axis=1), "ep", split_axis=0, concat_axis=0, tiled=True
    )
    piece_len = pieces.shape[1]
    gathered_pieces = jnp.take(first[:, :piece_len], sources, axis=0)
    arrived = first[:, piece_len:].reshape(peers * steps * capacity, row_part)

    partial = jnp.dot(arrived, w_hi, preferred_element_type=jnp.float32) + jnp.dot(
        arrived, w_lo, preferred_element_type=jnp.float32
    )
    hidden = lax.psum_scatter(partial, "dp", scatter_dimension=1, tiled=True)
    act = jax.nn.silu(hidden).astype(jnp.bfloat16)
    act = act.reshape(peers, steps * capacity * act.shape[1])

    second = lax.all_to_all(
        jnp.concatenate([gathered_pieces, act], axis=1), "ep", split_axis=0, concat_axis=0, tiled=True
    )
    new_block = second[:, :piece_len].reshape(rows, cols)
    returned = second[:, piece_len:].reshape(peers * steps * capacity, -1)
    picked = returned[target].astype(jnp.float32).reshape(steps, group_size, top_count, -1)
    combined = jnp.sum(gate_values[:, :, :, None] * picked, axis=2).astype(jnp.bfloat16)
    return (combined, new_block[None])


def solution(mesh):
    placed = (
        P(None, ("ep", "dp"), None),
        P(None, "ep", None),
        P(None, "ep", None),
        P("ep", None, "dp"),
        P(None, None, "dp"),
        P(),
        P(),
    )
    return jax.shard_map(
        shards,
        mesh=mesh,
        in_specs=placed,
        out_specs=(P(None, "ep", "dp"), P("ep", None, "dp")),
        check_vma=False,
    )
```

time: 317 us -> 290 us (0.915)
  waiting for transfers between devices: 176 us -> 116 us
  local copies, waits for them, and re-layouts: 54.2 us -> 73.7 us
  other arithmetic: 5.92 us -> 23.8 us
  starting transfers between devices: 62.7 us -> 46.4 us
  between operations: 2.82 us -> 16.3 us
  blocking collectives: 10.5 us -> 6.95 us
    all_to_all x6 -> x4, waiting for transfers between devices: 176 us -> 94.8 us  [the longest x1 52 us: shards(): lax.all_to_all(jnp.concatenate([gathered_pieces, act], axis=1), 'ep', spl...]
    unnamed x13 -> x33, local copies, waits for them, and re-layouts: 2.49 us -> 43.8 us
    reduce_scatter x0 -> x1, waiting for transfers between devices: none -> 21.2 us  [shards(): hidden = lax.psum_scatter(partial, 'dp', scatter_dimension=1, tiled=True)]
    all_to_all x6 -> x4, starting transfers between devices: 62.7 us -> 46.4 us  [the longest x1 22.5 us: shards(): lax.all_to_all(jnp.concatenate([pieces, send_tokens], axis=1), 'ep', spli...]
    while x21 -> x0, local copies, waits for them, and re-layouts: 15.9 us -> none  [the longest x5 12.7 us: serve_rows(): activated = lax.map(one_slot, arrived)]
    all_to_all x0 -> x4, other arithmetic: none -> 9.97 us  [the longest x2 5.39 us: shards(): lax.all_to_all(jnp.concatenate([pieces, send_tokens], axis=1), 'ep', spli...]
    convert_element_type x2 -> x4, other arithmetic: 0.18 us -> 9.45 us  [the longest x1 4.55 us: shards(): w_lo = (w32 - w_hi.astype(jnp.float32)).astype(jnp.bfloat16)]
    another operation x6 -> x2, local copies, waits for them, and re-layouts: 12.9 us -> 7.75 us  [the longest x1 4.47 us: shards(): pieces = old_block.reshape(peers, rows // peers * cols)]
  transfers between devices with their start and end apart: 6 -> 5, of which waited for: 6 -> 3; matrix products, arithmetic and copies ran while one was open for 13% -> 17% of each run, Pallas kernels for 0% -> 0%
where the time goes in v1:
time: 290 us; the launch traced here: 288 us
  waiting for transfers between devices  116 us (40%)
  local copies, waits for them, and re-layouts  73.7 us (25%)
  starting transfers between devices  46.4 us (16%)
  other arithmetic  23.8 us (8%)
  between operations  16.3 us (6%)
  blocking collectives  6.95 us (2%)
  matrix products  5.21 us (2%)
    all_to_all x1, waiting for transfers between devices, shards(): lax.all_to_all(jnp.concatenate([gathered_pieces, act], axis=1), 'ep', spl...  52 us
    unnamed x33, local copies, waits for them, and re-layouts  43.8 us
    all_to_all x1, waiting for transfers between devices, shards(): lax.all_to_all(jnp.concatenate([pieces, send_tokens], axis=1), 'ep', spli...  42.8 us
    all_to_all x1, starting transfers between devices, shards(): lax.all_to_all(jnp.concatenate([pieces, send_tokens], axis=1), 'ep', spli...  22.5 us
    reduce_scatter x1, waiting for transfers between devices, shards(): hidden = lax.psum_scatter(partial, 'dp', scatter_dimension=1, tiled=True)  21.2 us
    all_to_all x1, starting transfers between devices, shards(): lax.all_to_all(jnp.concatenate([gathered_pieces, act], axis=1), 'ep', spl...  14.5 us
    all_gather x1, blocking collectives, shards(): lax.all_gather(scale_table[old_expert[my_slot]], 'dp', axis=1, tiled=True)  6.95 us
  transfers between devices with their start and end apart: 5, of which 3 were waited for; matrix products, arithmetic and copies ran while one was open for 17% of the time, Pallas kernels for 0%

profile of v1, /device:TPU:1, one launch (start us, length us, event | category | flops | bytes accessed | tf_op | source)
XLA Modules:
  0.0 288.5 jit_solution(11411212066454031922)
XLA Ops:
  7.2 3.8 %copy.43 = bf16[2,4,3584]{1,0,2:T(2,128)(2,1)S(1)} copy(bf16[2,4,3584]{2,1,0:T(4,128)(2,1)} %param.7) | data formatting | bytes 114688 | tf_op args[0]
  11.0 4.3 %reshape.277 = bf16[4,2,3584]{2,1,0:T(2,128)(2,1)} reshape(bf16[3584,2,4]{2,1,0:T(2,128)(2,1)S(1)} %bitcast.65) | data formatting | bytes 114688
  15.3 4.8 %all-to-all-start = ((bf16[4,2,3584]{2,1,0:T(2,128)(2,1)}), bf16[4,2,3584]{2,1,0:T(2,128)(2,1)S(1)}, u32[]{:S(2)}, u32[]{:S(2)}) async-start(bf16[4,2,3584]{2,1,0:T(2,128)(2,1)} %reshape.277), calls=%async_computation | async-start | bytes 114688 | tf_op jit(solution)/shard_map/all_to_all | solution.py:55
  20.5 0.2 reduce_window_sum.11
  20.7 0.2 select_reduce_fusion
  20.9 0.2 select_reduce_fusion.2
  21.1 1.9 gather_fusion
  23.1 1.4 scatter_custom_fusion
  24.6 4.5 %reshape_squeeze.3 = bf16[128,7168]{1,0:T(8,128)(2,1)} reshape(bf16[1,3584,256]{2,1,0:T(8,128)(2,1)} %param.10) | data formatting | bytes 3670016 | tf_op jit(solution)/shard_map/reshape;squeeze | solution.py:68
  29.0 4.6 %all-to-all-start.2 = ((bf16[4,896,256]{2,1,0:T(8,128)(2,1)}), bf16[4,896,256]{2,1,0:T(8,128)(2,1)}, u32[]{:S(2)}, u32[]{:S(2)}) async-start(bf16[4,896,256]{2,1,0:T(8,128)(2,1)} %bitcast.10), calls=%async_computation.2 | async-start | bytes 3670016 | tf_op jit(solution)/shard_map/all_to_all | solution.py:46
  33.6 3.9 %reshape.278 = bf16[3584,2,4]{2,1,0:T(2,128)(2,1)S(1)} reshape(bf16[4,2,3584]{2,1,0:T(2,128)(2,1)S(1)} %all-to-all-done) | data formatting | bytes 114688
  37.6 1.3 copy.44
  38.9 2.1 gather_fusion.1
  41.0 1.5 reshape.218
  42.5 2.0 maximum_bitcast_fusion
  44.4 0.5 broadcast.167
  44.9 3.4 %reduce = bf16[128,10752]{1,0:T(8,128)(2,1)} reduce(bf16[128,1,10752]{2,0,1:T(8,128)(2,1)S(1)} %maximum_bitcast_fusion, bf16[]{:T(256)} %broadcast.167), dimensions={1}, to_apply=%copy.47.reduce_sub_computation | reduce | bytes 5505026 | tf_op jit(solution)/shard_map/all_to_all | solution.py:69
  48.4 4.2 %reshape.279 = bf16[128,2,5376]{2,1,0:T(2,128)(2,1)} reshape(bf16[128,10752]{1,0:T(8,128)(2,1)} %reduce) | data formatting | bytes 5505024
  52.6 22.5 %all-to-all-start.1 = ((bf16[128,2,5376]{2,1,0:T(2,128)(2,1)}), bf16[128,2,5376]{2,1,0:T(2,128)(2,1)S(1)}, u32[]{:S(2)}, u32[]{:S(2)}) async-start(bf16[128,2,5376]{2,1,0:T(2,128)(2,1)} %reshape.279), calls=%async_computation.1 | async-start | bytes 5505024 | tf_op jit(solution)/shard_map/all_to_all | solution.py:69
  75.1 0.6 dynamic_slice.9
  77.9 6.9 %all-gather = f32[1,28,8]{1,0,2:T(1,128)S(1)} all-gather(f32[1,28,2]{1,0,2:T(1,128)S(1)} %copy.54), channel_id=2, replica_groups=mesh['ep'=128,'dp'=4] {'dp'}, dimensions={2}, use_global_device_ids=true | all-gather | bytes 1120 | tf_op jit(solution)/shard_map/all_gather | solution.py:47
  85.0 3.6 %convert_bitcast_fusion = f32[896,4,256]{2,0,1:T(8,128)} fusion(bf16[4,896,256]{2,1,0:T(8,128)(2,1)} %all-to-all-done.2), kind=kLoop, calls=%fused_computation.5 | loop fusion | flops 917504 | bytes 5505024 | tf_op jit(solution)/shard_map/convert_element_type | solution.py:51
  88.7 4.6 %copy.48 = f32[896,4,256]{0,2,1:T(8,128)} copy(f32[896,4,256]{2,0,1:T(8,128)} %convert_bitcast_fusion) | data formatting | bytes 7340032 | tf_op jit(solution)/shard_map/convert_element_type | solution.py:51
  93.3 4.5 %subtract_convert_fusion = (bf16[896,8,128]{0,2,1:T(8,128)(2,1)}, bf16[896,8,128]{0,2,1:T(8,128)(2,1)}) fusion(f32[896,8,128]{0,2,1:T(8,128)} %bitcast.59, f32[896,8]{0,1:T(8,128)S(1)} %broadcast_bitcast_fusion), kind=kLoop, calls=%fused_computation.6 | loop fusion | flops 4587520 | bytes 7368704 | tf_op jit(solution)/shard_map/convert_element_type | solution.py:53
  97.8 42.8 %all-to-all-done.1 = bf16[128,2,5376]{2,1,0:T(2,128)(2,1)S(1)} async-done(((bf16[128,2,5376]{2,1,0:T(2,128)(2,1)}), bf16[128,2,5376]{2,1,0:T(2,128)(2,1)S(1)}, u32[]{:S(2)}, u32[]{:S(2)}) %all-to-all-start.1) | async-done | bytes 2752544 | tf_op jit(solution)/shard_map/all_to_all | solution.py:69
  140.6 7.1 %reshape.280 = bf16[128,1,10752]{2,1,0:T(2,128)(2,1)} reshape(bf16[128,2,5376]{2,1,0:T(2,128)(2,1)S(1)} %all-to-all-done.1) | data formatting | bytes 5505024
  147.7 2.9 %copy.58 = bf16[128,1,10752]{2,0,1:T(8,128)(2,1)S(1)} copy(bf16[128,1,10752]{2,1,0:T(2,128)(2,1)} %reshape.280) | data formatting | bytes 5505024
  150.7 1.5 copy-done.2
  152.3 1.5 reshape.219
  153.8 2.6 fusion.10
  156.4 2.6 convolution_add_fusion
  159.1 1.6 slice.24
  160.7 2.9 %gather_fusion.2 = bf16[128,7168]{1,0:T(8,128)(2,1)} fusion(bf16[128,7168]{1,0:T(8,128)(2,1)S(1)} %slice.24, s32[1024]{0:T(1024)S(1)} %pad_clamp_fusion.1), kind=kCustom, calls=%fused_computation.2 | custom fusion | bytes 3670528 | tf_op jit(solution)/shard_map/jit(_take)/gather | solution.py:73
  163.6 3.0 %broadcast_select_fusion = bf16[128,7168]{1,0:T(8,128)(2,1)} fusion(bf16[128,7168]{1,0:T(8,128)(2,1)} %gather_fusion.2, pred[128]{0:T(512)(128)(4,1)S(1)} %compare_and_fusion), kind=kLoop, calls=%fused_computation.12 | loop fusion | flops 917504 | bytes 3670144 | tf_op jit(solution)/shard_map/jit(_take)/select_n | solution.py:73
  166.6 21.2 %reduce-scatter.2.cloned.1.call-done = f32[512,256]{1,0:T(8,128)} async-done(((f32[512,1024]{1,0:T(8,128)}), f32[512,256]{1,0:T(8,128)}) %reduce-scatter.2.cloned.1.call-update) | async-done | bytes 524304 | tf_op jit(solution)/shard_map/reduce_scatter | solution.py:79
  187.7 1.2 multiply_convert_fusion.1
  188.9 0.2 reshape.221
  189.1 1.6 maximum_bitcast_fusion.1
  190.7 2.9 %reduce.1 = bf16[128,8192]{1,0:T(8,128)(2,1)} reduce(bf16[128,1,8192]{2,0,1:T(8,128)(2,1)S(1)} %maximum_bitcast_fusion.1, bf16[]{:T(256)} %broadcast.167), dimensions={1}, to_apply=%copy.51.reduce_sub_computation | reduce | bytes 4194306 | tf_op jit(solution)/shard_map/all_to_all | solution.py:83
  193.7 4.5 %reshape.281 = bf16[128,2,4096]{2,1,0:T(2,128)(2,1)} reshape(bf16[128,8192]{1,0:T(8,128)(2,1)} %reduce.1) | data formatting | bytes 4194304
  198.2 14.5 %all-to-all-start.3 = ((bf16[128,2,4096]{2,1,0:T(2,128)(2,1)}), bf16[128,2,4096]{2,1,0:T(2,128)(2,1)S(1)}, u32[]{:S(2)}, u32[]{:S(2)}) async-start(bf16[128,2,4096]{2,1,0:T(2,128)(2,1)} %reshape.281), calls=%async_computation.4 | async-start | bytes 4194304 | tf_op jit(solution)/shard_map/all_to_all | solution.py:83
  212.8 52.0 %all-to-all-done.3 = bf16[128,2,4096]{2,1,0:T(2,128)(2,1)S(1)} async-done(((bf16[128,2,4096]{2,1,0:T(2,128)(2,1)}), bf16[128,2,4096]{2,1,0:T(2,128)(2,1)S(1)}, u32[]{:S(2)}, u32[]{:S(2)}) %all-to-all-start.3) | async-done | bytes 2097184 | tf_op jit(solution)/shard_map/all_to_all | solution.py:83
  264.8 6.8 %reshape.282 = bf16[128,1,8192]{2,1,0:T(2,128)(2,1)} reshape(bf16[128,2,4096]{2,1,0:T(2,128)(2,1)S(1)} %all-to-all-done.3) | data formatting | bytes 4194304
  271.6 4.5 %copy.59 = bf16[128,1,8192]{2,0,1:T(8,128)(2,1)S(1)} copy(bf16[128,1,8192]{2,1,0:T(2,128)(2,1)} %reshape.282) | data formatting | bytes 4194304
  276.2 0.2 reshape.222
  276.4 3.3 %broadcast_in_dim_reshape.4 = bf16[1,3584,256]{2,1,0:T(8,128)(2,1)} reshape(bf16[128,7168]{1,0:T(8,128)(2,1)S(1)} %slice.27) | data formatting | bytes 3670016 | tf_op jit(solution)/shard_map/broadcast_in_dim;reshape | solution.py:90
  279.7 1.1 gather_fusion.3
  280.8 0.8 fusion
  (52 shorter events, 1.4 us)
Async XLA Ops:
  7.2 70.5 %copy-start = (f32[128,28,2]{0,2,1:T(2,128)S(1)}, f32[128,28,2]{0,2,1:T(2,128)}, u32[]{:S(2)}) copy-start(f32[128,28,2]{0,2,1:T(2,128)} %param.11) | copy-start | bytes 86020
  7.2 12.9 %copy-start.6 = (s32[2,16,8]{1,2,0:T(8,128)S(1)}, s32[2,16,8]{1,2,0:T(8,128)}, u32[]{:S(2)}) copy-start(s32[2,16,8]{1,2,0:T(8,128)} %param.8) | copy-start | bytes 3076
  7.2 13.7 %copy-start.9 = (s32[128]{0:T(128)S(1)}, s32[128]{0:T(128)}, u32[]{:S(2)}) copy-start(s32[128]{0:T(128)} %param.12) | copy-start | bytes 1540
  7.2 13.7 %copy-start.8 = (s32[128]{0:T(128)S(1)}, s32[128]{0:T(128)}, u32[]{:S(2)}) copy-start(s32[128]{0:T(128)} %param.13) | copy-start | bytes 1540
  15.3 13.8 %all-to-all-start = ((bf16[4,2,3584]{2,1,0:T(2,128)(2,1)}), bf16[4,2,3584]{2,1,0:T(2,128)(2,1)S(1)}, u32[]{:S(2)}, u32[]{:S(2)}) async-start(bf16[4,2,3584]{2,1,0:T(2,128)(2,1)} %reshape.277), calls=%async_computation | async-start | bytes 114688 | tf_op jit(solution)/shard_map/all_to_all | solution.py:55
  29.0 23.6 %all-to-all-start.2 = ((bf16[4,896,256]{2,1,0:T(8,128)(2,1)}), bf16[4,896,256]{2,1,0:T(8,128)(2,1)}, u32[]{:S(2)}, u32[]{:S(2)}) async-start(bf16[4,896,256]{2,1,0:T(8,128)(2,1)} %bitcast.10), calls=%async_computation.2 | async-start | bytes 3670016 | tf_op jit(solution)/shard_map/all_to_all | solution.py:46
  52.6 88.0 %all-to-all-start.1 = ((bf16[128,2,5376]{2,1,0:T(2,128)(2,1)}), bf16[128,2,5376]{2,1,0:T(2,128)(2,1)S(1)}, u32[]{:S(2)}, u32[]{:S(2)}) async-start(bf16[128,2,5376]{2,1,0:T(2,128)(2,1)} %reshape.279), calls=%async_computation.1 | async-start | bytes 5505024 | tf_op jit(solution)/shard_map/all_to_all | solution.py:69
  75.1 112.7 %reduce-scatter.2.cloned.1.call-start = ((), (), s32[]{:S(2)}) async-start(), calls=%async_computation.5 | async-start | bytes 2621440 | tf_op jit(solution)/shard_map/reduce_scatter | solution.py:79
  150.6 1.6 copy-start.2
  150.6 3.1 %copy-start.4 = (bf16[896,8,128]{0,2,1:T(8,128)(2,1)S(1)}, bf16[896,8,128]{0,2,1:T(8,128)(2,1)}, u32[]{:S(2)}) copy-start(bf16[896,8,128]{0,2,1:T(8,128)(2,1)} %get-tuple-element.5) | copy-start | bytes 5505028
  153.8 2.6 copy-start.3
  153.8 2.6 copy-start.5
  198.2 14.5 %copy-start.7 = (f32[2,16,8]{1,2,0:T(8,128)S(1)}, f32[2,16,8]{1,2,0:T(8,128)}, u32[]{:S(2)}) copy-start(f32[2,16,8]{1,2,0:T(8,128)} %param.9) | copy-start | bytes 3076
  198.2 66.6 %all-to-all-start.3 = ((bf16[128,2,4096]{2,1,0:T(2,128)(2,1)}), bf16[128,2,4096]{2,1,0:T(2,128)(2,1)S(1)}, u32[]{:S(2)}, u32[]{:S(2)}) async-start(bf16[128,2,4096]{2,1,0:T(2,128)(2,1)} %reshape.281), calls=%async_computation.4 | async-start | bytes 4194304 | tf_op jit(solution)/shard_map/all_to_all | solution.py:83
  276.2 5.4 %copy-start.1 = (f32[128,28,2]{0,2,1:T(2,128)S(1)}, f32[128,28,2]{0,2,1:T(2,128)}, u32[]{:S(2)}) copy-start(f32[128,28,2]{0,2,1:T(2,128)} %param.11) | copy-start | bytes 86020
Sparse Core Ops, SparseCore 0:
  159.1 28.5 reduce-scatter.1

commit v2 on v1

--- a/solution.py
+++ b/solution.py
@@ -29,6 +29,16 @@
     return (slot * steps + step) * capacity + rank
 
 
+def dp_exchange(parts, n_dp, my_dp):
+    got = [parts[my_dp]]
+    for shift in range(1, n_dp):
+        pairs = [(k, (k + shift) % n_dp) for k in range(n_dp)]
+        got.append(lax.ppermute(parts[(my_dp + shift) % n_dp], "dp", pairs))
+    by_shift = jnp.stack(got)
+    order = (my_dp - jnp.arange(n_dp, dtype=jnp.int32)) % n_dp
+    return by_shift[order]
+
+
 def shards(tokens, routing, gate_values, held_weight, scale_table, old_expert, new_expert):
     peers = lax.axis_size("ep")
     n_dp = lax.axis_size("dp")
@@ -43,16 +53,25 @@
     owners = inverse_place(old_expert)
     sources = source_slots(old_expert, new_expert)
 
-    w_rows = lax.all_to_all(old_block, "dp", split_axis=0, concat_axis=1, tiled=True)
-    my_scales = lax.all_gather(scale_table[old_expert[my_slot]], "dp", axis=1, tiled=True)
+    pieces = old_block.reshape(peers, rows // peers, cols)
+    staged = lax.all_to_all(pieces, "ep", split_axis=0, concat_axis=0, tiled=True)
+
+    w_parts = dp_exchange(old_block.reshape(n_dp, row_part, cols), n_dp, my_dp)
+    w_rows = jnp.transpose(w_parts, (1, 0, 2)).reshape(row_part, n_dp * cols)
+    own_scales = scale_table[old_expert[my_slot]]
     row_blocks = row_part // blk
-    my_scales = lax.dynamic_slice_in_dim(my_scales, my_dp * row_blocks, row_blocks, axis=0)
+    s_parts = dp_exchange(own_scales.reshape(n_dp, row_blocks, own_scales.shape[1]), n_dp, my_dp)
+    my_scales = jnp.transpose(s_parts, (1, 0, 2)).reshape(row_blocks, -1)
     widened = jnp.repeat(jnp.repeat(my_scales, blk, axis=0), blk, axis=1)
     w32 = w_rows.astype(jnp.float32) * widened
-    w_hi = w32.astype(jnp.bfloat16)
-    w_lo = (w32 - w_hi.astype(jnp.float32)).astype(jnp.bfloat16)
+    hi32 = lax.reduce_precision(w32, exponent_bits=8, mantissa_bits=7)
+    w_hi = hi32.astype(jnp.bfloat16)
+    w_lo = (w32 - hi32).astype(jnp.bfloat16)
 
-    feats = lax.all_to_all(tokens, "dp", split_axis=2, concat_axis=1, tiled=True)
+    t_parts = dp_exchange(
+        jnp.transpose(tokens.reshape(steps, tokens.shape[1], n_dp, row_part), (2, 0, 1, 3)), n_dp, my_dp
+    )
+    feats = jnp.transpose(t_parts, (1, 0, 2, 3)).reshape(steps * group_size, row_part)
 
     target = route_targets(routing, owners, peers, capacity)
     token_of = jnp.broadcast_to(
@@ -62,29 +81,22 @@
     pick = jnp.zeros((peers * steps * capacity,), jnp.int32).at[target.reshape(-1)].set(
         (step_of * group_size + token_of).reshape(-1)
     )
-    send_tokens = feats.reshape(steps * group_size, row_part)[pick]
-    send_tokens = send_tokens.reshape(peers, steps * capacity * row_part)
+    send_tokens = feats[pick].reshape(peers, steps * capacity, row_part)
+    arrived = lax.all_to_all(send_tokens, "ep", split_axis=0, concat_axis=0, tiled=True)
 
-    pieces = old_block.reshape(peers, (rows // peers) * cols)
-    first = lax.all_to_all(
-        jnp.concatenate([pieces, send_tokens], axis=1), "ep", split_axis=0, concat_axis=0, tiled=True
-    )
-    piece_len = pieces.shape[1]
-    gathered_pieces = jnp.take(first[:, :piece_len], sources, axis=0)
-    arrived = first[:, piece_len:].reshape(peers * steps * capacity, row_part)
+    new_block = lax.all_to_all(
+        jnp.take(staged, sources, axis=0), "ep", split_axis=0, concat_axis=0, tiled=True
+    ).reshape(rows, cols)
 
+    arrived = arrived.reshape(peers * steps * capacity, row_part)
     partial = jnp.dot(arrived, w_hi, preferred_element_type=jnp.float32) + jnp.dot(
         arrived, w_lo, preferred_element_type=jnp.float32
     )
     hidden = lax.psum_scatter(partial, "dp", scatter_dimension=1, tiled=True)
     act = jax.nn.silu(hidden).astype(jnp.bfloat16)
-    act = act.reshape(peers, steps * capacity * act.shape[1])
-
-    second = lax.all_to_all(
-        jnp.concatenate([gathered_pieces, act], axis=1), "ep", split_axis=0, concat_axis=0, tiled=True
-    )
-    new_block = second[:, :piece_len].reshape(rows, cols)
-    returned = second[:, piece_len:].reshape(peers * steps * capacity, -1)
+    act = act.reshape(peers, steps * capacity, act.shape[1])
+    returned = lax.all_to_all(act, "ep", split_axis=0, concat_axis=0, tiled=True)
+    returned = returned.reshape(peers * steps * capacity, -1)
     picked = returned[target].astype(jnp.float32).reshape(steps, group_size, top_count, -1)
     combined = jnp.sum(gate_values[:, :, :, None] * picked, axis=2).astype(jnp.bfloat16)
     return (combined, new_block[None])

time: 290 us -> 265 us (0.914)
  local copies, waits for them, and re-layouts: 73.7 us -> 28.2 us
  starting transfers between devices: 46.4 us -> 77.2 us
  blocking collectives: 6.95 us -> 0 us
  other arithmetic: 23.8 us -> 17.7 us
  waiting for transfers between devices: 116 us -> 119 us
    unnamed x33 -> x18, local copies, waits for them, and re-layouts: 43.8 us -> 0.91 us
    ppermute x0 -> x9, starting transfers between devices: none -> 27.9 us  [dp_exchange(): got.append(lax.ppermute(parts[(my_dp + shift) % n_dp], 'dp', pairs))]
    all_to_all x4 -> x0, other arithmetic: 9.97 us -> none  [the longest x2 5.39 us: shards(): lax.all_to_all(jnp.concatenate([pieces, send_tokens], axis=1), 'ep', spli...]
    ppermute x0 -> x9, waiting for transfers between devices: none -> 9.39 us  [dp_exchange(): got.append(lax.ppermute(parts[(my_dp + shift) % n_dp], 'dp', pairs))]
    all_gather x1 -> x0, blocking collectives: 6.95 us -> none  [shards(): lax.all_gather(scale_table[old_expert[my_slot]], 'dp', axis=1, tiled=True)]
    all_to_all x4, waiting for transfers between devices: 94.8 us -> 90.5 us  [the longest x1 50.2 us: shards(): lax.all_to_all(jnp.take(staged, sources, axis=0), 'ep', split_axis=0, con...]
    gather x2 -> x5, local copies, waits for them, and re-layouts: 4.99 us -> 8.68 us  [the longest x3 4.61 us: dp_exchange(): return by_shift[order]]
    all_to_all x4, starting transfers between devices: 46.4 us -> 49.3 us  [the longest x1 18.4 us: shards(): lax.all_to_all(send_tokens, 'ep', split_axis=0, concat_axis=0, tiled=True)]
  transfers between devices with their start and end apart: 5 -> 14, of which waited for: 3 -> 6; matrix products, arithmetic and copies ran while one was open for 17% -> 15% of each run, Pallas kernels for 0% -> 0%
where the time goes in v2:
time: 265 us; the launch traced here: 264 us
  waiting for transfers between devices  119 us (45%)
  starting transfers between devices  77.2 us (29%)
  local copies, waits for them, and re-layouts  28.2 us (11%)
  other arithmetic  17.7 us (7%)
  between operations  16.5 us (6%)
  matrix products  5.81 us (2%)
    all_to_all x1, waiting for transfers between devices, shards(): lax.all_to_all(jnp.take(staged, sources, axis=0), 'ep', split_axis=0, con...  50.2 us
    all_to_all x1, waiting for transfers between devices, shards(): lax.all_to_all(pieces, 'ep', split_axis=0, concat_axis=0, tiled=True)  31.3 us
    ppermute x9, starting transfers between devices, dp_exchange(): got.append(lax.ppermute(parts[(my_dp + shift) % n_dp], 'dp', pairs))  27.9 us
    reduce_scatter x1, waiting for transfers between devices, shards(): hidden = lax.psum_scatter(partial, 'dp', scatter_dimension=1, tiled=True)  18.8 us
    all_to_all x1, starting transfers between devices, shards(): lax.all_to_all(send_tokens, 'ep', split_axis=0, concat_axis=0, tiled=True)  18.4 us
    all_to_all x1, starting transfers between devices, shards(): lax.all_to_all(pieces, 'ep', split_axis=0, concat_axis=0, tiled=True)  16.2 us
    ppermute x9, waiting for transfers between devices, dp_exchange(): got.append(lax.ppermute(parts[(my_dp + shift) % n_dp], 'dp', pairs))  9.39 us
    all_to_all x1, waiting for transfers between devices, shards(): lax.all_to_all(act, 'ep', split_axis=0, concat_axis=0, tiled=True)  9.01 us
  transfers between devices with their start and end apart: 14, of which 6 were waited for; matrix products, arithmetic and copies ran while one was open for 15% of the time, Pallas kernels for 0%

profile of v2, /device:TPU:1, one launch (start us, length us, event | category | flops | bytes accessed | tf_op | source)
XLA Modules:
  0.0 264.2 jit_solution(16672659262043710350)
XLA Ops:
  7.2 0.8 reshape.269
  8.2 3.9 %collective-permute-start = (bf16[2,4,896]{2,1,0:T(4,128)(2,1)S(1)}, bf16[2,4,896]{2,1,0:T(4,128)(2,1)S(1)}, u32[]{:S(2)}, u32[]{:S(2)}) collective-permute-start(bf16[2,4,896]{2,1,0:T(4,128)(2,1)S(1)} %bitcast.93), channel_id=1, source_target_pairs={{0,1},{1,2},{2,3},{3,0},{4,5},{5,6},{6,7},{7,4},{8,9},{9,10},{10,1... | collective-permute-start | bytes 43016 | tf_op jit(solution)/shard_map/ppermute | solution.py:36
  12.2 4.4 %collective-permute-start.1 = (bf16[2,4,896]{2,1,0:T(4,128)(2,1)S(1)}, bf16[2,4,896]{2,1,0:T(4,128)(2,1)S(1)}, u32[]{:S(2)}, u32[]{:S(2)}) collective-permute-start(bf16[2,4,896]{2,1,0:T(4,128)(2,1)S(1)} %bitcast.94), channel_id=1, source_target_pairs={{0,2},{1,3},{2,0},{3,1},{4,6},{5,7},{6,4},{7,5},{8,10},{9,11},{10,... | collective-permute-start | bytes 43016 | tf_op jit(solution)/shard_map/ppermute | solution.py:36
  16.6 3.1 %collective-permute-start.2 = (bf16[2,4,896]{2,1,0:T(4,128)(2,1)S(1)}, bf16[2,4,896]{2,1,0:T(4,128)(2,1)S(1)}, u32[]{:S(2)}, u32[]{:S(2)}) collective-permute-start(bf16[2,4,896]{2,1,0:T(4,128)(2,1)S(1)} %bitcast.95), channel_id=1, source_target_pairs={{0,3},{1,0},{2,1},{3,2},{4,7},{5,4},{6,5},{7,6},{8,11},{9,8},{10,9... | collective-permute-start | bytes 43016 | tf_op jit(solution)/shard_map/ppermute | solution.py:36
  19.7 0.8 copy.44
  20.8 0.2 reduce_window_sum.11
  20.9 0.2 select_reduce_fusion
  21.2 0.8 select_reduce_fusion.1
  22.0 1.9 gather_fusion.1
  24.1 1.4 scatter_custom_fusion
  25.6 0.6 gather_fusion
  26.3 2.1 gather_fusion.2
  28.4 1.2 reshape.273
  29.5 18.4 %all-to-all-start = ((bf16[128,4,896]{2,1,0:T(4,128)(2,1)}), bf16[128,4,896]{2,1,0:T(4,128)(2,1)S(1)}, u32[]{:S(2)}, u32[]{:S(2)}) async-start(bf16[128,4,896]{2,1,0:T(4,128)(2,1)} %reshape.273), calls=%async_computation | async-start | bytes 1835008 | tf_op jit(solution)/shard_map/all_to_all | solution.py:85
  48.0 1.1 constant_dynamic-slice_fusion.5
  49.1 2.2 collective-permute-start.3
  51.4 2.5 collective-permute-start.4
  53.9 3.7 %collective-permute-start.5 = (bf16[896,256]{1,0:T(8,128)(2,1)}, bf16[896,256]{1,0:T(8,128)(2,1)}, u32[]{:S(2)}, u32[]{:S(2)}) collective-permute-start(bf16[896,256]{1,0:T(8,128)(2,1)} %get-tuple-element.7), channel_id=1, source_target_pairs={{0,3},{1,0},{2,1},{3,2},{4,7},{5,4},{6,5},{7,6},{8,11},{9,8},{10,9... | collective-permute-start | bytes 1376264 | tf_op jit(solution)/shard_map/ppermute | solution.py:36
  57.6 0.6 dynamic_slice.41
  60.5 2.5 collective-permute-start.6
  62.9 3.7 %collective-permute-start.7 = (f32[7,2]{0,1:T(2,128)S(1)}, f32[7,2]{0,1:T(2,128)S(1)}, u32[]{:S(2)}, u32[]{:S(2)}) collective-permute-start(f32[7,2]{0,1:T(2,128)S(1)} %bitcast.99), channel_id=1, source_target_pairs={{0,2},{1,3},{2,0},{3,1},{4,6},{5,7},{6,4},{7,5},{8,10},{9,11},{10,... | collective-permute-start | bytes 176 | tf_op jit(solution)/shard_map/ppermute | solution.py:36
  66.6 7.0 %collective-permute-done.6 = f32[7,2]{0,1:T(2,128)S(1)} collective-permute-done((f32[7,2]{0,1:T(2,128)S(1)}, f32[7,2]{0,1:T(2,128)S(1)}, u32[]{:S(2)}, u32[]{:S(2)}) %collective-permute-start.6) | collective-permute-done | bytes 88 | tf_op jit(solution)/shard_map/ppermute | solution.py:36
  73.6 1.9 collective-permute-start.8
  75.5 2.4 collective-permute-done.8
  77.9 0.6 gather_fusion.4
  78.7 2.8 %pad_maximum_fusion = bf16[4,896,256]{2,1,0:T(8,128)(2,1)} fusion(bf16[1,896,256]{2,1,0:T(8,128)(2,1)} %bitcast.20, bf16[1,896,256]{2,1,0:T(8,128)(2,1)} %bitcast.18, bf16[1,896,256]{2,1,0:T(8,128)(2,1)} %bitcast.16, bf16[1,896,256]{2,1,0:T(8,128)(2,1)S(1)} %get-tuple-element.6), kind=kLoop, calls=%fused_computation.13 | loop fusion | flops 2752512 | bytes 3670016 | tf_op jit(solution)/shard_map/stack | solution.py:37
  81.4 3.4 %gather_fusion.3 = bf16[4,896,256]{2,1,0:T(8,128)(2,1)} fusion(bf16[4,896,256]{2,1,0:T(8,128)(2,1)} %pad_maximum_fusion, s32[1024]{0:T(1024)S(1)} %pad_clamp_fusion.4), kind=kCustom, calls=%fused_computation.3 | custom fusion | bytes 3670032 | tf_op jit(solution)/shard_map/gather | solution.py:39
  84.9 3.6 %convert_bitcast_fusion = f32[896,4,256]{2,0,1:T(8,128)} fusion(bf16[4,896,256]{2,1,0:T(8,128)(2,1)} %gather_fusion.3), kind=kLoop, calls=%fused_computation.11 | loop fusion | flops 917504 | bytes 5505024 | tf_op jit(solution)/shard_map/convert_element_type | solution.py:66
  88.5 4.7 %copy.46 = f32[896,4,256]{0,2,1:T(8,128)} copy(f32[896,4,256]{2,0,1:T(8,128)} %convert_bitcast_fusion) | data formatting | bytes 7340032 | tf_op jit(solution)/shard_map/convert_element_type | solution.py:66
  93.1 4.7 %fusion = (bf16[896,8,128]{0,2,1:T(8,128)(2,1)}, bf16[896,8,128]{0,2,1:T(8,128)(2,1)}) fusion(f32[896,8,128]{0,2,1:T(8,128)} %bitcast.83, f32[896,8]{0,1:T(8,128)S(1)} %broadcast_bitcast_fusion), kind=kLoop, calls=%fused_computation.10 | loop fusion | flops 4587520 | bytes 7368704 | tf_op jit(solution)/shard_map/convert_element_type | solution.py:69
  97.8 1.2 reshape.274
  99.0 3.2 %fusion.13 = f32[512,1024]{1,0:T(8,128)S(1)} fusion(bf16[512,896]{1,0:T(8,128)(2,1)} %reshape.274, bf16[896,1024]{0,1:T(8,128)(2,1)} %bitcast.86), kind=kOutput, calls=%fused_computation.75 | convolution fusion | flops 939524096 | bytes 4849664 | tf_op jit(solution)/shard_map/dot_general | solution.py:92
  102.2 2.6 convolution_add_fusion
  104.8 1.5 reshape_squeeze.11
  106.4 16.2 %all-to-all-start.2 = ((bf16[128,28,256]{2,1,0:T(8,128)(2,1)}), bf16[128,28,256]{2,1,0:T(8,128)(2,1)S(1)}, u32[]{:S(2)}, u32[]{:S(2)}) async-start(bf16[128,28,256]{2,1,0:T(8,128)(2,1)} %reshape_squeeze.11), calls=%async_computation.3 | async-start | bytes 4194304 | tf_op jit(solution)/shard_map/all_to_all | solution.py:57
  122.6 18.8 %reduce-scatter.2.cloned.1.call-done = f32[512,256]{1,0:T(8,128)} async-done(((f32[512,1024]{1,0:T(8,128)}), f32[512,256]{1,0:T(8,128)}) %reduce-scatter.2.cloned.1.call-update) | async-done | bytes 524304 | tf_op jit(solution)/shard_map/reduce_scatter | solution.py:95
  141.5 1.2 multiply_convert_fusion
  142.7 0.8 reshape.277
  143.4 31.3 %all-to-all-done.2 = bf16[128,28,256]{2,1,0:T(8,128)(2,1)S(1)} async-done(((bf16[128,28,256]{2,1,0:T(8,128)(2,1)}), bf16[128,28,256]{2,1,0:T(8,128)(2,1)S(1)}, u32[]{:S(2)}, u32[]{:S(2)}) %all-to-all-start.2) | async-done | bytes 1835040 | tf_op jit(solution)/shard_map/all_to_all | solution.py:57
  174.7 7.7 %all-to-all-start.1 = ((bf16[128,4,256]{2,1,0:T(4,128)(2,1)}), bf16[128,4,256]{2,1,0:T(4,128)(2,1)S(1)}, u32[]{:S(2)}, u32[]{:S(2)}) async-start(bf16[128,4,256]{2,1,0:T(4,128)(2,1)} %reshape.277), calls=%async_computation.2 | async-start | bytes 524288 | tf_op jit(solution)/shard_map/all_to_all | solution.py:98
  182.5 2.0 gather_fusion.6
  184.5 3.2 %broadcast_select_fusion = bf16[128,28,256]{2,1,0:T(8,128)(2,1)} fusion(bf16[128,28,256]{2,1,0:T(8,128)(2,1)} %gather_fusion.6, pred[128]{0:T(512)(128)(4,1)S(1)} %compare_and_fusion), kind=kLoop, calls=%fused_computation.12 | loop fusion | flops 917504 | bytes 3670144 | tf_op jit(solution)/shard_map/jit(_take)/select_n | solution.py:88
  187.7 9.0 %all-to-all-done.1 = bf16[128,4,256]{2,1,0:T(4,128)(2,1)S(1)} async-done(((bf16[128,4,256]{2,1,0:T(4,128)(2,1)}), bf16[128,4,256]{2,1,0:T(4,128)(2,1)S(1)}, u32[]{:S(2)}, u32[]{:S(2)}) %all-to-all-start.1) | async-done | bytes 262176 | tf_op jit(solution)/shard_map/all_to_all | solution.py:98
  196.7 7.0 %all-to-all-start.3 = ((bf16[128,28,256]{2,1,0:T(8,128)(2,1)}), bf16[128,28,256]{2,1,0:T(8,128)(2,1)S(1)}, u32[]{:S(2)}, u32[]{:S(2)}) async-start(bf16[128,28,256]{2,1,0:T(8,128)(2,1)} %broadcast_select_fusion), calls=%async_computation.4 | async-start | bytes 4194304 | tf_op jit(solution)/shard_map/all_to_all | solution.py:87
  203.8 1.2 gather_fusion.5
  205.0 0.8 fusion.1
  205.7 50.2 %all-to-all-done.3 = bf16[128,28,256]{2,1,0:T(8,128)(2,1)S(1)} async-done(((bf16[128,28,256]{2,1,0:T(8,128)(2,1)}), bf16[128,28,256]{2,1,0:T(8,128)(2,1)S(1)}, u32[]{:S(2)}, u32[]{:S(2)}) %all-to-all-start.3) | async-done | bytes 1835040 | tf_op jit(solution)/shard_map/all_to_all | solution.py:87
  255.9 1.4 broadcast_in_dim_reshape.4
  (59 shorter events, 1.5 us)
Async XLA Ops:
  7.2 53.0 %copy-start = (f32[128,28,2]{0,2,1:T(2,128)S(1)}, f32[128,28,2]{0,2,1:T(2,128)}, u32[]{:S(2)}) copy-start(f32[128,28,2]{0,2,1:T(2,128)} %param.11) | copy-start | bytes 86020
  8.2 17.3 %collective-permute-start = (bf16[2,4,896]{2,1,0:T(4,128)(2,1)S(1)}, bf16[2,4,896]{2,1,0:T(4,128)(2,1)S(1)}, u32[]{:S(2)}, u32[]{:S(2)}) collective-permute-start(bf16[2,4,896]{2,1,0:T(4,128)(2,1)S(1)} %bitcast.93), channel_id=1, source_target_pairs={{0,1},{1,2},{2,3},{3,0},{4,5},{5,6},{6,7},{7,4},{8,9},{9,10},{10,1... | collective-permute-start | bytes 43016 | tf_op jit(solution)/shard_map/ppermute | solution.py:36
  12.2 13.3 %collective-permute-start.1 = (bf16[2,4,896]{2,1,0:T(4,128)(2,1)S(1)}, bf16[2,4,896]{2,1,0:T(4,128)(2,1)S(1)}, u32[]{:S(2)}, u32[]{:S(2)}) collective-permute-start(bf16[2,4,896]{2,1,0:T(4,128)(2,1)S(1)} %bitcast.94), channel_id=1, source_target_pairs={{0,2},{1,3},{2,0},{3,1},{4,6},{5,7},{6,4},{7,5},{8,10},{9,11},{10,... | collective-permute-start | bytes 43016 | tf_op jit(solution)/shard_map/ppermute | solution.py:36
  16.6 9.0 %collective-permute-start.2 = (bf16[2,4,896]{2,1,0:T(4,128)(2,1)S(1)}, bf16[2,4,896]{2,1,0:T(4,128)(2,1)S(1)}, u32[]{:S(2)}, u32[]{:S(2)}) collective-permute-start(bf16[2,4,896]{2,1,0:T(4,128)(2,1)S(1)} %bitcast.95), channel_id=1, source_target_pairs={{0,3},{1,0},{2,1},{3,2},{4,7},{5,4},{6,5},{7,6},{8,11},{9,8},{10,9... | collective-permute-start | bytes 43016 | tf_op jit(solution)/shard_map/ppermute | solution.py:36
  28.3 19.7 %copy-start.1 = (bf16[1,3584,256]{2,1,0:T(8,128)(2,1)S(1)}, bf16[1,3584,256]{2,1,0:T(8,128)(2,1)}, u32[]{:S(2)}) copy-start(bf16[1,3584,256]{2,1,0:T(8,128)(2,1)} %param.10) | copy-start | bytes 5505028
  29.5 68.3 %all-to-all-start = ((bf16[128,4,896]{2,1,0:T(4,128)(2,1)}), bf16[128,4,896]{2,1,0:T(4,128)(2,1)S(1)}, u32[]{:S(2)}, u32[]{:S(2)}) async-start(bf16[128,4,896]{2,1,0:T(4,128)(2,1)} %reshape.273), calls=%async_computation | async-start | bytes 1835008 | tf_op jit(solution)/shard_map/all_to_all | solution.py:85
  48.0 93.5 %reduce-scatter.2.cloned.1.call-start = ((), (), s32[]{:S(2)}) async-start(), calls=%async_computation.5 | async-start | bytes 2621440 | tf_op jit(solution)/shard_map/reduce_scatter | solution.py:95
  48.0 9.6 %copy-start.5 = (s32[128]{0:T(128)S(1)}, s32[128]{0:T(128)}, u32[]{:S(2)}) copy-start(s32[128]{0:T(128)} %param.12) | copy-start | bytes 1540
  49.1 29.5 %collective-permute-start.3 = (bf16[896,256]{1,0:T(8,128)(2,1)}, bf16[896,256]{1,0:T(8,128)(2,1)}, u32[]{:S(2)}, u32[]{:S(2)}) collective-permute-start(bf16[896,256]{1,0:T(8,128)(2,1)} %get-tuple-element.9), channel_id=1, source_target_pairs={{0,1},{1,2},{2,3},{3,0},{4,5},{5,6},{6,7},{7,4},{8,9},{9,10},{10,1... | collective-permute-start | bytes 1376264 | tf_op jit(solution)/shard_map/ppermute | solution.py:36
  51.4 27.3 %collective-permute-start.4 = (bf16[896,256]{1,0:T(8,128)(2,1)}, bf16[896,256]{1,0:T(8,128)(2,1)}, u32[]{:S(2)}, u32[]{:S(2)}) collective-permute-start(bf16[896,256]{1,0:T(8,128)(2,1)} %get-tuple-element.8), channel_id=1, source_target_pairs={{0,2},{1,3},{2,0},{3,1},{4,6},{5,7},{6,4},{7,5},{8,10},{9,11},{10,... | collective-permute-start | bytes 1376264 | tf_op jit(solution)/shard_map/ppermute | solution.py:36
  53.9 24.8 %collective-permute-start.5 = (bf16[896,256]{1,0:T(8,128)(2,1)}, bf16[896,256]{1,0:T(8,128)(2,1)}, u32[]{:S(2)}, u32[]{:S(2)}) collective-permute-start(bf16[896,256]{1,0:T(8,128)(2,1)} %get-tuple-element.7), channel_id=1, source_target_pairs={{0,3},{1,0},{2,1},{3,2},{4,7},{5,4},{6,5},{7,6},{8,11},{9,8},{10,9... | collective-permute-start | bytes 1376264 | tf_op jit(solution)/shard_map/ppermute | solution.py:36
  60.5 13.2 %collective-permute-start.6 = (f32[7,2]{0,1:T(2,128)S(1)}, f32[7,2]{0,1:T(2,128)S(1)}, u32[]{:S(2)}, u32[]{:S(2)}) collective-permute-start(f32[7,2]{0,1:T(2,128)S(1)} %bitcast.100), channel_id=1, source_target_pairs={{0,1},{1,2},{2,3},{3,0},{4,5},{5,6},{6,7},{7,4},{8,9},{9,10},{10,1... | collective-permute-start | bytes 176 | tf_op jit(solution)/shard_map/ppermute | solution.py:36
  62.9 12.6 %collective-permute-start.7 = (f32[7,2]{0,1:T(2,128)S(1)}, f32[7,2]{0,1:T(2,128)S(1)}, u32[]{:S(2)}, u32[]{:S(2)}) collective-permute-start(f32[7,2]{0,1:T(2,128)S(1)} %bitcast.99), channel_id=1, source_target_pairs={{0,2},{1,3},{2,0},{3,1},{4,6},{5,7},{6,4},{7,5},{8,10},{9,11},{10,... | collective-permute-start | bytes 176 | tf_op jit(solution)/shard_map/ppermute | solution.py:36
  73.6 4.3 %collective-permute-start.8 = (f32[7,2]{0,1:T(2,128)S(1)}, f32[7,2]{0,1:T(2,128)S(1)}, u32[]{:S(2)}, u32[]{:S(2)}) collective-permute-start(f32[7,2]{0,1:T(2,128)S(1)} %bitcast.98), channel_id=1, source_target_pairs={{0,3},{1,0},{2,1},{3,2},{4,7},{5,4},{6,5},{7,6},{8,11},{9,8},{10,9... | collective-permute-start | bytes 176 | tf_op jit(solution)/shard_map/ppermute | solution.py:36
  99.0 3.2 %copy-start.2 = (bf16[896,8,128]{0,2,1:T(8,128)(2,1)S(1)}, bf16[896,8,128]{0,2,1:T(8,128)(2,1)}, u32[]{:S(2)}) copy-start(bf16[896,8,128]{0,2,1:T(8,128)(2,1)} %get-tuple-element.4) | copy-start | bytes 5505028
  99.0 3.2 %copy-start.3 = (bf16[512,896]{1,0:T(8,128)(2,1)S(1)}, bf16[512,896]{1,0:T(8,128)(2,1)}, u32[]{:S(2)}) copy-start(bf16[512,896]{1,0:T(8,128)(2,1)} %reshape.274) | copy-start | bytes 2752516
  106.4 68.4 %all-to-all-start.2 = ((bf16[128,28,256]{2,1,0:T(8,128)(2,1)}), bf16[128,28,256]{2,1,0:T(8,128)(2,1)S(1)}, u32[]{:S(2)}, u32[]{:S(2)}) async-start(bf16[128,28,256]{2,1,0:T(8,128)(2,1)} %reshape_squeeze.11), calls=%async_computation.3 | async-start | bytes 4194304 | tf_op jit(solution)/shard_map/all_to_all | solution.py:57
  174.7 21.9 %all-to-all-start.1 = ((bf16[128,4,256]{2,1,0:T(4,128)(2,1)}), bf16[128,4,256]{2,1,0:T(4,128)(2,1)S(1)}, u32[]{:S(2)}, u32[]{:S(2)}) async-start(bf16[128,4,256]{2,1,0:T(4,128)(2,1)} %reshape.277), calls=%async_computation.2 | async-start | bytes 524288 | tf_op jit(solution)/shard_map/all_to_all | solution.py:98
  187.7 16.0 %copy-start.4 = (f32[2,16,8]{1,2,0:T(8,128)S(1)}, f32[2,16,8]{1,2,0:T(8,128)}, u32[]{:S(2)}) copy-start(f32[2,16,8]{1,2,0:T(8,128)} %param.9) | copy-start | bytes 3076
  196.7 59.2 %all-to-all-start.3 = ((bf16[128,28,256]{2,1,0:T(8,128)(2,1)}), bf16[128,28,256]{2,1,0:T(8,128)(2,1)S(1)}, u32[]{:S(2)}, u32[]{:S(2)}) async-start(bf16[128,28,256]{2,1,0:T(8,128)(2,1)} %broadcast_select_fusion), calls=%async_computation.4 | async-start | bytes 4194304 | tf_op jit(solution)/shard_map/all_to_all | solution.py:87
Sparse Core Ops, SparseCore 0:
  105.0 36.4 reduce-scatter.1

commit v3 on v2

--- a/solution.py
+++ b/solution.py
@@ -29,14 +29,12 @@
     return (slot * steps + step) * capacity + rank
 
 
-def dp_exchange(parts, n_dp, my_dp):
+def dp_shifts(parts, n_dp, my_dp):
     got = [parts[my_dp]]
     for shift in range(1, n_dp):
         pairs = [(k, (k + shift) % n_dp) for k in range(n_dp)]
         got.append(lax.ppermute(parts[(my_dp + shift) % n_dp], "dp", pairs))
-    by_shift = jnp.stack(got)
-    order = (my_dp - jnp.arange(n_dp, dtype=jnp.int32)) % n_dp
-    return by_shift[order]
+    return got
 
 
 def shards(tokens, routing, gate_values, held_weight, scale_table, old_expert, new_expert):
@@ -45,6 +43,7 @@
     my_slot = lax.axis_index("ep")
     my_dp = lax.axis_index("dp")
     steps, group_size, top_count = routing.shape
+    local_tokens = tokens.shape[1]
     capacity = 2
     old_block = held_weight[0]
     rows, cols = old_block.shape
@@ -56,45 +55,49 @@
     pieces = old_block.reshape(peers, rows // peers, cols)
     staged = lax.all_to_all(pieces, "ep", split_axis=0, concat_axis=0, tiled=True)
 
-    w_parts = dp_exchange(old_block.reshape(n_dp, row_part, cols), n_dp, my_dp)
-    w_rows = jnp.transpose(w_parts, (1, 0, 2)).reshape(row_part, n_dp * cols)
+    w_parts = dp_shifts(old_block.reshape(n_dp, row_part, cols), n_dp, my_dp)
     own_scales = scale_table[old_expert[my_slot]]
     row_blocks = row_part // blk
-    s_parts = dp_exchange(own_scales.reshape(n_dp, row_blocks, own_scales.shape[1]), n_dp, my_dp)
-    my_scales = jnp.transpose(s_parts, (1, 0, 2)).reshape(row_blocks, -1)
+    s_parts = dp_shifts(own_scales.reshape(n_dp, row_blocks, own_scales.shape[1]), n_dp, my_dp)
+    w_rows = jnp.concatenate(w_parts, axis=1)
+    my_scales = jnp.concatenate(s_parts, axis=1)
     widened = jnp.repeat(jnp.repeat(my_scales, blk, axis=0), blk, axis=1)
     w32 = w_rows.astype(jnp.float32) * widened
     hi32 = lax.reduce_precision(w32, exponent_bits=8, mantissa_bits=7)
     w_hi = hi32.astype(jnp.bfloat16)
     w_lo = (w32 - hi32).astype(jnp.bfloat16)
 
-    t_parts = dp_exchange(
-        jnp.transpose(tokens.reshape(steps, tokens.shape[1], n_dp, row_part), (2, 0, 1, 3)), n_dp, my_dp
+    t_parts = dp_shifts(
+        jnp.transpose(tokens.reshape(steps, local_tokens, n_dp, row_part), (2, 0, 1, 3)), n_dp, my_dp
     )
-    feats = jnp.transpose(t_parts, (1, 0, 2, 3)).reshape(steps * group_size, row_part)
+    feats = jnp.stack(t_parts).reshape(n_dp * steps * local_tokens, row_part)
 
     target = route_targets(routing, owners, peers, capacity)
     token_of = jnp.broadcast_to(
         jnp.arange(group_size, dtype=jnp.int32)[None, :, None], (steps, group_size, top_count)
     ).reshape(steps, -1)
     step_of = jnp.broadcast_to(jnp.arange(steps, dtype=jnp.int32)[:, None], token_of.shape)
-    pick = jnp.zeros((peers * steps * capacity,), jnp.int32).at[target.reshape(-1)].set(
-        (step_of * group_size + token_of).reshape(-1)
-    )
+    part_of = (my_dp - token_of // local_tokens) % n_dp
+    row_of = (part_of * steps + step_of) * local_tokens + token_of % local_tokens
+    pick = jnp.zeros((peers * steps * capacity,), jnp.int32).at[target.reshape(-1)].set(row_of.reshape(-1))
     send_tokens = feats[pick].reshape(peers, steps * capacity, row_part)
+    staged, send_tokens = lax.optimization_barrier((staged, send_tokens))
     arrived = lax.all_to_all(send_tokens, "ep", split_axis=0, concat_axis=0, tiled=True)
 
-    new_block = lax.all_to_all(
-        jnp.take(staged, sources, axis=0), "ep", split_axis=0, concat_axis=0, tiled=True
-    ).reshape(rows, cols)
+    regrouped, arrived = lax.optimization_barrier((jnp.take(staged, sources, axis=0), arrived))
+    new_block = lax.all_to_all(regrouped, "ep", split_axis=0, concat_axis=0, tiled=True).reshape(rows, cols)
 
     arrived = arrived.reshape(peers * steps * capacity, row_part)
     partial = jnp.dot(arrived, w_hi, preferred_element_type=jnp.float32) + jnp.dot(
         arrived, w_lo, preferred_element_type=jnp.float32
     )
-    hidden = lax.psum_scatter(partial, "dp", scatter_dimension=1, tiled=True)
+    hidden = partial[:, :cols]
+    for shift in range(1, n_dp):
+        pairs = [(k, (k - shift) % n_dp) for k in range(n_dp)]
+        hidden = hidden + lax.ppermute(partial[:, shift * cols:(shift + 1) * cols], "dp", pairs)
     act = jax.nn.silu(hidden).astype(jnp.bfloat16)
-    act = act.reshape(peers, steps * capacity, act.shape[1])
+    act = act.reshape(peers, steps * capacity, cols)
+    act, new_block = lax.optimization_barrier((act, new_block))
     returned = lax.all_to_all(act, "ep", split_axis=0, concat_axis=0, tiled=True)
     returned = returned.reshape(peers * steps * capacity, -1)
     picked = returned[target].astype(jnp.float32).reshape(steps, group_size, top_count, -1)

time: 265 us -> 230 us (0.87)
  waiting for transfers between devices: 119 us -> 91.5 us
  starting transfers between devices: 77.2 us -> 90.6 us
  between operations: 16.5 us -> 3.11 us
  other arithmetic: 17.7 us -> 10.6 us
    all_to_all x1, waiting for transfers between devices: 50.2 us -> 0.01 us  [shards(): lax.all_to_all(regrouped, 'ep', split_axis=0, concat_axis=0, tiled=True)]
    all_to_all x1, waiting for transfers between devices: 0.01 us -> 22.6 us  [shards(): lax.all_to_all(send_tokens, 'ep', split_axis=0, concat_axis=0, tiled=True)]
    reduce_scatter x1 -> x0, waiting for transfers between devices: 18.8 us -> none  [shards(): hidden = lax.psum_scatter(partial, 'dp', scatter_dimension=1, tiled=True)]
    ppermute x9 -> x12, starting transfers between devices: 27.9 us -> 41.9 us  [the longest x9 31.6 us: dp_shifts(): got.append(lax.ppermute(parts[(my_dp + shift) % n_dp], 'dp', pairs))]
    ppermute x9 -> x12, waiting for transfers between devices: 9.39 us -> 21.3 us  [the longest x3 18.2 us: shards(): lax.ppermute(partial[:, shift * cols:(shift + 1) * cols], 'dp', pairs)]
    all_to_all x1, starting transfers between devices: 18.4 us -> 7.72 us  [shards(): lax.all_to_all(send_tokens, 'ep', split_axis=0, concat_axis=0, tiled=True)]
    all_to_all x1, starting transfers between devices: 7.72 us -> 15.4 us  [shards(): lax.all_to_all(act, 'ep', split_axis=0, concat_axis=0, tiled=True)]
    concatenate x0 -> x5, local copies, waits for them, and re-layouts: none -> 6.89 us  [the longest x4 6.81 us: shards(): w_rows = jnp.concatenate(w_parts, axis=1)]
  transfers between devices with their start and end apart: 14 -> 16, of which waited for: 6 -> 7; matrix products, arithmetic and copies ran while one was open for 15% -> 16% of each run, Pallas kernels for 0% -> 0%
where the time goes in v3:
time: 230 us; the launch traced here: 228 us
  waiting for transfers between devices  91.5 us (40%)
  starting transfers between devices  90.6 us (39%)
  local copies, waits for them, and re-layouts  28.1 us (12%)
  other arithmetic  10.6 us (5%)
  matrix products  4.42 us (2%)
  between operations  3.11 us (1%)
    all_to_all x1, waiting for transfers between devices, shards(): lax.all_to_all(pieces, 'ep', split_axis=0, concat_axis=0, tiled=True)  33.5 us
    ppermute x9, starting transfers between devices, dp_shifts(): got.append(lax.ppermute(parts[(my_dp + shift) % n_dp], 'dp', pairs))  31.6 us
    all_to_all x1, waiting for transfers between devices, shards(): lax.all_to_all(send_tokens, 'ep', split_axis=0, concat_axis=0, tiled=True)  22.6 us
    all_to_all x1, starting transfers between devices, shards(): lax.all_to_all(pieces, 'ep', split_axis=0, concat_axis=0, tiled=True)  18.6 us
    ppermute x3, waiting for transfers between devices, shards(): lax.ppermute(partial[:, shift * cols:(shift + 1) * cols], 'dp', pairs)  18.2 us
    all_to_all x1, starting transfers between devices, shards(): lax.all_to_all(act, 'ep', split_axis=0, concat_axis=0, tiled=True)  15.4 us
    all_to_all x1, waiting for transfers between devices, shards(): lax.all_to_all(act, 'ep', split_axis=0, concat_axis=0, tiled=True)  14.1 us
    ppermute x3, starting transfers between devices, shards(): lax.ppermute(partial[:, shift * cols:(shift + 1) * cols], 'dp', pairs)  10.3 us
  transfers between devices with their start and end apart: 16, of which 7 were waited for; matrix products, arithmetic and copies ran while one was open for 16% of the time, Pallas kernels for 0%

profile of v3, /device:TPU:1, one launch (start us, length us, event | category | flops | bytes accessed | tf_op | source)
XLA Modules:
  0.0 228.2 jit_solution(643783699117861281)
XLA Ops:
  0.6 3.8 %reshape_squeeze.9 = bf16[128,28,256]{2,1,0:T(8,128)(2,1)} reshape(bf16[1,3584,256]{2,1,0:T(8,128)(2,1)} %param.10) | data formatting | bytes 3670016 | tf_op jit(solution)/shard_map/reshape;squeeze | solution.py:55
  4.4 18.6 %all-to-all-start = ((bf16[128,28,256]{2,1,0:T(8,128)(2,1)}), bf16[128,28,256]{2,1,0:T(8,128)(2,1)S(1)}, u32[]{:S(2)}, u32[]{:S(2)}) async-start(bf16[128,28,256]{2,1,0:T(8,128)(2,1)} %reshape_squeeze.9), calls=%async_computation | async-start | bytes 4194304 | tf_op jit(solution)/shard_map/all_to_all | solution.py:56
  23.3 3.1 %collective-permute-start = (bf16[2,4,896]{2,1,0:T(4,128)(2,1)S(1)}, bf16[2,4,896]{2,1,0:T(4,128)(2,1)S(1)}, u32[]{:S(2)}, u32[]{:S(2)}) collective-permute-start(bf16[2,4,896]{2,1,0:T(4,128)(2,1)S(1)} %bitcast.85), channel_id=1, source_target_pairs={{0,1},{1,2},{2,3},{3,0},{4,5},{5,6},{6,7},{7,4},{8,9},{9,10},{10,1... | collective-permute-start | bytes 43016 | tf_op jit(solution)/shard_map/ppermute | solution.py:36
  26.4 4.4 %collective-permute-start.1 = (bf16[2,4,896]{2,1,0:T(4,128)(2,1)S(1)}, bf16[2,4,896]{2,1,0:T(4,128)(2,1)S(1)}, u32[]{:S(2)}, u32[]{:S(2)}) collective-permute-start(bf16[2,4,896]{2,1,0:T(4,128)(2,1)S(1)} %bitcast.86), channel_id=1, source_target_pairs={{0,2},{1,3},{2,0},{3,1},{4,6},{5,7},{6,4},{7,5},{8,10},{9,11},{10,... | collective-permute-start | bytes 43016 | tf_op jit(solution)/shard_map/ppermute | solution.py:36
  30.8 3.1 %collective-permute-start.2 = (bf16[2,4,896]{2,1,0:T(4,128)(2,1)S(1)}, bf16[2,4,896]{2,1,0:T(4,128)(2,1)S(1)}, u32[]{:S(2)}, u32[]{:S(2)}) collective-permute-start(bf16[2,4,896]{2,1,0:T(4,128)(2,1)S(1)} %bitcast.87), channel_id=1, source_target_pairs={{0,3},{1,0},{2,1},{3,2},{4,7},{5,4},{6,5},{7,6},{8,11},{9,8},{10,9... | collective-permute-start | bytes 43016 | tf_op jit(solution)/shard_map/ppermute | solution.py:36
  34.2 0.2 reduce_window_sum.11
  34.6 0.2 select_reduce_fusion.2
  34.7 1.9 gather_fusion
  36.6 0.2 select_reduce_fusion
  36.9 1.4 scatter_custom_fusion
  38.4 2.1 gather_fusion.1
  40.5 1.1 reshape.225
  41.6 33.5 %all-to-all-done = bf16[128,28,256]{2,1,0:T(8,128)(2,1)S(1)} async-done(((bf16[128,28,256]{2,1,0:T(8,128)(2,1)}), bf16[128,28,256]{2,1,0:T(8,128)(2,1)S(1)}, u32[]{:S(2)}, u32[]{:S(2)}) %all-to-all-start) | async-done | bytes 1835040 | tf_op jit(solution)/shard_map/all_to_all | solution.py:56
  75.1 7.7 %all-to-all-start.1 = ((bf16[128,4,896]{2,1,0:T(4,128)(2,1)}), bf16[128,4,896]{2,1,0:T(4,128)(2,1)S(1)}, u32[]{:S(2)}, u32[]{:S(2)}) async-start(bf16[128,4,896]{2,1,0:T(4,128)(2,1)} %reshape.225), calls=%async_computation.1 | async-start | bytes 1835008 | tf_op jit(solution)/shard_map/all_to_all | solution.py:85
  82.9 2.0 gather_fusion.2
  84.9 3.2 %broadcast_select_fusion = bf16[128,28,256]{2,1,0:T(8,128)(2,1)} fusion(bf16[128,28,256]{2,1,0:T(8,128)(2,1)} %gather_fusion.2, pred[128]{0:T(512)(128)(4,1)S(1)} %compare_and_fusion), kind=kLoop, calls=%fused_computation.9 | loop fusion | flops 917504 | bytes 3670144 | tf_op jit(solution)/shard_map/jit(_take)/select_n | solution.py:87
  88.1 22.6 %all-to-all-done.1 = bf16[128,4,896]{2,1,0:T(4,128)(2,1)S(1)} async-done(((bf16[128,4,896]{2,1,0:T(4,128)(2,1)}), bf16[128,4,896]{2,1,0:T(4,128)(2,1)S(1)}, u32[]{:S(2)}, u32[]{:S(2)}) %all-to-all-start.1) | async-done | bytes 917536 | tf_op jit(solution)/shard_map/all_to_all | solution.py:85
  110.7 7.0 %all-to-all-start.2 = ((bf16[128,28,256]{2,1,0:T(8,128)(2,1)}), bf16[128,28,256]{2,1,0:T(8,128)(2,1)S(1)}, u32[]{:S(2)}, u32[]{:S(2)}) async-start(bf16[128,28,256]{2,1,0:T(8,128)(2,1)} %broadcast_select_fusion), calls=%async_computation.2 | async-start | bytes 4194304 | tf_op jit(solution)/shard_map/all_to_all | solution.py:88
  117.7 2.7 %constant_dynamic-slice_fusion.3 = (bf16[1,896,256]{2,1,0:T(8,128)(2,1)}, bf16[896,256]{1,0:T(8,128)(2,1)}, bf16[896,256]{1,0:T(8,128)(2,1)}, bf16[896,256]{1,0:T(8,128)(2,1)}) fusion(bf16[4,896,256]{2,1,0:T(8,128)(2,1)} %bitcast.76, s32[]{:T(128)S(6)} %select_n.133, s32[]{:T(128)S(6)} %select_n.139, s32[]{:T(128)S(6)} %select_n.137, s32[]{:T(128)S(6)} %select_n.135), kind=kLoop, calls=%fused_computation.50 | loop fusion | bytes 3670032 | tf_op jit(solution)/shard_map/dynamic_slice | solution.py:33
  120.4 3.1 %collective-permute-start.3 = (bf16[896,256]{1,0:T(8,128)(2,1)}, bf16[896,256]{1,0:T(8,128)(2,1)}, u32[]{:S(2)}, u32[]{:S(2)}) collective-permute-start(bf16[896,256]{1,0:T(8,128)(2,1)} %get-tuple-element.24), channel_id=1, source_target_pairs={{0,1},{1,2},{2,3},{3,0},{4,5},{5,6},{6,7},{7,4},{8,9},{9,10},{10,1... | collective-permute-start | bytes 1376264 | tf_op jit(solution)/shard_map/ppermute | solution.py:36
  123.5 4.4 %collective-permute-start.4 = (bf16[896,256]{1,0:T(8,128)(2,1)}, bf16[896,256]{1,0:T(8,128)(2,1)}, u32[]{:S(2)}, u32[]{:S(2)}) collective-permute-start(bf16[896,256]{1,0:T(8,128)(2,1)} %get-tuple-element.23), channel_id=1, source_target_pairs={{0,2},{1,3},{2,0},{3,1},{4,6},{5,7},{6,4},{7,5},{8,10},{9,11},{10,... | collective-permute-start | bytes 1376264 | tf_op jit(solution)/shard_map/ppermute | solution.py:36
  127.8 3.1 %collective-permute-start.5 = (bf16[896,256]{1,0:T(8,128)(2,1)}, bf16[896,256]{1,0:T(8,128)(2,1)}, u32[]{:S(2)}, u32[]{:S(2)}) collective-permute-start(bf16[896,256]{1,0:T(8,128)(2,1)} %get-tuple-element.22), channel_id=1, source_target_pairs={{0,3},{1,0},{2,1},{3,2},{4,7},{5,4},{6,5},{7,6},{8,11},{9,8},{10,9... | collective-permute-start | bytes 1376264 | tf_op jit(solution)/shard_map/ppermute | solution.py:36
  130.9 0.6 dynamic_slice.41
  133.8 2.2 collective-permute-start.6
  136.0 2.8 %collective-permute-start.7 = (f32[7,2]{0,1:T(2,128)S(1)}, f32[7,2]{0,1:T(2,128)S(1)}, u32[]{:S(2)}, u32[]{:S(2)}) collective-permute-start(f32[7,2]{0,1:T(2,128)S(1)} %bitcast.91), channel_id=1, source_target_pairs={{0,2},{1,3},{2,0},{3,1},{4,6},{5,7},{6,4},{7,5},{8,10},{9,11},{10,... | collective-permute-start | bytes 176 | tf_op jit(solution)/shard_map/ppermute | solution.py:36
  138.8 1.1 concatenate.16
  139.9 2.5 %collective-permute-done.6 = f32[7,2]{0,1:T(2,128)S(1)} collective-permute-done((f32[7,2]{0,1:T(2,128)S(1)}, f32[7,2]{0,1:T(2,128)S(1)}, u32[]{:S(2)}, u32[]{:S(2)}) %collective-permute-start.6) | collective-permute-done | bytes 88 | tf_op jit(solution)/shard_map/ppermute | solution.py:36
  142.5 5.6 %collective-permute-start.8 = (f32[7,2]{0,1:T(2,128)S(1)}, f32[7,2]{0,1:T(2,128)S(1)}, u32[]{:S(2)}, u32[]{:S(2)}) collective-permute-start(f32[7,2]{0,1:T(2,128)S(1)} %bitcast.90), channel_id=1, source_target_pairs={{0,3},{1,0},{2,1},{3,2},{4,7},{5,4},{6,5},{7,6},{8,11},{9,8},{10,9... | collective-permute-start | bytes 176 | tf_op jit(solution)/shard_map/ppermute | solution.py:36
  148.1 0.5 collective-permute-done.8
  148.7 1.9 concatenate.17
  150.6 1.9 concatenate.18
  152.5 1.9 concatenate.19
  154.4 5.6 %reduce-precision_convert_fusion = (bf16[896,8,128]{2,1,0:T(8,128)(2,1)}, bf16[896,8,128]{2,1,0:T(8,128)(2,1)}) fusion(f32[896,8]{1,0:T(8,128)S(1)} %bitcast.77, bf16[896,2,128]{2,1,0:T(2,128)(2,1)} %concatenate.19, bf16[896,2,128]{2,1,0:T(2,128)(2,1)} %concatenate.18, bf16[896,2,128]{2,1,0:T(2,128)(2,1)} %concatenate.17, bf16[896,2,128]{2,1,0:T(2,128)(2,1)S(1)} %concatenate.16), kind=kLoop, calls=%fused_computation.6 | loop fusion | flops 11927552 | bytes 5533696 | tf_op jit(solution)/shard_map/convert_element_type | solution.py:67
  160.0 1.1 reshape.226
  161.1 3.2 %fusion.1 = f32[512,1024]{1,0:T(8,128)S(1)} fusion(bf16[512,896]{1,0:T(8,128)(2,1)} %reshape.226, bf16[112,8,8,128]{3,2,1,0:T(8,128)(2,1)} %bitcast.80), kind=kOutput, calls=%fused_computation.10 | convolution fusion | flops 939524096 | bytes 4849664 | tf_op jit(solution)/shard_map/dot_general | solution.py:91
  164.3 1.3 fusion.7
  165.7 3.7 %collective-permute-start.10 = (f32[512,256]{1,0:T(8,128)S(1)}, f32[512,256]{1,0:T(8,128)S(1)}, u32[]{:S(2)}, u32[]{:S(2)}) collective-permute-start(f32[512,256]{1,0:T(8,128)S(1)} %get-tuple-element.20), channel_id=1, source_target_pairs={{0,2},{1,3},{2,0},{3,1},{4,6},{5,7},{6,4},{7,5},{8,10},{9,11},{10,... | collective-permute-start | bytes 1572872 | tf_op jit(solution)/shard_map/ppermute | solution.py:97
  169.5 3.9 %collective-permute-start.11 = (f32[512,256]{1,0:T(8,128)S(1)}, f32[512,256]{1,0:T(8,128)S(1)}, u32[]{:S(2)}, u32[]{:S(2)}) collective-permute-start(f32[512,256]{1,0:T(8,128)S(1)} %get-tuple-element.19), channel_id=1, source_target_pairs={{0,1},{1,2},{2,3},{3,0},{4,5},{5,6},{6,7},{7,4},{8,9},{9,10},{10,1... | collective-permute-start | bytes 1572872 | tf_op jit(solution)/shard_map/ppermute | solution.py:97
  173.3 2.7 %collective-permute-start.9 = (f32[512,256]{1,0:T(8,128)S(1)}, f32[512,256]{1,0:T(8,128)S(1)}, u32[]{:S(2)}, u32[]{:S(2)}) collective-permute-start(f32[512,256]{1,0:T(8,128)S(1)} %get-tuple-element.18), channel_id=1, source_target_pairs={{0,3},{1,0},{2,1},{3,2},{4,7},{5,4},{6,5},{7,6},{8,11},{9,8},{10,9... | collective-permute-start | bytes 1572872 | tf_op jit(solution)/shard_map/ppermute | solution.py:97
  176.0 4.0 %collective-permute-done.10 = f32[512,256]{1,0:T(8,128)S(1)} collective-permute-done((f32[512,256]{1,0:T(8,128)S(1)}, f32[512,256]{1,0:T(8,128)S(1)}, u32[]{:S(2)}, u32[]{:S(2)}) %collective-permute-start.10) | collective-permute-done | bytes 524320 | tf_op jit(solution)/shard_map/ppermute | solution.py:97
  180.0 14.2 %collective-permute-done.11 = f32[512,256]{1,0:T(8,128)S(1)} collective-permute-done((f32[512,256]{1,0:T(8,128)S(1)}, f32[512,256]{1,0:T(8,128)S(1)}, u32[]{:S(2)}, u32[]{:S(2)}) %collective-permute-start.11) | collective-permute-done | bytes 524320 | tf_op jit(solution)/shard_map/ppermute | solution.py:97
  194.2 0.2 multiply_convert_fusion
  194.4 0.8 reshape.228
  195.2 1.4 reshape.229
  196.6 15.4 %all-to-all-start.3 = ((bf16[128,4,256]{2,1,0:T(4,128)(2,1)}), bf16[128,4,256]{2,1,0:T(4,128)(2,1)S(1)}, u32[]{:S(2)}, u32[]{:S(2)}) async-start(bf16[128,4,256]{2,1,0:T(4,128)(2,1)} %reshape.228), calls=%async_computation.3 | async-start | bytes 524288 | tf_op jit(solution)/shard_map/all_to_all | solution.py:101
  212.1 14.1 %all-to-all-done.3 = bf16[128,4,256]{2,1,0:T(4,128)(2,1)S(1)} async-done(((bf16[128,4,256]{2,1,0:T(4,128)(2,1)}), bf16[128,4,256]{2,1,0:T(4,128)(2,1)S(1)}, u32[]{:S(2)}, u32[]{:S(2)}) %all-to-all-start.3) | async-done | bytes 262176 | tf_op jit(solution)/shard_map/all_to_all | solution.py:101
  226.3 1.2 gather_fusion.3
  227.4 0.8 fusion.12
  (61 shorter events, 1.5 us)
Async XLA Ops:
  0.6 132.8 %copy-start = (f32[128,28,2]{0,2,1:T(2,128)S(1)}, f32[128,28,2]{0,2,1:T(2,128)}, u32[]{:S(2)}) copy-start(f32[128,28,2]{0,2,1:T(2,128)} %param.11) | copy-start | bytes 86020
  4.4 18.6 %copy-start.3 = (bf16[2,4,3584]{2,1,0:T(4,128)(2,1)S(1)}, bf16[2,4,3584]{2,1,0:T(4,128)(2,1)}, u32[]{:S(2)}) copy-start(bf16[2,4,3584]{2,1,0:T(4,128)(2,1)} %param.7) | copy-start | bytes 172036
  4.4 29.4 %copy-start.4 = (s32[2,16,8]{1,2,0:T(8,128)S(1)}, s32[2,16,8]{1,2,0:T(8,128)}, u32[]{:S(2)}) copy-start(s32[2,16,8]{1,2,0:T(8,128)} %param.8) | copy-start | bytes 3076
  4.4 30.1 %copy-start.6 = (s32[128]{0:T(128)S(1)}, s32[128]{0:T(128)}, u32[]{:S(2)}) copy-start(s32[128]{0:T(128)} %param.13) | copy-start | bytes 1540
  4.4 30.1 %copy-start.7 = (s32[128]{0:T(128)S(1)}, s32[128]{0:T(128)}, u32[]{:S(2)}) copy-start(s32[128]{0:T(128)} %param.12) | copy-start | bytes 1540
  4.4 70.7 %all-to-all-start = ((bf16[128,28,256]{2,1,0:T(8,128)(2,1)}), bf16[128,28,256]{2,1,0:T(8,128)(2,1)S(1)}, u32[]{:S(2)}, u32[]{:S(2)}) async-start(bf16[128,28,256]{2,1,0:T(8,128)(2,1)} %reshape_squeeze.9), calls=%async_computation | async-start | bytes 4194304 | tf_op jit(solution)/shard_map/all_to_all | solution.py:56
  23.3 15.0 %collective-permute-start = (bf16[2,4,896]{2,1,0:T(4,128)(2,1)S(1)}, bf16[2,4,896]{2,1,0:T(4,128)(2,1)S(1)}, u32[]{:S(2)}, u32[]{:S(2)}) collective-permute-start(bf16[2,4,896]{2,1,0:T(4,128)(2,1)S(1)} %bitcast.85), channel_id=1, source_target_pairs={{0,1},{1,2},{2,3},{3,0},{4,5},{5,6},{6,7},{7,4},{8,9},{9,10},{10,1... | collective-permute-start | bytes 43016 | tf_op jit(solution)/shard_map/ppermute | solution.py:36
  26.4 11.9 %collective-permute-start.1 = (bf16[2,4,896]{2,1,0:T(4,128)(2,1)S(1)}, bf16[2,4,896]{2,1,0:T(4,128)(2,1)S(1)}, u32[]{:S(2)}, u32[]{:S(2)}) collective-permute-start(bf16[2,4,896]{2,1,0:T(4,128)(2,1)S(1)} %bitcast.86), channel_id=1, source_target_pairs={{0,2},{1,3},{2,0},{3,1},{4,6},{5,7},{6,4},{7,5},{8,10},{9,11},{10,... | collective-permute-start | bytes 43016 | tf_op jit(solution)/shard_map/ppermute | solution.py:36
  30.8 7.5 %collective-permute-start.2 = (bf16[2,4,896]{2,1,0:T(4,128)(2,1)S(1)}, bf16[2,4,896]{2,1,0:T(4,128)(2,1)S(1)}, u32[]{:S(2)}, u32[]{:S(2)}) collective-permute-start(bf16[2,4,896]{2,1,0:T(4,128)(2,1)S(1)} %bitcast.87), channel_id=1, source_target_pairs={{0,3},{1,0},{2,1},{3,2},{4,7},{5,4},{6,5},{7,6},{8,11},{9,8},{10,9... | collective-permute-start | bytes 43016 | tf_op jit(solution)/shard_map/ppermute | solution.py:36
  75.1 35.6 %all-to-all-start.1 = ((bf16[128,4,896]{2,1,0:T(4,128)(2,1)}), bf16[128,4,896]{2,1,0:T(4,128)(2,1)S(1)}, u32[]{:S(2)}, u32[]{:S(2)}) async-start(bf16[128,4,896]{2,1,0:T(4,128)(2,1)} %reshape.225), calls=%async_computation.1 | async-start | bytes 1835008 | tf_op jit(solution)/shard_map/all_to_all | solution.py:85
  110.7 84.5 %all-to-all-start.2 = ((bf16[128,28,256]{2,1,0:T(8,128)(2,1)}), bf16[128,28,256]{2,1,0:T(8,128)(2,1)S(1)}, u32[]{:S(2)}, u32[]{:S(2)}) async-start(bf16[128,28,256]{2,1,0:T(8,128)(2,1)} %broadcast_select_fusion), calls=%async_computation.2 | async-start | bytes 4194304 | tf_op jit(solution)/shard_map/all_to_all | solution.py:88
  120.4 28.3 %collective-permute-start.3 = (bf16[896,256]{1,0:T(8,128)(2,1)}, bf16[896,256]{1,0:T(8,128)(2,1)}, u32[]{:S(2)}, u32[]{:S(2)}) collective-permute-start(bf16[896,256]{1,0:T(8,128)(2,1)} %get-tuple-element.24), channel_id=1, source_target_pairs={{0,1},{1,2},{2,3},{3,0},{4,5},{5,6},{6,7},{7,4},{8,9},{9,10},{10,1... | collective-permute-start | bytes 1376264 | tf_op jit(solution)/shard_map/ppermute | solution.py:36
  123.5 27.1 %collective-permute-start.4 = (bf16[896,256]{1,0:T(8,128)(2,1)}, bf16[896,256]{1,0:T(8,128)(2,1)}, u32[]{:S(2)}, u32[]{:S(2)}) collective-permute-start(bf16[896,256]{1,0:T(8,128)(2,1)} %get-tuple-element.23), channel_id=1, source_target_pairs={{0,2},{1,3},{2,0},{3,1},{4,6},{5,7},{6,4},{7,5},{8,10},{9,11},{10,... | collective-permute-start | bytes 1376264 | tf_op jit(solution)/shard_map/ppermute | solution.py:36
  127.8 24.6 %collective-permute-start.5 = (bf16[896,256]{1,0:T(8,128)(2,1)}, bf16[896,256]{1,0:T(8,128)(2,1)}, u32[]{:S(2)}, u32[]{:S(2)}) collective-permute-start(bf16[896,256]{1,0:T(8,128)(2,1)} %get-tuple-element.22), channel_id=1, source_target_pairs={{0,3},{1,0},{2,1},{3,2},{4,7},{5,4},{6,5},{7,6},{8,11},{9,8},{10,9... | collective-permute-start | bytes 1376264 | tf_op jit(solution)/shard_map/ppermute | solution.py:36
  133.8 8.7 %collective-permute-start.6 = (f32[7,2]{0,1:T(2,128)S(1)}, f32[7,2]{0,1:T(2,128)S(1)}, u32[]{:S(2)}, u32[]{:S(2)}) collective-permute-start(f32[7,2]{0,1:T(2,128)S(1)} %bitcast.92), channel_id=1, source_target_pairs={{0,1},{1,2},{2,3},{3,0},{4,5},{5,6},{6,7},{7,4},{8,9},{9,10},{10,1... | collective-permute-start | bytes 176 | tf_op jit(solution)/shard_map/ppermute | solution.py:36
  136.0 12.1 %collective-permute-start.7 = (f32[7,2]{0,1:T(2,128)S(1)}, f32[7,2]{0,1:T(2,128)S(1)}, u32[]{:S(2)}, u32[]{:S(2)}) collective-permute-start(f32[7,2]{0,1:T(2,128)S(1)} %bitcast.91), channel_id=1, source_target_pairs={{0,2},{1,3},{2,0},{3,1},{4,6},{5,7},{6,4},{7,5},{8,10},{9,11},{10,... | collective-permute-start | bytes 176 | tf_op jit(solution)/shard_map/ppermute | solution.py:36
  142.5 6.1 %collective-permute-start.8 = (f32[7,2]{0,1:T(2,128)S(1)}, f32[7,2]{0,1:T(2,128)S(1)}, u32[]{:S(2)}, u32[]{:S(2)}) collective-permute-start(f32[7,2]{0,1:T(2,128)S(1)} %bitcast.90), channel_id=1, source_target_pairs={{0,3},{1,0},{2,1},{3,2},{4,7},{5,4},{6,5},{7,6},{8,11},{9,8},{10,9... | collective-permute-start | bytes 176 | tf_op jit(solution)/shard_map/ppermute | solution.py:36
  161.1 3.2 %copy-start.1 = (bf16[896,8,128]{2,1,0:T(8,128)(2,1)S(1)}, bf16[896,8,128]{2,1,0:T(8,128)(2,1)}, u32[]{:S(2)}) copy-start(bf16[896,8,128]{2,1,0:T(8,128)(2,1)} %get-tuple-element.16) | copy-start | bytes 5505028
  161.1 3.2 %copy-start.2 = (bf16[512,896]{1,0:T(8,128)(2,1)S(1)}, bf16[512,896]{1,0:T(8,128)(2,1)}, u32[]{:S(2)}) copy-start(bf16[512,896]{1,0:T(8,128)(2,1)} %reshape.226) | copy-start | bytes 2752516
  165.7 14.3 %collective-permute-start.10 = (f32[512,256]{1,0:T(8,128)S(1)}, f32[512,256]{1,0:T(8,128)S(1)}, u32[]{:S(2)}, u32[]{:S(2)}) collective-permute-start(f32[512,256]{1,0:T(8,128)S(1)} %get-tuple-element.20), channel_id=1, source_target_pairs={{0,2},{1,3},{2,0},{3,1},{4,6},{5,7},{6,4},{7,5},{8,10},{9,11},{10,... | collective-permute-start | bytes 1572872 | tf_op jit(solution)/shard_map/ppermute | solution.py:97
  169.5 24.7 %collective-permute-start.11 = (f32[512,256]{1,0:T(8,128)S(1)}, f32[512,256]{1,0:T(8,128)S(1)}, u32[]{:S(2)}, u32[]{:S(2)}) collective-permute-start(f32[512,256]{1,0:T(8,128)S(1)} %get-tuple-element.19), channel_id=1, source_target_pairs={{0,1},{1,2},{2,3},{3,0},{4,5},{5,6},{6,7},{7,4},{8,9},{9,10},{10,1... | collective-permute-start | bytes 1572872 | tf_op jit(solution)/shard_map/ppermute | solution.py:97
  173.3 20.9 %collective-permute-start.9 = (f32[512,256]{1,0:T(8,128)S(1)}, f32[512,256]{1,0:T(8,128)S(1)}, u32[]{:S(2)}, u32[]{:S(2)}) collective-permute-start(f32[512,256]{1,0:T(8,128)S(1)} %get-tuple-element.18), channel_id=1, source_target_pairs={{0,3},{1,0},{2,1},{3,2},{4,7},{5,4},{6,5},{7,6},{8,11},{9,8},{10,9... | collective-permute-start | bytes 1572872 | tf_op jit(solution)/shard_map/ppermute | solution.py:97
  195.2 16.8 %copy-start.5 = (f32[2,16,8]{1,2,0:T(8,128)S(1)}, f32[2,16,8]{1,2,0:T(8,128)}, u32[]{:S(2)}) copy-start(f32[2,16,8]{1,2,0:T(8,128)} %param.9) | copy-start | bytes 3076
  196.6 29.6 %all-to-all-start.3 = ((bf16[128,4,256]{2,1,0:T(4,128)(2,1)}), bf16[128,4,256]{2,1,0:T(4,128)(2,1)S(1)}, u32[]{:S(2)}, u32[]{:S(2)}) async-start(bf16[128,4,256]{2,1,0:T(4,128)(2,1)} %reshape.228), calls=%async_computation.3 | async-start | bytes 524288 | tf_op jit(solution)/shard_map/all_to_all | solution.py:101

commit v4 on v3

--- a/solution.py
+++ b/solution.py
@@ -55,22 +55,22 @@
     pieces = old_block.reshape(peers, rows // peers, cols)
     staged = lax.all_to_all(pieces, "ep", split_axis=0, concat_axis=0, tiled=True)
 
-    w_parts = dp_shifts(old_block.reshape(n_dp, row_part, cols), n_dp, my_dp)
     own_scales = scale_table[old_expert[my_slot]]
-    row_blocks = row_part // blk
-    s_parts = dp_shifts(own_scales.reshape(n_dp, row_blocks, own_scales.shape[1]), n_dp, my_dp)
-    w_rows = jnp.concatenate(w_parts, axis=1)
-    my_scales = jnp.concatenate(s_parts, axis=1)
-    widened = jnp.repeat(jnp.repeat(my_scales, blk, axis=0), blk, axis=1)
-    w32 = w_rows.astype(jnp.float32) * widened
+    widened = jnp.repeat(jnp.repeat(own_scales, blk, axis=0), blk, axis=1)
+    w32 = old_block.astype(jnp.float32) * widened
     hi32 = lax.reduce_precision(w32, exponent_bits=8, mantissa_bits=7)
-    w_hi = hi32.astype(jnp.bfloat16)
-    w_lo = (w32 - hi32).astype(jnp.bfloat16)
-
-    t_parts = dp_shifts(
-        jnp.transpose(tokens.reshape(steps, local_tokens, n_dp, row_part), (2, 0, 1, 3)), n_dp, my_dp
+    w_pair = jnp.stack([hi32.astype(jnp.bfloat16), (w32 - hi32).astype(jnp.bfloat16)])
+    w_out = jnp.transpose(w_pair.reshape(2, n_dp, row_part, cols), (1, 0, 2, 3))
+    t_out = jnp.transpose(tokens.reshape(steps, local_tokens, n_dp, row_part), (2, 0, 1, 3))
+    token_rows = steps * local_tokens * row_part // cols
+    payload = jnp.concatenate(
+        [t_out.reshape(n_dp, token_rows, cols), w_out.reshape(n_dp, 2 * row_part, cols)], axis=1
     )
-    feats = jnp.stack(t_parts).reshape(n_dp * steps * local_tokens, row_part)
+    got = dp_shifts(payload, n_dp, my_dp)
+    feats = jnp.stack([g[:token_rows] for g in got]).reshape(n_dp * steps * local_tokens, row_part)
+    w_got = [g[token_rows:].reshape(2, row_part, cols) for g in got]
+    w_hi = jnp.concatenate([w[0] for w in w_got], axis=1)
+    w_lo = jnp.concatenate([w[1] for w in w_got], axis=1)
 
     target = route_targets(routing, owners, peers, capacity)
     token_of = jnp.broadcast_to(
@@ -81,7 +81,7 @@
     row_of = (part_of * steps + step_of) * local_tokens + token_of % local_tokens
     pick = jnp.zeros((peers * steps * capacity,), jnp.int32).at[target.reshape(-1)].set(row_of.reshape(-1))
     send_tokens = feats[pick].reshape(peers, steps * capacity, row_part)
-    staged, send_tokens = lax.optimization_barrier((staged, send_tokens))
+    staged, send_tokens, w_hi, w_lo = lax.optimization_barrier((staged, send_tokens, w_hi, w_lo))
     arrived = lax.all_to_all(send_tokens, "ep", split_axis=0, concat_axis=0, tiled=True)
 
     regrouped, arrived = lax.optimization_barrier((jnp.take(staged, sources, axis=0), arrived))

time: 230 us -> 231 us (level)
  starting transfers between devices: 90.6 us -> 60.1 us
  waiting for transfers between devices: 91.5 us -> 109 us
  local copies, waits for them, and re-layouts: 28.1 us -> 39.1 us
  other arithmetic: 10.6 us -> 14.3 us
    ppermute x9 -> x3, starting transfers between devices: 31.6 us -> 11.3 us  [dp_shifts(): got.append(lax.ppermute(parts[(my_dp + shift) % n_dp], 'dp', pairs))]
    all_to_all x1, waiting for transfers between devices: 0.01 us -> 17.3 us  [shards(): lax.all_to_all(regrouped, 'ep', split_axis=0, concat_axis=0, tiled=True)]
    all_to_all x1, waiting for transfers between devices: 33.5 us -> 25.1 us  [shards(): lax.all_to_all(pieces, 'ep', split_axis=0, concat_axis=0, tiled=True)]
    all_to_all x1, starting transfers between devices: 15.4 us -> 7.68 us  [shards(): lax.all_to_all(act, 'ep', split_axis=0, concat_axis=0, tiled=True)]
    concatenate x5 -> x0, local copies, waits for them, and re-layouts: 6.89 us -> none  [the longest x4 6.81 us: shards(): w_rows = jnp.concatenate(w_parts, axis=1)]
    ppermute x9 -> x3, waiting for transfers between devices: 3.08 us -> 9.67 us  [dp_shifts(): got.append(lax.ppermute(parts[(my_dp + shift) % n_dp], 'dp', pairs))]
    concatenate x1 -> x2, other arithmetic: 0.01 us -> 6.23 us  [the longest x1 4.11 us: shards(): jnp.concatenate([t_out.reshape(n_dp, token_rows, cols), w_out.reshape(n_d...]
    reshape x1 -> x3, local copies, waits for them, and re-layouts: 0.02 us -> 6.03 us  [the longest x1 5.91 us: shards(): widened = jnp.repeat(jnp.repeat(own_scales, blk, axis=0), blk, axis=1)]
  transfers between devices with their start and end apart: 16 -> 10, of which waited for: 7 -> 9; matrix products, arithmetic and copies ran while one was open for 16% -> 13% of each run, Pallas kernels for 0% -> 0%
where the time goes in v4:
time: 231 us; the launch traced here: 230 us
  waiting for transfers between devices  109 us (47%)
  starting transfers between devices  60.1 us (26%)
  local copies, waits for them, and re-layouts  39.1 us (17%)
  other arithmetic  14.3 us (6%)
  matrix products  4.43 us (2%)
  between operations  3.01 us (1%)
    all_to_all x1, waiting for transfers between devices, shards(): lax.all_to_all(pieces, 'ep', split_axis=0, concat_axis=0, tiled=True)  25.1 us
    all_to_all x1, waiting for transfers between devices, shards(): lax.all_to_all(send_tokens, 'ep', split_axis=0, concat_axis=0, tiled=True)  22.6 us
    ppermute x3, waiting for transfers between devices, shards(): lax.ppermute(partial[:, shift * cols:(shift + 1) * cols], 'dp', pairs)  20.3 us
    all_to_all x1, starting transfers between devices, shards(): lax.all_to_all(pieces, 'ep', split_axis=0, concat_axis=0, tiled=True)  18.6 us
    all_to_all x1, waiting for transfers between devices, shards(): lax.all_to_all(regrouped, 'ep', split_axis=0, concat_axis=0, tiled=True)  17.3 us
    all_to_all x1, waiting for transfers between devices, shards(): lax.all_to_all(act, 'ep', split_axis=0, concat_axis=0, tiled=True)  14.1 us
    ppermute x3, starting transfers between devices, dp_shifts(): got.append(lax.ppermute(parts[(my_dp + shift) % n_dp], 'dp', pairs))  11.3 us
    ppermute x3, waiting for transfers between devices, dp_shifts(): got.append(lax.ppermute(parts[(my_dp + shift) % n_dp], 'dp', pairs))  9.67 us
  transfers between devices with their start and end apart: 10, of which 9 were waited for; matrix products, arithmetic and copies ran while one was open for 13% of the time, Pallas kernels for 0%

profile of v4, /device:TPU:1, one launch (start us, length us, event | category | flops | bytes accessed | tf_op | source)
XLA Modules:
  0.0 230.0 jit_solution(6705026528370180933)
XLA Ops:
  0.7 1.2 dynamic_slice.18
  4.2 0.8 copy.30
  5.2 5.8 %broadcast_in_dim.68 = f32[3584,2,128]{2,1,0:T(2,128)} broadcast(f32[3584,2]{1,0:T(8,128)S(1)} %bitcast.73), dimensions={0,1} | broadcast | bytes 3698688 | tf_op jit(solution)/shard_map/broadcast_in_dim | solution.py:59
  11.0 5.9 %reshape.224 = f32[1,3584,256]{2,1,0:T(8,128)} reshape(f32[3584,2,128]{2,1,0:T(2,128)} %broadcast_in_dim.68) | data formatting | bytes 7340032 | tf_op jit(solution)/shard_map/reshape | solution.py:59
  16.9 2.8 %reduce-precision_convert_fusion = (bf16[1,3584,256]{2,1,0:T(8,128)(2,1)S(1)}, bf16[1,3584,256]{2,1,0:T(8,128)(2,1)S(1)}) fusion(f32[1,3584,256]{2,1,0:T(8,128)} %reshape.224, bf16[1,3584,256]{2,1,0:T(8,128)(2,1)S(1)} %copy-done.1), kind=kLoop, calls=%fused_computation.10 | loop fusion | flops 5505024 | bytes 9175040 | tf_op jit(solution)/shard_map/convert_element_type | solution.py:62
  20.1 2.1 copy.25
  22.2 4.1 %fusion.3 = (bf16[1,1820,256]{2,1,0:T(8,128)(2,1)S(1)}, bf16[1820,256]{1,0:T(8,128)(2,1)}, bf16[1820,256]{1,0:T(8,128)(2,1)}, bf16[1820,256]{1,0:T(8,128)(2,1)}) fusion(s32[]{:T(128)S(6)} %select_n.115, bf16[4,1792,256]{2,1,0:T(8,128)(2,1)} %bitcast.70, bf16[4,28,256]{2,1,0:T(8,128)(2,1)S(1)} %reshape.222, s32[]{:T(128)S(6)} %select_n.117, ...), kind=kLoop, calls=%fused_computation.24 | loop fusion | flops 7454720 | bytes 7454736 | tf_op jit(solution)/shard_map/concatenate | solution.py:66
  26.3 3.9 %collective-permute-start = (bf16[1820,256]{1,0:T(8,128)(2,1)}, bf16[1820,256]{1,0:T(8,128)(2,1)}, u32[]{:S(2)}, u32[]{:S(2)}) collective-permute-start(bf16[1820,256]{1,0:T(8,128)(2,1)} %get-tuple-element.23), channel_id=1, source_target_pairs={{0,1},{1,2},{2,3},{3,0},{4,5},{5,6},{6,7},{7,4},{8,9},{9,10},{10,1... | collective-permute-start | bytes 2795528 | tf_op jit(solution)/shard_map/ppermute | solution.py:36
  30.3 4.4 %collective-permute-start.1 = (bf16[1820,256]{1,0:T(8,128)(2,1)}, bf16[1820,256]{1,0:T(8,128)(2,1)}, u32[]{:S(2)}, u32[]{:S(2)}) collective-permute-start(bf16[1820,256]{1,0:T(8,128)(2,1)} %get-tuple-element.24), channel_id=1, source_target_pairs={{0,2},{1,3},{2,0},{3,1},{4,6},{5,7},{6,4},{7,5},{8,10},{9,11},{10,... | collective-permute-start | bytes 2795528 | tf_op jit(solution)/shard_map/ppermute | solution.py:36
  34.6 3.1 %collective-permute-start.2 = (bf16[1820,256]{1,0:T(8,128)(2,1)}, bf16[1820,256]{1,0:T(8,128)(2,1)}, u32[]{:S(2)}, u32[]{:S(2)}) collective-permute-start(bf16[1820,256]{1,0:T(8,128)(2,1)} %get-tuple-element.25), channel_id=1, source_target_pairs={{0,3},{1,0},{2,1},{3,2},{4,7},{5,4},{6,5},{7,6},{8,11},{9,8},{10,9... | collective-permute-start | bytes 2795528 | tf_op jit(solution)/shard_map/ppermute | solution.py:36
  37.7 1.5 reshape_squeeze.3
  39.2 18.6 %all-to-all-start = ((bf16[128,28,256]{2,1,0:T(8,128)(2,1)}), bf16[128,28,256]{2,1,0:T(8,128)(2,1)S(1)}, u32[]{:S(2)}, u32[]{:S(2)}) async-start(bf16[128,28,256]{2,1,0:T(8,128)(2,1)} %reshape_squeeze.3), calls=%async_computation | async-start | bytes 4194304 | tf_op jit(solution)/shard_map/all_to_all | solution.py:56
  58.7 1.9 gather_fusion
  60.8 1.4 scatter_custom_fusion
  62.2 1.1 slice_bitcast_fusion
  63.4 0.7 slice_bitcast_fusion.4
  64.1 9.0 %collective-permute-done.1 = bf16[1820,256]{1,0:T(8,128)(2,1)} collective-permute-done((bf16[1820,256]{1,0:T(8,128)(2,1)}, bf16[1820,256]{1,0:T(8,128)(2,1)}, u32[]{:S(2)}, u32[]{:S(2)}) %collective-permute-start.1) | collective-permute-done | bytes 931872 | tf_op jit(solution)/shard_map/ppermute | solution.py:36
  73.1 0.7 slice_bitcast_fusion.3
  73.9 0.6 collective-permute-done.2
  74.5 0.7 slice_bitcast_fusion.2
  75.3 2.1 gather_fusion.1
  77.4 1.1 reshape.229
  78.5 1.4 fusion.25
  79.9 1.5 fusion.26
  81.4 1.4 fusion.27
  82.8 2.1 pad_maximum_fusion
  84.9 25.1 %all-to-all-done = bf16[128,28,256]{2,1,0:T(8,128)(2,1)S(1)} async-done(((bf16[128,28,256]{2,1,0:T(8,128)(2,1)}), bf16[128,28,256]{2,1,0:T(8,128)(2,1)S(1)}, u32[]{:S(2)}, u32[]{:S(2)}) %all-to-all-start) | async-done | bytes 1835040 | tf_op jit(solution)/shard_map/all_to_all | solution.py:56
  109.9 7.7 %all-to-all-start.1 = ((bf16[128,4,896]{2,1,0:T(4,128)(2,1)}), bf16[128,4,896]{2,1,0:T(4,128)(2,1)S(1)}, u32[]{:S(2)}, u32[]{:S(2)}) async-start(bf16[128,4,896]{2,1,0:T(4,128)(2,1)} %reshape.229), calls=%async_computation.1 | async-start | bytes 1835008 | tf_op jit(solution)/shard_map/all_to_all | solution.py:85
  117.7 2.0 gather_fusion.2
  119.7 3.2 %broadcast_select_fusion = bf16[128,28,256]{2,1,0:T(8,128)(2,1)} fusion(bf16[128,28,256]{2,1,0:T(8,128)(2,1)} %gather_fusion.2, pred[128]{0:T(512)(128)(4,1)S(1)} %compare_and_fusion), kind=kLoop, calls=%fused_computation.18 | loop fusion | flops 917504 | bytes 3670144 | tf_op jit(solution)/shard_map/jit(_take)/select_n | solution.py:87
  122.9 22.6 %all-to-all-done.1 = bf16[128,4,896]{2,1,0:T(4,128)(2,1)S(1)} async-done(((bf16[128,4,896]{2,1,0:T(4,128)(2,1)}), bf16[128,4,896]{2,1,0:T(4,128)(2,1)S(1)}, u32[]{:S(2)}, u32[]{:S(2)}) %all-to-all-start.1) | async-done | bytes 917536 | tf_op jit(solution)/shard_map/all_to_all | solution.py:85
  145.5 7.0 %all-to-all-start.2 = ((bf16[128,28,256]{2,1,0:T(8,128)(2,1)}), bf16[128,28,256]{2,1,0:T(8,128)(2,1)S(1)}, u32[]{:S(2)}, u32[]{:S(2)}) async-start(bf16[128,28,256]{2,1,0:T(8,128)(2,1)} %broadcast_select_fusion), calls=%async_computation.2 | async-start | bytes 4194304 | tf_op jit(solution)/shard_map/all_to_all | solution.py:88
  152.5 1.1 reshape.230
  153.6 3.2 %fusion.28 = f32[512,1024]{1,0:T(8,128)S(1)} fusion(bf16[512,896]{1,0:T(8,128)(2,1)} %reshape.230, bf16[896,1024]{1,0:T(8,128)(2,1)} %get-tuple-element.13), kind=kOutput, calls=%fused_computation.87 | convolution fusion | flops 939524096 | bytes 4849664 | tf_op jit(solution)/shard_map/dot_general | solution.py:91
  156.8 1.3 convolution_add_fusion
  158.2 1.9 collective-permute-start.3
  160.1 3.4 %collective-permute-start.5 = (f32[512,256]{1,0:T(8,128)S(1)}, f32[512,256]{1,0:T(8,128)S(1)}, u32[]{:S(2)}, u32[]{:S(2)}) collective-permute-start(f32[512,256]{1,0:T(8,128)S(1)} %get-tuple-element.27), channel_id=1, source_target_pairs={{0,1},{1,2},{2,3},{3,0},{4,5},{5,6},{6,7},{7,4},{8,9},{9,10},{10,1... | collective-permute-start | bytes 1572872 | tf_op jit(solution)/shard_map/ppermute | solution.py:97
  163.5 2.6 %collective-permute-start.4 = (f32[512,256]{1,0:T(8,128)S(1)}, f32[512,256]{1,0:T(8,128)S(1)}, u32[]{:S(2)}, u32[]{:S(2)}) collective-permute-start(f32[512,256]{1,0:T(8,128)S(1)} %get-tuple-element.28), channel_id=1, source_target_pairs={{0,2},{1,3},{2,0},{3,1},{4,6},{5,7},{6,4},{7,5},{8,10},{9,11},{10,... | collective-permute-start | bytes 1572872 | tf_op jit(solution)/shard_map/ppermute | solution.py:97
  166.0 6.5 %collective-permute-done.3 = f32[512,256]{1,0:T(8,128)S(1)} collective-permute-done((f32[512,256]{1,0:T(8,128)S(1)}, f32[512,256]{1,0:T(8,128)S(1)}, u32[]{:S(2)}, u32[]{:S(2)}) %collective-permute-start.3) | collective-permute-done | bytes 524320 | tf_op jit(solution)/shard_map/ppermute | solution.py:97
  172.6 3.7 %collective-permute-done.5 = f32[512,256]{1,0:T(8,128)S(1)} collective-permute-done((f32[512,256]{1,0:T(8,128)S(1)}, f32[512,256]{1,0:T(8,128)S(1)}, u32[]{:S(2)}, u32[]{:S(2)}) %collective-permute-start.5) | collective-permute-done | bytes 524320 | tf_op jit(solution)/shard_map/ppermute | solution.py:97
  176.3 10.1 %collective-permute-done.4 = f32[512,256]{1,0:T(8,128)S(1)} collective-permute-done((f32[512,256]{1,0:T(8,128)S(1)}, f32[512,256]{1,0:T(8,128)S(1)}, u32[]{:S(2)}, u32[]{:S(2)}) %collective-permute-start.4) | collective-permute-done | bytes 524320 | tf_op jit(solution)/shard_map/ppermute | solution.py:97
  186.6 0.8 reshape.231
  187.4 17.3 %all-to-all-done.2 = bf16[128,28,256]{2,1,0:T(8,128)(2,1)S(1)} async-done(((bf16[128,28,256]{2,1,0:T(8,128)(2,1)}), bf16[128,28,256]{2,1,0:T(8,128)(2,1)S(1)}, u32[]{:S(2)}, u32[]{:S(2)}) %all-to-all-start.2) | async-done | bytes 1835040 | tf_op jit(solution)/shard_map/all_to_all | solution.py:88
  204.7 1.4 reshape.232
  206.1 7.7 %all-to-all-start.3 = ((bf16[128,4,256]{2,1,0:T(4,128)(2,1)}), bf16[128,4,256]{2,1,0:T(4,128)(2,1)S(1)}, u32[]{:S(2)}, u32[]{:S(2)}) async-start(bf16[128,4,256]{2,1,0:T(4,128)(2,1)} %reshape.231), calls=%async_computation.3 | async-start | bytes 524288 | tf_op jit(solution)/shard_map/all_to_all | solution.py:101
  213.9 14.1 %all-to-all-done.3 = bf16[128,4,256]{2,1,0:T(4,128)(2,1)S(1)} async-done(((bf16[128,4,256]{2,1,0:T(4,128)(2,1)}), bf16[128,4,256]{2,1,0:T(4,128)(2,1)S(1)}, u32[]{:S(2)}, u32[]{:S(2)}) %all-to-all-start.3) | async-done | bytes 262176 | tf_op jit(solution)/shard_map/all_to_all | solution.py:101
  228.1 1.2 gather_fusion.3
  229.2 0.8 fusion.10
  (55 shorter events, 2.5 us)
Async XLA Ops:
  0.6 3.2 %copy-start = (f32[128,28,2]{0,2,1:T(2,128)S(1)}, f32[128,28,2]{0,2,1:T(2,128)}, u32[]{:S(2)}) copy-start(f32[128,28,2]{0,2,1:T(2,128)} %param.11) | copy-start | bytes 86020
  11.0 5.9 %copy-start.1 = (bf16[1,3584,256]{2,1,0:T(8,128)(2,1)S(1)}, bf16[1,3584,256]{2,1,0:T(8,128)(2,1)}, u32[]{:S(2)}) copy-start(bf16[1,3584,256]{2,1,0:T(8,128)(2,1)} %param.10) | copy-start | bytes 5505028
  26.3 37.0 %collective-permute-start = (bf16[1820,256]{1,0:T(8,128)(2,1)}, bf16[1820,256]{1,0:T(8,128)(2,1)}, u32[]{:S(2)}, u32[]{:S(2)}) collective-permute-start(bf16[1820,256]{1,0:T(8,128)(2,1)} %get-tuple-element.23), channel_id=1, source_target_pairs={{0,1},{1,2},{2,3},{3,0},{4,5},{5,6},{6,7},{7,4},{8,9},{9,10},{10,1... | collective-permute-start | bytes 2795528 | tf_op jit(solution)/shard_map/ppermute | solution.py:36
  30.3 42.9 %collective-permute-start.1 = (bf16[1820,256]{1,0:T(8,128)(2,1)}, bf16[1820,256]{1,0:T(8,128)(2,1)}, u32[]{:S(2)}, u32[]{:S(2)}) collective-permute-start(bf16[1820,256]{1,0:T(8,128)(2,1)} %get-tuple-element.24), channel_id=1, source_target_pairs={{0,2},{1,3},{2,0},{3,1},{4,6},{5,7},{6,4},{7,5},{8,10},{9,11},{10,... | collective-permute-start | bytes 2795528 | tf_op jit(solution)/shard_map/ppermute | solution.py:36
  34.6 39.9 %collective-permute-start.2 = (bf16[1820,256]{1,0:T(8,128)(2,1)}, bf16[1820,256]{1,0:T(8,128)(2,1)}, u32[]{:S(2)}, u32[]{:S(2)}) collective-permute-start(bf16[1820,256]{1,0:T(8,128)(2,1)} %get-tuple-element.25), channel_id=1, source_target_pairs={{0,3},{1,0},{2,1},{3,2},{4,7},{5,4},{6,5},{7,6},{8,11},{9,8},{10,9... | collective-permute-start | bytes 2795528 | tf_op jit(solution)/shard_map/ppermute | solution.py:36
  39.2 18.6 %copy-start.6 = (s32[2,16,8]{1,2,0:T(8,128)S(1)}, s32[2,16,8]{1,2,0:T(8,128)}, u32[]{:S(2)}) copy-start(s32[2,16,8]{1,2,0:T(8,128)} %param.8) | copy-start | bytes 3076
  39.2 19.3 %copy-start.8 = (s32[128]{0:T(128)S(1)}, s32[128]{0:T(128)}, u32[]{:S(2)}) copy-start(s32[128]{0:T(128)} %param.12) | copy-start | bytes 1540
  39.2 19.3 %copy-start.9 = (s32[128]{0:T(128)S(1)}, s32[128]{0:T(128)}, u32[]{:S(2)}) copy-start(s32[128]{0:T(128)} %param.13) | copy-start | bytes 1540
  39.2 70.7 %all-to-all-start = ((bf16[128,28,256]{2,1,0:T(8,128)(2,1)}), bf16[128,28,256]{2,1,0:T(8,128)(2,1)S(1)}, u32[]{:S(2)}, u32[]{:S(2)}) async-start(bf16[128,28,256]{2,1,0:T(8,128)(2,1)} %reshape_squeeze.3), calls=%async_computation | async-start | bytes 4194304 | tf_op jit(solution)/shard_map/all_to_all | solution.py:56
  79.9 2.9 %copy-start.2 = (bf16[896,256]{1,0:T(8,128)(2,1)S(1)}, bf16[896,256]{1,0:T(8,128)(2,1)}, u32[]{:S(2)}) copy-start(bf16[896,256]{1,0:T(8,128)(2,1)} %get-tuple-element.29) | copy-start | bytes 1376260
  79.9 2.9 %copy-start.3 = (bf16[896,256]{1,0:T(8,128)(2,1)S(1)}, bf16[896,256]{1,0:T(8,128)(2,1)}, u32[]{:S(2)}) copy-start(bf16[896,256]{1,0:T(8,128)(2,1)} %get-tuple-element.30) | copy-start | bytes 1376260
  109.9 35.6 %all-to-all-start.1 = ((bf16[128,4,896]{2,1,0:T(4,128)(2,1)}), bf16[128,4,896]{2,1,0:T(4,128)(2,1)S(1)}, u32[]{:S(2)}, u32[]{:S(2)}) async-start(bf16[128,4,896]{2,1,0:T(4,128)(2,1)} %reshape.229), calls=%async_computation.1 | async-start | bytes 1835008 | tf_op jit(solution)/shard_map/all_to_all | solution.py:85
  145.5 59.2 %all-to-all-start.2 = ((bf16[128,28,256]{2,1,0:T(8,128)(2,1)}), bf16[128,28,256]{2,1,0:T(8,128)(2,1)S(1)}, u32[]{:S(2)}, u32[]{:S(2)}) async-start(bf16[128,28,256]{2,1,0:T(8,128)(2,1)} %broadcast_select_fusion), calls=%async_computation.2 | async-start | bytes 4194304 | tf_op jit(solution)/shard_map/all_to_all | solution.py:88
  153.6 3.2 %copy-start.4 = (bf16[896,1024]{1,0:T(8,128)(2,1)S(1)}, bf16[896,1024]{1,0:T(8,128)(2,1)}, u32[]{:S(2)}) copy-start(bf16[896,1024]{1,0:T(8,128)(2,1)} %get-tuple-element.14) | copy-start | bytes 5505028
  153.6 3.2 %copy-start.5 = (bf16[512,896]{1,0:T(8,128)(2,1)S(1)}, bf16[512,896]{1,0:T(8,128)(2,1)}, u32[]{:S(2)}) copy-start(bf16[512,896]{1,0:T(8,128)(2,1)} %reshape.230) | copy-start | bytes 2752516
  158.2 14.4 %collective-permute-start.3 = (f32[512,256]{1,0:T(8,128)S(1)}, f32[512,256]{1,0:T(8,128)S(1)}, u32[]{:S(2)}, u32[]{:S(2)}) collective-permute-start(f32[512,256]{1,0:T(8,128)S(1)} %get-tuple-element.26), channel_id=1, source_target_pairs={{0,3},{1,0},{2,1},{3,2},{4,7},{5,4},{6,5},{7,6},{8,11},{9,8},{10,9... | collective-permute-start | bytes 1572872 | tf_op jit(solution)/shard_map/ppermute | solution.py:97
  160.1 16.1 %collective-permute-start.5 = (f32[512,256]{1,0:T(8,128)S(1)}, f32[512,256]{1,0:T(8,128)S(1)}, u32[]{:S(2)}, u32[]{:S(2)}) collective-permute-start(f32[512,256]{1,0:T(8,128)S(1)} %get-tuple-element.27), channel_id=1, source_target_pairs={{0,1},{1,2},{2,3},{3,0},{4,5},{5,6},{6,7},{7,4},{8,9},{9,10},{10,1... | collective-permute-start | bytes 1572872 | tf_op jit(solution)/shard_map/ppermute | solution.py:97
  163.5 22.9 %collective-permute-start.4 = (f32[512,256]{1,0:T(8,128)S(1)}, f32[512,256]{1,0:T(8,128)S(1)}, u32[]{:S(2)}, u32[]{:S(2)}) collective-permute-start(f32[512,256]{1,0:T(8,128)S(1)} %get-tuple-element.28), channel_id=1, source_target_pairs={{0,2},{1,3},{2,0},{3,1},{4,6},{5,7},{6,4},{7,5},{8,10},{9,11},{10,... | collective-permute-start | bytes 1572872 | tf_op jit(solution)/shard_map/ppermute | solution.py:97
  187.4 26.4 %copy-start.7 = (f32[2,16,8]{1,2,0:T(8,128)S(1)}, f32[2,16,8]{1,2,0:T(8,128)}, u32[]{:S(2)}) copy-start(f32[2,16,8]{1,2,0:T(8,128)} %param.9) | copy-start | bytes 3076
  206.1 21.9 %all-to-all-start.3 = ((bf16[128,4,256]{2,1,0:T(4,128)(2,1)}), bf16[128,4,256]{2,1,0:T(4,128)(2,1)S(1)}, u32[]{:S(2)}, u32[]{:S(2)}) async-start(bf16[128,4,256]{2,1,0:T(4,128)(2,1)} %reshape.231), calls=%async_computation.3 | async-start | bytes 524288 | tf_op jit(solution)/shard_map/all_to_all | solution.py:101

commit v5 on v3

--- a/solution.py
+++ b/solution.py
@@ -37,7 +37,7 @@
     return got
 
 
-def shards(tokens, routing, gate_values, held_weight, scale_table, old_expert, new_expert):
+def layer(tokens, routing, gate_values, held_weight, scale_table, old_expert, new_expert):
     peers = lax.axis_size("ep")
     n_dp = lax.axis_size("dp")
     my_slot = lax.axis_index("ep")
@@ -55,22 +55,16 @@
     pieces = old_block.reshape(peers, rows // peers, cols)
     staged = lax.all_to_all(pieces, "ep", split_axis=0, concat_axis=0, tiled=True)
 
-    w_parts = dp_shifts(old_block.reshape(n_dp, row_part, cols), n_dp, my_dp)
     own_scales = scale_table[old_expert[my_slot]]
-    row_blocks = row_part // blk
-    s_parts = dp_shifts(own_scales.reshape(n_dp, row_blocks, own_scales.shape[1]), n_dp, my_dp)
-    w_rows = jnp.concatenate(w_parts, axis=1)
-    my_scales = jnp.concatenate(s_parts, axis=1)
-    widened = jnp.repeat(jnp.repeat(my_scales, blk, axis=0), blk, axis=1)
-    w32 = w_rows.astype(jnp.float32) * widened
+    col_scales = jnp.repeat(own_scales, blk, axis=1)
+    w32 = old_block.reshape(-1, blk, cols).astype(jnp.float32) * col_scales[:, None, :]
     hi32 = lax.reduce_precision(w32, exponent_bits=8, mantissa_bits=7)
-    w_hi = hi32.astype(jnp.bfloat16)
-    w_lo = (w32 - hi32).astype(jnp.bfloat16)
-
-    t_parts = dp_shifts(
+    w_hi = hi32.astype(jnp.bfloat16).reshape(rows, cols)
+    w_lo = (w32 - hi32).astype(jnp.bfloat16).reshape(rows, cols)
+    got = dp_shifts(
         jnp.transpose(tokens.reshape(steps, local_tokens, n_dp, row_part), (2, 0, 1, 3)), n_dp, my_dp
     )
-    feats = jnp.stack(t_parts).reshape(n_dp * steps * local_tokens, row_part)
+    feats = jnp.stack(got).reshape(n_dp * steps * local_tokens, row_part)
 
     target = route_targets(routing, owners, peers, capacity)
     token_of = jnp.broadcast_to(
@@ -81,20 +75,17 @@
     row_of = (part_of * steps + step_of) * local_tokens + token_of % local_tokens
     pick = jnp.zeros((peers * steps * capacity,), jnp.int32).at[target.reshape(-1)].set(row_of.reshape(-1))
     send_tokens = feats[pick].reshape(peers, steps * capacity, row_part)
-    staged, send_tokens = lax.optimization_barrier((staged, send_tokens))
+    staged, send_tokens, w_hi, w_lo = lax.optimization_barrier((staged, send_tokens, w_hi, w_lo))
     arrived = lax.all_to_all(send_tokens, "ep", split_axis=0, concat_axis=0, tiled=True)
 
     regrouped, arrived = lax.optimization_barrier((jnp.take(staged, sources, axis=0), arrived))
     new_block = lax.all_to_all(regrouped, "ep", split_axis=0, concat_axis=0, tiled=True).reshape(rows, cols)
 
     arrived = arrived.reshape(peers * steps * capacity, row_part)
-    partial = jnp.dot(arrived, w_hi, preferred_element_type=jnp.float32) + jnp.dot(
-        arrived, w_lo, preferred_element_type=jnp.float32
+    full = lax.all_gather(arrived, "dp", axis=1, tiled=True)
+    hidden = jnp.dot(full, w_hi, preferred_element_type=jnp.float32) + jnp.dot(
+        full, w_lo, preferred_element_type=jnp.float32
     )
-    hidden = partial[:, :cols]
-    for shift in range(1, n_dp):
-        pairs = [(k, (k - shift) % n_dp) for k in range(n_dp)]
-        hidden = hidden + lax.ppermute(partial[:, shift * cols:(shift + 1) * cols], "dp", pairs)
     act = jax.nn.silu(hidden).astype(jnp.bfloat16)
     act = act.reshape(peers, steps * capacity, cols)
     act, new_block = lax.optimization_barrier((act, new_block))
@@ -116,7 +107,7 @@
         P(),
     )
     return jax.shard_map(
-        shards,
+        layer,
         mesh=mesh,
         in_specs=placed,
         out_specs=(P(None, "ep", "dp"), P("ep", None, "dp")),

time: 230 us -> 219 us (0.952)
  blocking collectives: 0 us -> 59.2 us
  starting transfers between devices: 90.6 us -> 44.5 us
  waiting for transfers between devices: 91.5 us -> 64.6 us
  between operations: 3.11 us -> 16.4 us
  local copies, waits for them, and re-layouts: 28.1 us -> 21.1 us
  other arithmetic: 10.6 us -> 7.38 us
    all_to_all x0 -> x1, blocking collectives: none -> 59.2 us  [layer(): lax.all_to_all(regrouped, 'ep', split_axis=0, concat_axis=0, tiled=True)]
    ppermute x9 -> x3, starting transfers between devices: 31.6 us -> 10.5 us  [dp_shifts(): got.append(lax.ppermute(parts[(my_dp + shift) % n_dp], 'dp', pairs))]
    ppermute x3 -> x0, waiting for transfers between devices: 18.2 us -> none  [shards(): lax.ppermute(partial[:, shift * cols:(shift + 1) * cols], 'dp', pairs)]
    all_to_all x4 -> x3, starting transfers between devices: 48.6 us -> 34 us  [the longest x1 18.6 us: layer(): lax.all_to_all(pieces, 'ep', split_axis=0, concat_axis=0, tiled=True)]
    ppermute x3 -> x0, starting transfers between devices: 10.3 us -> none  [shards(): lax.ppermute(partial[:, shift * cols:(shift + 1) * cols], 'dp', pairs)]
    concatenate x5 -> x0, local copies, waits for them, and re-layouts: 6.89 us -> none  [the longest x4 6.81 us: shards(): w_rows = jnp.concatenate(w_parts, axis=1)]
    all_to_all x4 -> x3, waiting for transfers between devices: 70.2 us -> 64.6 us  [the longest x1 26.6 us: layer(): lax.all_to_all(pieces, 'ep', split_axis=0, concat_axis=0, tiled=True)]
    ppermute x9 -> x3, waiting for transfers between devices: 3.08 us -> 0.01 us  [dp_shifts(): got.append(lax.ppermute(parts[(my_dp + shift) % n_dp], 'dp', pairs))]
  transfers between devices with their start and end apart: 16 -> 7, of which waited for: 7 -> 3; matrix products, arithmetic and copies ran while one was open for 16% -> 9% of each run, Pallas kernels for 0% -> 0%
where the time goes in v5:
time: 219 us; the launch traced here: 218 us
  waiting for transfers between devices  64.6 us (29%)
  blocking collectives  59.2 us (27%)
  starting transfers between devices  44.5 us (20%)
  local copies, waits for them, and re-layouts  21.1 us (10%)
  between operations  16.4 us (7%)
  other arithmetic  7.38 us (3%)
  matrix products  4.99 us (2%)
    all_to_all x1, blocking collectives, layer(): lax.all_to_all(regrouped, 'ep', split_axis=0, concat_axis=0, tiled=True)  59.2 us
    all_to_all x1, waiting for transfers between devices, layer(): lax.all_to_all(pieces, 'ep', split_axis=0, concat_axis=0, tiled=True)  26.6 us
    all_to_all x1, waiting for transfers between devices, layer(): lax.all_to_all(send_tokens, 'ep', split_axis=0, concat_axis=0, tiled=True)  23.8 us
    all_to_all x1, starting transfers between devices, layer(): lax.all_to_all(pieces, 'ep', split_axis=0, concat_axis=0, tiled=True)  18.6 us
    all_to_all x1, waiting for transfers between devices, layer(): lax.all_to_all(act, 'ep', split_axis=0, concat_axis=0, tiled=True)  14.1 us
    ppermute x3, starting transfers between devices, dp_shifts(): got.append(lax.ppermute(parts[(my_dp + shift) % n_dp], 'dp', pairs))  10.5 us
    all_to_all x1, starting transfers between devices, layer(): lax.all_to_all(send_tokens, 'ep', split_axis=0, concat_axis=0, tiled=True)  7.72 us
    all_to_all x1, starting transfers between devices, layer(): lax.all_to_all(act, 'ep', split_axis=0, concat_axis=0, tiled=True)  7.69 us
  transfers between devices with their start and end apart: 7, of which 3 were waited for; matrix products, arithmetic and copies ran while one was open for 9% of the time, Pallas kernels for 0%

profile of v5, /device:TPU:1, one launch (start us, length us, event | category | flops | bytes accessed | tf_op | source)
XLA Modules:
  0.0 218.2 jit_solution(6434524917890989390)
XLA Ops:
  7.2 0.0 copy-start
  7.2 3.8 %reshape_squeeze.4 = bf16[128,28,256]{2,1,0:T(8,128)(2,1)} reshape(bf16[1,3584,256]{2,1,0:T(8,128)(2,1)} %param.10) | data formatting | bytes 3670016 | tf_op jit(solution)/shard_map/reshape;squeeze | solution.py:55
  10.9 18.6 %all-to-all-start = ((bf16[128,28,256]{2,1,0:T(8,128)(2,1)}), bf16[128,28,256]{2,1,0:T(8,128)(2,1)S(1)}, u32[]{:S(2)}, u32[]{:S(2)}) async-start(bf16[128,28,256]{2,1,0:T(8,128)(2,1)} %reshape_squeeze.4), calls=%async_computation | async-start | bytes 4194304 | tf_op jit(solution)/shard_map/all_to_all | solution.py:56
  29.6 0.1 constant_dynamic-slice_fusion.3
  29.8 3.1 %collective-permute-start = (bf16[2,4,896]{2,1,0:T(4,128)(2,1)S(1)}, bf16[2,4,896]{2,1,0:T(4,128)(2,1)S(1)}, u32[]{:S(2)}, u32[]{:S(2)}) collective-permute-start(bf16[2,4,896]{2,1,0:T(4,128)(2,1)S(1)} %bitcast.75), channel_id=1, source_target_pairs={{0,1},{1,2},{2,3},{3,0},{4,5},{5,6},{6,7},{7,4},{8,9},{9,10},{10,1... | collective-permute-start | bytes 43016 | tf_op jit(solution)/shard_map/ppermute | solution.py:36
  32.9 4.4 %collective-permute-start.1 = (bf16[2,4,896]{2,1,0:T(4,128)(2,1)S(1)}, bf16[2,4,896]{2,1,0:T(4,128)(2,1)S(1)}, u32[]{:S(2)}, u32[]{:S(2)}) collective-permute-start(bf16[2,4,896]{2,1,0:T(4,128)(2,1)S(1)} %bitcast.76), channel_id=1, source_target_pairs={{0,2},{1,3},{2,0},{3,1},{4,6},{5,7},{6,4},{7,5},{8,10},{9,11},{10,... | collective-permute-start | bytes 43016 | tf_op jit(solution)/shard_map/ppermute | solution.py:36
  37.3 3.1 %collective-permute-start.2 = (bf16[2,4,896]{2,1,0:T(4,128)(2,1)S(1)}, bf16[2,4,896]{2,1,0:T(4,128)(2,1)S(1)}, u32[]{:S(2)}, u32[]{:S(2)}) collective-permute-start(bf16[2,4,896]{2,1,0:T(4,128)(2,1)S(1)} %bitcast.77), channel_id=1, source_target_pairs={{0,3},{1,0},{2,1},{3,2},{4,7},{5,4},{6,5},{7,6},{8,11},{9,8},{10,9... | collective-permute-start | bytes 43016 | tf_op jit(solution)/shard_map/ppermute | solution.py:36
  40.4 0.1 copy.26
  40.4 0.1 eq.51
  40.5 0.1 reshape.198
  40.6 0.6 dynamic_slice.13
  42.5 0.1 fusion.2
  42.6 0.2 reduce_window_sum.11
  42.8 0.1 reshape.199
  43.0 0.2 select_reduce_fusion.2
  43.1 1.9 gather_fusion
  45.0 0.2 select_reduce_fusion
  45.2 1.4 scatter_custom_fusion
  47.3 0.1 constant_dynamic-slice_fusion.4
  47.4 0.1 copy.28
  47.5 0.1 copy.29
  47.6 0.1 broadcast_in_dim.67
  47.8 4.0 %fusion = (bf16[3584,256]{1,0:T(8,128)(2,1)}, bf16[3584,256]{1,0:T(8,128)(2,1)}) fusion(bf16[1,3584,256]{2,1,0:T(8,128)(2,1)} %param.10, f32[28,256]{1,0:T(8,128)S(1)} %bitcast.69), kind=kLoop, calls=%fused_computation.7 | loop fusion | flops 5505024 | bytes 5533696 | tf_op jit(solution)/shard_map/convert_element_type | solution.py:63
  51.7 0.0 collective-permute-done
  51.8 0.0 collective-permute-done.1
  51.8 0.1 pad_maximum_fusion
  51.9 2.1 gather_fusion.1
  53.9 1.1 reshape.200
  55.0 26.6 %all-to-all-done = bf16[128,28,256]{2,1,0:T(8,128)(2,1)S(1)} async-done(((bf16[128,28,256]{2,1,0:T(8,128)(2,1)}), bf16[128,28,256]{2,1,0:T(8,128)(2,1)S(1)}, u32[]{:S(2)}, u32[]{:S(2)}) %all-to-all-start) | async-done | bytes 1835040 | tf_op jit(solution)/shard_map/all_to_all | solution.py:56
  81.6 7.7 %all-to-all-start.1 = ((bf16[128,4,896]{2,1,0:T(4,128)(2,1)}), bf16[128,4,896]{2,1,0:T(4,128)(2,1)S(1)}, u32[]{:S(2)}, u32[]{:S(2)}) async-start(bf16[128,4,896]{2,1,0:T(4,128)(2,1)} %reshape.200), calls=%async_computation.1 | async-start | bytes 1835008 | tf_op jit(solution)/shard_map/all_to_all | solution.py:79
  89.4 0.0 all-gather.2.cloned.1.call-start
  89.5 2.0 gather_fusion.2
  91.5 1.9 broadcast_select_fusion
  93.4 23.8 %all-to-all-done.1 = bf16[128,4,896]{2,1,0:T(4,128)(2,1)S(1)} async-done(((bf16[128,4,896]{2,1,0:T(4,128)(2,1)}), bf16[128,4,896]{2,1,0:T(4,128)(2,1)S(1)}, u32[]{:S(2)}, u32[]{:S(2)}) %all-to-all-start.1) | async-done | bytes 917536 | tf_op jit(solution)/shard_map/all_to_all | solution.py:79
  117.2 1.1 reshape.201
  118.3 0.0 all-gather.2.cloned.1.call-update
  118.4 59.2 %all_to_all.20 = bf16[128,28,256]{2,1,0:T(8,128)(2,1)} all-to-all(bf16[128,28,256]{2,1,0:T(8,128)(2,1)S(1)} %broadcast_select_fusion), channel_id=1, replica_groups=mesh['ep'=128,'dp'=4] {'ep'}, dimensions={0} | all-to-all | bytes 3670016 | tf_op jit(solution)/shard_map/all_to_all | solution.py:82
  177.6 3.7 %reshape.203 = bf16[3584,256]{1,0:T(8,128)(2,1)} reshape(bf16[128,28,256]{2,1,0:T(8,128)(2,1)} %all_to_all.20) | data formatting | bytes 3670016 | tf_op jit(solution)/shard_map/reshape | solution.py:82
  181.3 3.9 %fusion.15 = f32[512,256]{1,0:T(8,128)S(1)} fusion(bf16[512,3584]{1,0:T(8,128)(2,1)} %all-gather.2.cloned.1.call-done, bf16[3584,256]{1,0:T(8,128)(2,1)} %get-tuple-element.13), kind=kOutput, calls=%fused_computation.64 | convolution fusion | flops 939524096 | bytes 6029312 | tf_op jit(solution)/shard_map/dot_general | solution.py:86
  185.2 0.4 copy-done.7
  185.6 1.1 multiply_convert_fusion
  186.7 0.8 reshape.202
  187.5 7.7 %all-to-all-start.3 = ((bf16[128,4,256]{2,1,0:T(4,128)(2,1)}), bf16[128,4,256]{2,1,0:T(4,128)(2,1)S(1)}, u32[]{:S(2)}, u32[]{:S(2)}) async-start(bf16[128,4,256]{2,1,0:T(4,128)(2,1)} %reshape.202), calls=%async_computation.3 | async-start | bytes 524288 | tf_op jit(solution)/shard_map/all_to_all | solution.py:92
  195.2 0.1 copy.21
  195.3 14.1 %all-to-all-done.3 = bf16[128,4,256]{2,1,0:T(4,128)(2,1)S(1)} async-done(((bf16[128,4,256]{2,1,0:T(4,128)(2,1)}), bf16[128,4,256]{2,1,0:T(4,128)(2,1)S(1)}, u32[]{:S(2)}, u32[]{:S(2)}) %all-to-all-start.3) | async-done | bytes 262176 | tf_op jit(solution)/shard_map/all_to_all | solution.py:92
  209.4 0.1 reshape.204
  209.5 1.2 gather_fusion.3
  210.6 0.8 fusion.1
  (37 shorter events, 0.2 us)
Async XLA Ops:
  7.2 40.1 %copy-start = (f32[128,28,2]{0,2,1:T(2,128)S(1)}, f32[128,28,2]{0,2,1:T(2,128)}, u32[]{:S(2)}) copy-start(f32[128,28,2]{0,2,1:T(2,128)} %param.11) | copy-start | bytes 86020
  10.9 18.6 %copy-start.2 = (bf16[2,4,3584]{2,1,0:T(4,128)(2,1)S(1)}, bf16[2,4,3584]{2,1,0:T(4,128)(2,1)}, u32[]{:S(2)}) copy-start(bf16[2,4,3584]{2,1,0:T(4,128)(2,1)} %param.7) | copy-start | bytes 172036
  10.9 29.4 %copy-start.3 = (s32[2,16,8]{1,2,0:T(8,128)S(1)}, s32[2,16,8]{1,2,0:T(8,128)}, u32[]{:S(2)}) copy-start(s32[2,16,8]{1,2,0:T(8,128)} %param.8) | copy-start | bytes 3076
  10.9 29.7 %copy-start.5 = (s32[128]{0:T(128)S(1)}, s32[128]{0:T(128)}, u32[]{:S(2)}) copy-start(s32[128]{0:T(128)} %param.12) | copy-start | bytes 1540
  10.9 32.0 %copy-start.6 = (s32[128]{0:T(128)S(1)}, s32[128]{0:T(128)}, u32[]{:S(2)}) copy-start(s32[128]{0:T(128)} %param.13) | copy-start | bytes 1540
  10.9 70.7 %all-to-all-start = ((bf16[128,28,256]{2,1,0:T(8,128)(2,1)}), bf16[128,28,256]{2,1,0:T(8,128)(2,1)S(1)}, u32[]{:S(2)}, u32[]{:S(2)}) async-start(bf16[128,28,256]{2,1,0:T(8,128)(2,1)} %reshape_squeeze.4), calls=%async_computation | async-start | bytes 4194304 | tf_op jit(solution)/shard_map/all_to_all | solution.py:56
  29.8 22.0 %collective-permute-start = (bf16[2,4,896]{2,1,0:T(4,128)(2,1)S(1)}, bf16[2,4,896]{2,1,0:T(4,128)(2,1)S(1)}, u32[]{:S(2)}, u32[]{:S(2)}) collective-permute-start(bf16[2,4,896]{2,1,0:T(4,128)(2,1)S(1)} %bitcast.75), channel_id=1, source_target_pairs={{0,1},{1,2},{2,3},{3,0},{4,5},{5,6},{6,7},{7,4},{8,9},{9,10},{10,1... | collective-permute-start | bytes 43016 | tf_op jit(solution)/shard_map/ppermute | solution.py:36
  32.9 18.8 %collective-permute-start.1 = (bf16[2,4,896]{2,1,0:T(4,128)(2,1)S(1)}, bf16[2,4,896]{2,1,0:T(4,128)(2,1)S(1)}, u32[]{:S(2)}, u32[]{:S(2)}) collective-permute-start(bf16[2,4,896]{2,1,0:T(4,128)(2,1)S(1)} %bitcast.76), channel_id=1, source_target_pairs={{0,2},{1,3},{2,0},{3,1},{4,6},{5,7},{6,4},{7,5},{8,10},{9,11},{10,... | collective-permute-start | bytes 43016 | tf_op jit(solution)/shard_map/ppermute | solution.py:36
  37.3 14.5 %collective-permute-start.2 = (bf16[2,4,896]{2,1,0:T(4,128)(2,1)S(1)}, bf16[2,4,896]{2,1,0:T(4,128)(2,1)S(1)}, u32[]{:S(2)}, u32[]{:S(2)}) collective-permute-start(bf16[2,4,896]{2,1,0:T(4,128)(2,1)S(1)} %bitcast.77), channel_id=1, source_target_pairs={{0,3},{1,0},{2,1},{3,2},{4,7},{5,4},{6,5},{7,6},{8,11},{9,8},{10,9... | collective-permute-start | bytes 43016 | tf_op jit(solution)/shard_map/ppermute | solution.py:36
  81.6 35.6 %all-to-all-start.1 = ((bf16[128,4,896]{2,1,0:T(4,128)(2,1)}), bf16[128,4,896]{2,1,0:T(4,128)(2,1)S(1)}, u32[]{:S(2)}, u32[]{:S(2)}) async-start(bf16[128,4,896]{2,1,0:T(4,128)(2,1)} %reshape.200), calls=%async_computation.1 | async-start | bytes 1835008 | tf_op jit(solution)/shard_map/all_to_all | solution.py:79
  89.4 92.0 %all-gather.2.cloned.1.call-start = ((), (), s32[]{:S(2)}) async-start(), calls=%async_computation.4 | async-start | bytes 4587520 | tf_op jit(solution)/shard_map/all_gather | solution.py:85
  181.3 3.9 %copy-start.1 = (bf16[3584,256]{1,0:T(8,128)(2,1)S(1)}, bf16[3584,256]{1,0:T(8,128)(2,1)}, u32[]{:S(2)}) copy-start(bf16[3584,256]{1,0:T(8,128)(2,1)} %get-tuple-element.14) | copy-start | bytes 5505028
  181.3 4.2 %copy-start.7 = (bf16[512,3584]{1,0:T(8,128)(2,1)S(1)}, bf16[512,3584]{1,0:T(8,128)(2,1)}, u32[]{:S(2)}) copy-start(bf16[512,3584]{1,0:T(8,128)(2,1)} %all-gather.2.cloned.1.call-done) | copy-start | bytes 11010052
  185.6 9.6 %copy-start.4 = (f32[2,16,8]{1,2,0:T(8,128)S(1)}, f32[2,16,8]{1,2,0:T(8,128)}, u32[]{:S(2)}) copy-start(f32[2,16,8]{1,2,0:T(8,128)} %param.9) | copy-start | bytes 3076
  187.5 21.9 %all-to-all-start.3 = ((bf16[128,4,256]{2,1,0:T(4,128)(2,1)}), bf16[128,4,256]{2,1,0:T(4,128)(2,1)S(1)}, u32[]{:S(2)}, u32[]{:S(2)}) async-start(bf16[128,4,256]{2,1,0:T(4,128)(2,1)} %reshape.202), calls=%async_computation.3 | async-start | bytes 524288 | tf_op jit(solution)/shard_map/all_to_all | solution.py:92
Sparse Core Ops, SparseCore 0:
  118.5 42.6 all-gather.1

commit v6 on v5

--- a/solution.py
+++ b/solution.py
@@ -52,8 +52,9 @@
     owners = inverse_place(old_expert)
     sources = source_slots(old_expert, new_expert)
 
-    pieces = old_block.reshape(peers, rows // peers, cols)
-    staged = lax.all_to_all(pieces, "ep", split_axis=0, concat_axis=0, tiled=True)
+    everyone = peers * n_dp
+    pieces = old_block.reshape(everyone, rows // everyone, cols)
+    staged = lax.all_to_all(pieces, ("ep", "dp"), split_axis=0, concat_axis=0, tiled=True)
 
     own_scales = scale_table[old_expert[my_slot]]
     col_scales = jnp.repeat(own_scales, blk, axis=1)
@@ -78,8 +79,10 @@
     staged, send_tokens, w_hi, w_lo = lax.optimization_barrier((staged, send_tokens, w_hi, w_lo))
     arrived = lax.all_to_all(send_tokens, "ep", split_axis=0, concat_axis=0, tiled=True)
 
-    regrouped, arrived = lax.optimization_barrier((jnp.take(staged, sources, axis=0), arrived))
-    new_block = lax.all_to_all(regrouped, "ep", split_axis=0, concat_axis=0, tiled=True).reshape(rows, cols)
+    holder = jnp.arange(everyone, dtype=jnp.int32)
+    from_block = sources[holder // n_dp] * n_dp + holder % n_dp
+    regrouped, arrived = lax.optimization_barrier((jnp.take(staged, from_block, axis=0), arrived))
+    new_block = lax.all_to_all(regrouped, ("ep", "dp"), split_axis=0, concat_axis=0, tiled=True).reshape(rows, cols)
 
     arrived = arrived.reshape(peers * steps * capacity, row_part)
     full = lax.all_gather(arrived, "dp", axis=1, tiled=True)

time: 219 us -> 232 us (1.059)
  blocking collectives: 59.2 us -> 65.3 us
  starting transfers between devices: 44.5 us -> 49.9 us
  local copies, waits for them, and re-layouts: 21.1 us -> 25.4 us
  waiting for transfers between devices: 64.6 us -> 61.2 us
    all_to_all x1, blocking collectives: 59.2 us -> 65.3 us  [layer(): lax.all_to_all(regrouped, ('ep', 'dp'), split_axis=0, concat_axis=0, tile...]
    all_to_all x1, waiting for transfers between devices: 23.8 us -> 18.7 us  [layer(): lax.all_to_all(send_tokens, 'ep', split_axis=0, concat_axis=0, tiled=True)]
    gather x1 -> x2, local copies, waits for them, and re-layouts: 2.03 us -> 6.11 us  [the longest x1 3.35 us: layer(): from_block = sources[holder // n_dp] * n_dp + holder % n_dp]
    all_to_all x1, starting transfers between devices: 18.6 us -> 22.2 us  [layer(): lax.all_to_all(pieces, ('ep', 'dp'), split_axis=0, concat_axis=0, tiled=T...]
  transfers between devices with their start and end apart: 7 -> 7, of which waited for: 3 -> 3; matrix products, arithmetic and copies ran while one was open for 9% -> 11% of each run, Pallas kernels for 0% -> 0%
where the time goes in v6:
time: 232 us
  blocking collectives  65.3 us (28%)
  waiting for transfers between devices  61.2 us (26%)
  starting transfers between devices  49.9 us (22%)
  local copies, waits for them, and re-layouts  25.4 us (11%)
  between operations  16.4 us (7%)
  other arithmetic  8.43 us (4%)
  matrix products  4.99 us (2%)
    all_to_all x1, blocking collectives, layer(): lax.all_to_all(regrouped, ('ep', 'dp'), split_axis=0, concat_axis=0, tile...  65.3 us
    all_to_all x1, waiting for transfers between devices, layer(): lax.all_to_all(pieces, ('ep', 'dp'), split_axis=0, concat_axis=0, tiled=T...  28.3 us
    all_to_all x1, starting transfers between devices, layer(): lax.all_to_all(pieces, ('ep', 'dp'), split_axis=0, concat_axis=0, tiled=T...  22.2 us
    all_to_all x1, waiting for transfers between devices, layer(): lax.all_to_all(send_tokens, 'ep', split_axis=0, concat_axis=0, tiled=True)  18.7 us
    all_to_all x1, waiting for transfers between devices, layer(): lax.all_to_all(act, 'ep', split_axis=0, concat_axis=0, tiled=True)  14.1 us
    ppermute x3, starting transfers between devices, dp_shifts(): got.append(lax.ppermute(parts[(my_dp + shift) % n_dp], 'dp', pairs))  10.7 us
    all_to_all x1, starting transfers between devices, layer(): lax.all_to_all(act, 'ep', split_axis=0, concat_axis=0, tiled=True)  8.6 us
    all_to_all x1, starting transfers between devices, layer(): lax.all_to_all(send_tokens, 'ep', split_axis=0, concat_axis=0, tiled=True)  8.49 us
  transfers between devices with their start and end apart: 7, of which 3 were waited for; matrix products, arithmetic and copies ran while one was open for 11% of the time, Pallas kernels for 0%

profile of v6, /device:TPU:1, one launch (start us, length us, event | category | flops | bytes accessed | tf_op | source)
XLA Modules:
  0.0 231.7 jit_solution(4493522255794284508)
XLA Ops:
  7.2 0.0 copy-start
  7.2 3.9 %reshape_squeeze.4 = bf16[512,7,256]{2,1,0:T(8,128)(2,1)} reshape(bf16[1,3584,256]{2,1,0:T(8,128)(2,1)} %param.10) | data formatting | bytes 3670016 | tf_op jit(solution)/shard_map/reshape;squeeze | solution.py:56
  11.1 22.2 %all-to-all-start = ((bf16[512,7,256]{2,1,0:T(8,128)(2,1)}), bf16[512,7,256]{2,1,0:T(8,128)(2,1)S(1)}, u32[]{:S(2)}, u32[]{:S(2)}) async-start(bf16[512,7,256]{2,1,0:T(8,128)(2,1)} %reshape_squeeze.4), calls=%async_computation | async-start | bytes 4194304 | tf_op jit(solution)/shard_map/all_to_all | solution.py:57
  33.3 0.1 constant_dynamic-slice_fusion.4
  33.5 3.3 %collective-permute-start = (bf16[2,4,896]{2,1,0:T(4,128)(2,1)S(1)}, bf16[2,4,896]{2,1,0:T(4,128)(2,1)S(1)}, u32[]{:S(2)}, u32[]{:S(2)}) collective-permute-start(bf16[2,4,896]{2,1,0:T(4,128)(2,1)S(1)} %bitcast.74), channel_id=1, source_target_pairs={{0,1},{1,2},{2,3},{3,0},{4,5},{5,6},{6,7},{7,4},{8,9},{9,10},{10,1... | collective-permute-start | bytes 43016 | tf_op jit(solution)/shard_map/ppermute | solution.py:36
  36.8 4.3 %collective-permute-start.1 = (bf16[2,4,896]{2,1,0:T(4,128)(2,1)S(1)}, bf16[2,4,896]{2,1,0:T(4,128)(2,1)S(1)}, u32[]{:S(2)}, u32[]{:S(2)}) collective-permute-start(bf16[2,4,896]{2,1,0:T(4,128)(2,1)S(1)} %bitcast.75), channel_id=1, source_target_pairs={{0,2},{1,3},{2,0},{3,1},{4,6},{5,7},{6,4},{7,5},{8,10},{9,11},{10,... | collective-permute-start | bytes 43016 | tf_op jit(solution)/shard_map/ppermute | solution.py:36
  41.1 3.1 %collective-permute-start.2 = (bf16[2,4,896]{2,1,0:T(4,128)(2,1)S(1)}, bf16[2,4,896]{2,1,0:T(4,128)(2,1)S(1)}, u32[]{:S(2)}, u32[]{:S(2)}) collective-permute-start(bf16[2,4,896]{2,1,0:T(4,128)(2,1)S(1)} %bitcast.76), channel_id=1, source_target_pairs={{0,3},{1,0},{2,1},{3,2},{4,7},{5,4},{6,5},{7,6},{8,11},{9,8},{10,9... | collective-permute-start | bytes 43016 | tf_op jit(solution)/shard_map/ppermute | solution.py:36
  44.2 0.1 copy.26
  44.3 0.1 eq.53
  44.4 0.1 reshape.266
  44.5 0.6 dynamic_slice.13
  46.4 0.1 fusion.2
  46.5 0.2 reduce_window_sum.11
  46.7 0.1 reshape.267
  46.8 0.2 select_reduce_fusion.2
  47.0 1.9 gather_fusion.1
  48.8 0.2 select_reduce_fusion
  49.1 1.4 scatter_custom_fusion
  51.1 0.1 constant_dynamic-slice_fusion
  51.3 0.1 copy.28
  51.4 0.1 copy.29
  51.5 0.1 broadcast_in_dim.68
  51.6 4.0 %fusion = (bf16[3584,256]{1,0:T(8,128)(2,1)}, bf16[3584,256]{1,0:T(8,128)(2,1)}) fusion(bf16[1,3584,256]{2,1,0:T(8,128)(2,1)} %param.10, f32[28,256]{1,0:T(8,128)S(1)} %bitcast.68), kind=kLoop, calls=%fused_computation.8 | loop fusion | flops 5505024 | bytes 5533696 | tf_op jit(solution)/shard_map/convert_element_type | solution.py:64
  55.6 0.0 collective-permute-done
  55.6 0.1 pad_maximum_fusion
  55.7 2.1 gather_fusion.2
  57.7 1.1 reshape.268
  58.9 28.3 %all-to-all-done = bf16[512,7,256]{2,1,0:T(8,128)(2,1)S(1)} async-done(((bf16[512,7,256]{2,1,0:T(8,128)(2,1)}), bf16[512,7,256]{2,1,0:T(8,128)(2,1)S(1)}, u32[]{:S(2)}, u32[]{:S(2)}) %all-to-all-start) | async-done | bytes 1835040 | tf_op jit(solution)/shard_map/all_to_all | solution.py:57
  87.2 8.5 %all-to-all-start.1 = ((bf16[128,4,896]{2,1,0:T(4,128)(2,1)}), bf16[128,4,896]{2,1,0:T(4,128)(2,1)S(1)}, u32[]{:S(2)}, u32[]{:S(2)}) async-start(bf16[128,4,896]{2,1,0:T(4,128)(2,1)} %reshape.268), calls=%async_computation.1 | async-start | bytes 1835008 | tf_op jit(solution)/shard_map/all_to_all | solution.py:80
  95.7 0.0 all-gather.2.cloned.1.call-start
  95.8 3.3 %gather_fusion = s32[512]{0:T(512)S(1)} fusion(s32[128]{0:T(128)S(1)} %get-tuple-element.18, s32[1024]{0:T(1024)S(1)} %pad_clamp_fusion.4), kind=kCustom, calls=%fused_computation | custom fusion | bytes 6144 | tf_op jit(solution)/shard_map/gather | solution.py:83
  99.2 2.8 %gather_fusion.3 = bf16[512,7,256]{2,1,0:T(8,128)(2,1)} fusion(bf16[512,7,256]{2,1,0:T(8,128)(2,1)S(1)} %all-to-all-done, s32[1024]{0:T(1024)S(1)} %pad_clamp_fusion.1), kind=kCustom, calls=%fused_computation.3 | custom fusion | bytes 3672064 | tf_op jit(solution)/shard_map/jit(_take)/gather | solution.py:84
  102.0 2.9 %broadcast_select_fusion = bf16[512,7,256]{2,1,0:T(8,128)(2,1)S(1)} fusion(bf16[512,7,256]{2,1,0:T(8,128)(2,1)} %gather_fusion.3, pred[512]{0:T(512)(128)(4,1)S(1)} %compare_and_fusion), kind=kLoop, calls=%fused_computation.10 | loop fusion | flops 917504 | bytes 3670528 | tf_op jit(solution)/shard_map/jit(_take)/select_n | solution.py:84
  104.9 18.7 %all-to-all-done.1 = bf16[128,4,896]{2,1,0:T(4,128)(2,1)S(1)} async-done(((bf16[128,4,896]{2,1,0:T(4,128)(2,1)}), bf16[128,4,896]{2,1,0:T(4,128)(2,1)S(1)}, u32[]{:S(2)}, u32[]{:S(2)}) %all-to-all-start.1) | async-done | bytes 917536 | tf_op jit(solution)/shard_map/all_to_all | solution.py:80
  123.6 1.1 reshape.269
  124.7 0.0 all-gather.2.cloned.1.call-update
  124.7 65.3 %all_to_all.20 = bf16[512,7,256]{2,1,0:T(8,128)(2,1)} all-to-all(bf16[512,7,256]{2,1,0:T(8,128)(2,1)S(1)} %broadcast_select_fusion), channel_id=1, replica_groups=mesh['ep'=128,'dp'=4] {'ep','dp'}, dimensions={0} | all-to-all | bytes 3670016 | tf_op jit(solution)/shard_map/all_to_all | solution.py:85
  190.1 3.9 %reshape.271 = bf16[3584,256]{1,0:T(8,128)(2,1)} reshape(bf16[512,7,256]{2,1,0:T(8,128)(2,1)} %all_to_all.20) | data formatting | bytes 3670016 | tf_op jit(solution)/shard_map/reshape | solution.py:85
  193.9 3.9 %fusion.19 = f32[512,256]{1,0:T(8,128)S(1)} fusion(bf16[512,3584]{1,0:T(8,128)(2,1)} %all-gather.2.cloned.1.call-done, bf16[3584,256]{1,0:T(8,128)(2,1)} %get-tuple-element.13), kind=kOutput, calls=%fused_computation.79 | convolution fusion | flops 939524096 | bytes 6029312 | tf_op jit(solution)/shard_map/dot_general | solution.py:89
  197.8 0.4 copy-done.7
  198.2 1.1 multiply_convert_fusion
  199.3 0.8 reshape.270
  200.1 8.6 %all-to-all-start.3 = ((bf16[128,4,256]{2,1,0:T(4,128)(2,1)}), bf16[128,4,256]{2,1,0:T(4,128)(2,1)S(1)}, u32[]{:S(2)}, u32[]{:S(2)}) async-start(bf16[128,4,256]{2,1,0:T(4,128)(2,1)} %reshape.270), calls=%async_computation.3 | async-start | bytes 524288 | tf_op jit(solution)/shard_map/all_to_all | solution.py:95
  208.7 0.1 copy.21
  208.8 14.1 %all-to-all-done.3 = bf16[128,4,256]{2,1,0:T(4,128)(2,1)S(1)} async-done(((bf16[128,4,256]{2,1,0:T(4,128)(2,1)}), bf16[128,4,256]{2,1,0:T(4,128)(2,1)S(1)}, u32[]{:S(2)}, u32[]{:S(2)}) %all-to-all-start.3) | async-done | bytes 262176 | tf_op jit(solution)/shard_map/all_to_all | solution.py:95
  222.9 0.1 reshape.272
  223.0 1.2 gather_fusion.4
  224.1 0.8 fusion.1
  (41 shorter events, 0.3 us)
Async XLA Ops:
  7.2 44.0 %copy-start = (f32[128,28,2]{0,2,1:T(2,128)S(1)}, f32[128,28,2]{0,2,1:T(2,128)}, u32[]{:S(2)}) copy-start(f32[128,28,2]{0,2,1:T(2,128)} %param.11) | copy-start | bytes 86020
  11.0 22.2 %copy-start.2 = (bf16[2,4,3584]{2,1,0:T(4,128)(2,1)S(1)}, bf16[2,4,3584]{2,1,0:T(4,128)(2,1)}, u32[]{:S(2)}) copy-start(bf16[2,4,3584]{2,1,0:T(4,128)(2,1)} %param.7) | copy-start | bytes 172036
  11.0 33.1 %copy-start.3 = (s32[2,16,8]{1,2,0:T(8,128)S(1)}, s32[2,16,8]{1,2,0:T(8,128)}, u32[]{:S(2)}) copy-start(s32[2,16,8]{1,2,0:T(8,128)} %param.8) | copy-start | bytes 3076
  11.0 33.4 %copy-start.5 = (s32[128]{0:T(128)S(1)}, s32[128]{0:T(128)}, u32[]{:S(2)}) copy-start(s32[128]{0:T(128)} %param.12) | copy-start | bytes 1540
  11.1 35.7 %copy-start.6 = (s32[128]{0:T(128)S(1)}, s32[128]{0:T(128)}, u32[]{:S(2)}) copy-start(s32[128]{0:T(128)} %param.13) | copy-start | bytes 1540
  11.1 76.2 %all-to-all-start = ((bf16[512,7,256]{2,1,0:T(8,128)(2,1)}), bf16[512,7,256]{2,1,0:T(8,128)(2,1)S(1)}, u32[]{:S(2)}, u32[]{:S(2)}) async-start(bf16[512,7,256]{2,1,0:T(8,128)(2,1)} %reshape_squeeze.4), calls=%async_computation | async-start | bytes 4194304 | tf_op jit(solution)/shard_map/all_to_all | solution.py:57
  33.5 22.1 %collective-permute-start = (bf16[2,4,896]{2,1,0:T(4,128)(2,1)S(1)}, bf16[2,4,896]{2,1,0:T(4,128)(2,1)S(1)}, u32[]{:S(2)}, u32[]{:S(2)}) collective-permute-start(bf16[2,4,896]{2,1,0:T(4,128)(2,1)S(1)} %bitcast.74), channel_id=1, source_target_pairs={{0,1},{1,2},{2,3},{3,0},{4,5},{5,6},{6,7},{7,4},{8,9},{9,10},{10,1... | collective-permute-start | bytes 43016 | tf_op jit(solution)/shard_map/ppermute | solution.py:36
  36.8 18.8 %collective-permute-start.1 = (bf16[2,4,896]{2,1,0:T(4,128)(2,1)S(1)}, bf16[2,4,896]{2,1,0:T(4,128)(2,1)S(1)}, u32[]{:S(2)}, u32[]{:S(2)}) collective-permute-start(bf16[2,4,896]{2,1,0:T(4,128)(2,1)S(1)} %bitcast.75), channel_id=1, source_target_pairs={{0,2},{1,3},{2,0},{3,1},{4,6},{5,7},{6,4},{7,5},{8,10},{9,11},{10,... | collective-permute-start | bytes 43016 | tf_op jit(solution)/shard_map/ppermute | solution.py:36
  41.1 14.5 %collective-permute-start.2 = (bf16[2,4,896]{2,1,0:T(4,128)(2,1)S(1)}, bf16[2,4,896]{2,1,0:T(4,128)(2,1)S(1)}, u32[]{:S(2)}, u32[]{:S(2)}) collective-permute-start(bf16[2,4,896]{2,1,0:T(4,128)(2,1)S(1)} %bitcast.76), channel_id=1, source_target_pairs={{0,3},{1,0},{2,1},{3,2},{4,7},{5,4},{6,5},{7,6},{8,11},{9,8},{10,9... | collective-permute-start | bytes 43016 | tf_op jit(solution)/shard_map/ppermute | solution.py:36
  87.2 36.3 %all-to-all-start.1 = ((bf16[128,4,896]{2,1,0:T(4,128)(2,1)}), bf16[128,4,896]{2,1,0:T(4,128)(2,1)S(1)}, u32[]{:S(2)}, u32[]{:S(2)}) async-start(bf16[128,4,896]{2,1,0:T(4,128)(2,1)} %reshape.268), calls=%async_computation.1 | async-start | bytes 1835008 | tf_op jit(solution)/shard_map/all_to_all | solution.py:80
  95.7 98.2 %all-gather.2.cloned.1.call-start = ((), (), s32[]{:S(2)}) async-start(), calls=%async_computation.4 | async-start | bytes 4587520 | tf_op jit(solution)/shard_map/all_gather | solution.py:88
  193.9 3.9 %copy-start.1 = (bf16[3584,256]{1,0:T(8,128)(2,1)S(1)}, bf16[3584,256]{1,0:T(8,128)(2,1)}, u32[]{:S(2)}) copy-start(bf16[3584,256]{1,0:T(8,128)(2,1)} %get-tuple-element.14) | copy-start | bytes 5505028
  193.9 4.2 %copy-start.7 = (bf16[512,3584]{1,0:T(8,128)(2,1)S(1)}, bf16[512,3584]{1,0:T(8,128)(2,1)}, u32[]{:S(2)}) copy-start(bf16[512,3584]{1,0:T(8,128)(2,1)} %all-gather.2.cloned.1.call-done) | copy-start | bytes 11010052
  198.2 10.5 %copy-start.4 = (f32[2,16,8]{1,2,0:T(8,128)S(1)}, f32[2,16,8]{1,2,0:T(8,128)}, u32[]{:S(2)}) copy-start(f32[2,16,8]{1,2,0:T(8,128)} %param.9) | copy-start | bytes 3076
  200.1 22.8 %all-to-all-start.3 = ((bf16[128,4,256]{2,1,0:T(4,128)(2,1)}), bf16[128,4,256]{2,1,0:T(4,128)(2,1)S(1)}, u32[]{:S(2)}, u32[]{:S(2)}) async-start(bf16[128,4,256]{2,1,0:T(4,128)(2,1)} %reshape.270), calls=%async_computation.3 | async-start | bytes 524288 | tf_op jit(solution)/shard_map/all_to_all | solution.py:95
Sparse Core Ops, SparseCore 0:
  124.8 62.3 all-gather.1

commit v7 on v5

--- a/solution.py
+++ b/solution.py
@@ -52,7 +52,7 @@
     owners = inverse_place(old_expert)
     sources = source_slots(old_expert, new_expert)
 
-    pieces = old_block.reshape(peers, rows // peers, cols)
+    pieces = old_block.reshape(peers, 2, rows * cols // (2 * peers))
     staged = lax.all_to_all(pieces, "ep", split_axis=0, concat_axis=0, tiled=True)
 
     own_scales = scale_table[old_expert[my_slot]]
@@ -79,7 +79,7 @@
     arrived = lax.all_to_all(send_tokens, "ep", split_axis=0, concat_axis=0, tiled=True)
 
     regrouped, arrived = lax.optimization_barrier((jnp.take(staged, sources, axis=0), arrived))
-    new_block = lax.all_to_all(regrouped, "ep", split_axis=0, concat_axis=0, tiled=True).reshape(rows, cols)
+    new_block = lax.all_to_all(regrouped, "ep", split_axis=0, concat_axis=0, tiled=True)
 
     arrived = arrived.reshape(peers * steps * capacity, row_part)
     full = lax.all_gather(arrived, "dp", axis=1, tiled=True)
@@ -90,6 +90,7 @@
     act = act.reshape(peers, steps * capacity, cols)
     act, new_block = lax.optimization_barrier((act, new_block))
     returned = lax.all_to_all(act, "ep", split_axis=0, concat_axis=0, tiled=True)
+    new_block = new_block.reshape(rows, cols)
     returned = returned.reshape(peers * steps * capacity, -1)
     picked = returned[target].astype(jnp.float32).reshape(steps, group_size, top_count, -1)
     combined = jnp.sum(gate_values[:, :, :, None] * picked, axis=2).astype(jnp.bfloat16)

time: 219 us -> 201 us (0.918)
  blocking collectives: 59.2 us -> 0 us
  waiting for transfers between devices: 64.6 us -> 91 us
  starting transfers between devices: 44.5 us -> 53.9 us
  local copies, waits for them, and re-layouts: 21.1 us -> 24 us
  other arithmetic: 7.38 us -> 10.1 us
    all_to_all x1 -> x0, blocking collectives: 59.2 us -> none  [layer(): lax.all_to_all(regrouped, 'ep', split_axis=0, concat_axis=0, tiled=True)]
    all_gather x1, waiting for transfers between devices: 0.01 us -> 35.9 us  [layer(): full = lax.all_gather(arrived, 'dp', axis=1, tiled=True)]
    all_to_all x0 -> x1, starting transfers between devices: none -> 6.97 us  [layer(): lax.all_to_all(regrouped, 'ep', split_axis=0, concat_axis=0, tiled=True)]
    all_to_all x1, waiting for transfers between devices: 23.8 us -> 17.6 us  [layer(): lax.all_to_all(send_tokens, 'ep', split_axis=0, concat_axis=0, tiled=True)]
    all_to_all x1, waiting for transfers between devices: 26.6 us -> 20.9 us  [layer(): lax.all_to_all(pieces, 'ep', split_axis=0, concat_axis=0, tiled=True)]
    all_to_all x0 -> x1, waiting for transfers between devices: none -> 4.62 us  [layer(): lax.all_to_all(regrouped, 'ep', split_axis=0, concat_axis=0, tiled=True)]
    reshape x1 -> x0, local copies, waits for them, and re-layouts: 3.74 us -> none  [layer(): lax.all_to_all(regrouped, 'ep', split_axis=0, concat_axis=0, tiled=True)]
    gather x1, local copies, waits for them, and re-layouts: 2.03 us -> 5.4 us  [layer(): jnp.take(staged, sources, axis=0)]
  transfers between devices with their start and end apart: 7 -> 8, of which waited for: 3 -> 5; matrix products, arithmetic and copies ran while one was open for 9% -> 15% of each run, Pallas kernels for 0% -> 0%
where the time goes in v7:
time: 201 us; the launch traced here: 200 us
  waiting for transfers between devices  91 us (45%)
  starting transfers between devices  53.9 us (27%)
  local copies, waits for them, and re-layouts  24 us (12%)
  between operations  16.4 us (8%)
  other arithmetic  10.1 us (5%)
  matrix products  4.99 us (2%)
    all_gather x1, waiting for transfers between devices, layer(): full = lax.all_gather(arrived, 'dp', axis=1, tiled=True)  35.9 us
    all_to_all x1, waiting for transfers between devices, layer(): lax.all_to_all(pieces, 'ep', split_axis=0, concat_axis=0, tiled=True)  20.9 us
    all_to_all x1, starting transfers between devices, layer(): lax.all_to_all(pieces, 'ep', split_axis=0, concat_axis=0, tiled=True)  18.6 us
    all_to_all x1, waiting for transfers between devices, layer(): lax.all_to_all(send_tokens, 'ep', split_axis=0, concat_axis=0, tiled=True)  17.6 us
    all_to_all x1, waiting for transfers between devices, layer(): lax.all_to_all(act, 'ep', split_axis=0, concat_axis=0, tiled=True)  12 us
    ppermute x3, starting transfers between devices, dp_shifts(): got.append(lax.ppermute(parts[(my_dp + shift) % n_dp], 'dp', pairs))  10.5 us
    all_to_all x1, starting transfers between devices, layer(): lax.all_to_all(act, 'ep', split_axis=0, concat_axis=0, tiled=True)  9.83 us
    all_to_all x1, starting transfers between devices, layer(): lax.all_to_all(send_tokens, 'ep', split_axis=0, concat_axis=0, tiled=True)  7.79 us
  transfers between devices with their start and end apart: 8, of which 5 were waited for; matrix products, arithmetic and copies ran while one was open for 15% of the time, Pallas kernels for 0%

profile of v7, /device:TPU:1, one launch (start us, length us, event | category | flops | bytes accessed | tf_op | source)
XLA Modules:
  0.0 200.4 jit_solution(4845365449002708653)
XLA Ops:
  7.2 0.0 copy-start
  7.2 4.9 %reshape_squeeze.4 = bf16[128,2,3584]{2,1,0:T(2,128)(2,1)} reshape(bf16[1,3584,256]{2,1,0:T(8,128)(2,1)} %param.10) | data formatting | bytes 3670016 | tf_op jit(solution)/shard_map/reshape;squeeze | solution.py:55
  12.1 18.6 %all-to-all-start = ((bf16[128,2,3584]{2,1,0:T(2,128)(2,1)}), bf16[128,2,3584]{2,1,0:T(2,128)(2,1)S(1)}, u32[]{:S(2)}, u32[]{:S(2)}) async-start(bf16[128,2,3584]{2,1,0:T(2,128)(2,1)} %reshape_squeeze.4), calls=%async_computation | async-start | bytes 3670016 | tf_op jit(solution)/shard_map/all_to_all | solution.py:56
  30.7 0.1 constant_dynamic-slice_fusion.3
  30.9 3.1 %collective-permute-start = (bf16[2,4,896]{2,1,0:T(4,128)(2,1)S(1)}, bf16[2,4,896]{2,1,0:T(4,128)(2,1)S(1)}, u32[]{:S(2)}, u32[]{:S(2)}) collective-permute-start(bf16[2,4,896]{2,1,0:T(4,128)(2,1)S(1)} %bitcast.73), channel_id=1, source_target_pairs={{0,1},{1,2},{2,3},{3,0},{4,5},{5,6},{6,7},{7,4},{8,9},{9,10},{10,1... | collective-permute-start | bytes 43016 | tf_op jit(solution)/shard_map/ppermute | solution.py:36
  34.0 4.4 %collective-permute-start.1 = (bf16[2,4,896]{2,1,0:T(4,128)(2,1)S(1)}, bf16[2,4,896]{2,1,0:T(4,128)(2,1)S(1)}, u32[]{:S(2)}, u32[]{:S(2)}) collective-permute-start(bf16[2,4,896]{2,1,0:T(4,128)(2,1)S(1)} %bitcast.74), channel_id=1, source_target_pairs={{0,2},{1,3},{2,0},{3,1},{4,6},{5,7},{6,4},{7,5},{8,10},{9,11},{10,... | collective-permute-start | bytes 43016 | tf_op jit(solution)/shard_map/ppermute | solution.py:36
  38.4 3.1 %collective-permute-start.2 = (bf16[2,4,896]{2,1,0:T(4,128)(2,1)S(1)}, bf16[2,4,896]{2,1,0:T(4,128)(2,1)S(1)}, u32[]{:S(2)}, u32[]{:S(2)}) collective-permute-start(bf16[2,4,896]{2,1,0:T(4,128)(2,1)S(1)} %bitcast.75), channel_id=1, source_target_pairs={{0,3},{1,0},{2,1},{3,2},{4,7},{5,4},{6,5},{7,6},{8,11},{9,8},{10,9... | collective-permute-start | bytes 43016 | tf_op jit(solution)/shard_map/ppermute | solution.py:36
  41.5 0.1 copy.26
  41.6 0.1 eq.51
  41.7 0.1 reshape.195
  41.8 0.6 dynamic_slice.13
  43.7 0.1 fusion.2
  43.8 0.2 reduce_window_sum.11
  44.0 0.1 reshape.196
  44.1 0.2 select_reduce_fusion.2
  44.3 1.9 gather_fusion
  46.1 0.2 select_reduce_fusion
  46.4 1.4 scatter_custom_fusion
  48.4 0.1 constant_dynamic-slice_fusion.4
  48.6 0.1 copy.28
  48.7 0.1 copy.29
  48.8 0.1 broadcast_in_dim.64
  48.9 4.0 %fusion = (bf16[3584,256]{1,0:T(8,128)(2,1)}, bf16[3584,256]{1,0:T(8,128)(2,1)}) fusion(bf16[1,3584,256]{2,1,0:T(8,128)(2,1)} %param.10, f32[28,256]{1,0:T(8,128)S(1)} %bitcast.67), kind=kLoop, calls=%fused_computation.7 | loop fusion | flops 5505024 | bytes 5533696 | tf_op jit(solution)/shard_map/convert_element_type | solution.py:63
  52.9 0.1 pad_maximum_fusion
  53.0 2.1 %gather_fusion.1 = bf16[512,896]{1,0:T(8,128)(2,1)S(1)} fusion(bf16[32,896]{1,0:T(8,128)(2,1)S(1)} %reshape.194, s32[1024]{0:T(1024)S(1)} %pad_clamp_fusion.2), kind=kCustom, calls=%fused_computation.1 | custom fusion | bytes 1837056 | tf_op jit(solution)/shard_map/gather | solution.py:77
  55.0 1.2 reshape.197
  56.2 20.9 %all-to-all-done = bf16[128,2,3584]{2,1,0:T(2,128)(2,1)S(1)} async-done(((bf16[128,2,3584]{2,1,0:T(2,128)(2,1)}), bf16[128,2,3584]{2,1,0:T(2,128)(2,1)S(1)}, u32[]{:S(2)}, u32[]{:S(2)}) %all-to-all-start) | async-done | bytes 1835040 | tf_op jit(solution)/shard_map/all_to_all | solution.py:56
  77.1 7.8 %all-to-all-start.1 = ((bf16[128,4,896]{2,1,0:T(4,128)(2,1)}), bf16[128,4,896]{2,1,0:T(4,128)(2,1)S(1)}, u32[]{:S(2)}, u32[]{:S(2)}) async-start(bf16[128,4,896]{2,1,0:T(4,128)(2,1)} %reshape.197), calls=%async_computation.1 | async-start | bytes 1835008 | tf_op jit(solution)/shard_map/all_to_all | solution.py:79
  84.9 0.2 all-gather.2.cloned.1.call-start
  85.2 5.4 %gather_fusion.2 = bf16[128,2,3584]{2,1,0:T(2,128)(2,1)} fusion(bf16[128,2,3584]{2,1,0:T(2,128)(2,1)S(1)} %all-to-all-done, s32[1024]{0:T(1024)S(1)} %pad_clamp_fusion.1), kind=kCustom, calls=%fused_computation.2 | custom fusion | bytes 3670528 | tf_op jit(solution)/shard_map/jit(_take)/gather | solution.py:81
  90.6 4.5 %broadcast_select_fusion = bf16[128,2,3584]{2,1,0:T(2,128)(2,1)} fusion(bf16[128,2,3584]{2,1,0:T(2,128)(2,1)} %gather_fusion.2, pred[128]{0:T(512)(128)(4,1)S(1)} %compare_and_fusion), kind=kLoop, calls=%fused_computation.9 | loop fusion | flops 917504 | bytes 3670144 | tf_op jit(solution)/shard_map/jit(_take)/select_n | solution.py:81
  95.1 17.6 %all-to-all-done.1 = bf16[128,4,896]{2,1,0:T(4,128)(2,1)S(1)} async-done(((bf16[128,4,896]{2,1,0:T(4,128)(2,1)}), bf16[128,4,896]{2,1,0:T(4,128)(2,1)S(1)}, u32[]{:S(2)}, u32[]{:S(2)}) %all-to-all-start.1) | async-done | bytes 917536 | tf_op jit(solution)/shard_map/all_to_all | solution.py:79
  112.7 1.1 reshape.198
  113.9 0.0 all-gather.2.cloned.1.call-update
  113.9 7.0 %all-to-all-start.2 = ((bf16[128,2,3584]{2,1,0:T(2,128)(2,1)}), bf16[128,2,3584]{2,1,0:T(2,128)(2,1)S(1)}, u32[]{:S(2)}, u32[]{:S(2)}) async-start(bf16[128,2,3584]{2,1,0:T(2,128)(2,1)} %broadcast_select_fusion), calls=%async_computation.2 | async-start | bytes 3670016 | tf_op jit(solution)/shard_map/all_to_all | solution.py:82
  120.9 35.9 %all-gather.2.cloned.1.call-done = bf16[512,3584]{1,0:T(8,128)(2,1)} async-done(((bf16[512,896]{1,0:T(8,128)(2,1)}), bf16[512,3584]{1,0:T(8,128)(2,1)}) %all-gather.2.cloned.1.call-update) | async-done | bytes 3670032 | tf_op jit(solution)/shard_map/all_gather | solution.py:85
  156.8 3.9 %fusion.15 = f32[512,256]{1,0:T(8,128)S(1)} fusion(bf16[512,3584]{1,0:T(8,128)(2,1)} %all-gather.2.cloned.1.call-done, bf16[3584,256]{1,0:T(8,128)(2,1)} %get-tuple-element.13), kind=kOutput, calls=%fused_computation.64 | convolution fusion | flops 939524096 | bytes 6029312 | tf_op jit(solution)/shard_map/dot_general | solution.py:86
  160.7 0.4 copy-done.7
  161.0 1.1 multiply_convert_fusion
  162.2 0.8 reshape.199
  162.9 4.6 %all-to-all-done.2 = bf16[128,2,3584]{2,1,0:T(2,128)(2,1)S(1)} async-done(((bf16[128,2,3584]{2,1,0:T(2,128)(2,1)}), bf16[128,2,3584]{2,1,0:T(2,128)(2,1)S(1)}, u32[]{:S(2)}, u32[]{:S(2)}) %all-to-all-start.2) | async-done | bytes 1835040 | tf_op jit(solution)/shard_map/all_to_all | solution.py:82
  167.5 9.8 %all-to-all-start.3 = ((bf16[128,4,256]{2,1,0:T(4,128)(2,1)}), bf16[128,4,256]{2,1,0:T(4,128)(2,1)S(1)}, u32[]{:S(2)}, u32[]{:S(2)}) async-start(bf16[128,4,256]{2,1,0:T(4,128)(2,1)} %reshape.199), calls=%async_computation.3 | async-start | bytes 524288 | tf_op jit(solution)/shard_map/all_to_all | solution.py:92
  177.4 0.1 copy.21
  177.5 2.1 %broadcast_in_dim_reshape.2 = bf16[1,3584,256]{2,1,0:T(8,128)(2,1)} reshape(bf16[128,2,3584]{2,1,0:T(2,128)(2,1)S(1)} %all-to-all-done.2) | data formatting | bytes 3670016 | tf_op jit(solution)/shard_map/broadcast_in_dim;reshape | solution.py:97
  179.6 12.0 %all-to-all-done.3 = bf16[128,4,256]{2,1,0:T(4,128)(2,1)S(1)} async-done(((bf16[128,4,256]{2,1,0:T(4,128)(2,1)}), bf16[128,4,256]{2,1,0:T(4,128)(2,1)S(1)}, u32[]{:S(2)}, u32[]{:S(2)}) %all-to-all-start.3) | async-done | bytes 262176 | tf_op jit(solution)/shard_map/all_to_all | solution.py:92
  191.6 0.1 reshape.200
  191.7 1.2 gather_fusion.3
  192.8 0.8 fusion.1
  (38 shorter events, 0.2 us)
Async XLA Ops:
  7.2 41.3 %copy-start = (f32[128,28,2]{0,2,1:T(2,128)S(1)}, f32[128,28,2]{0,2,1:T(2,128)}, u32[]{:S(2)}) copy-start(f32[128,28,2]{0,2,1:T(2,128)} %param.11) | copy-start | bytes 86020
  12.1 18.6 %copy-start.2 = (bf16[2,4,3584]{2,1,0:T(4,128)(2,1)S(1)}, bf16[2,4,3584]{2,1,0:T(4,128)(2,1)}, u32[]{:S(2)}) copy-start(bf16[2,4,3584]{2,1,0:T(4,128)(2,1)} %param.7) | copy-start | bytes 172036
  12.1 29.4 %copy-start.3 = (s32[2,16,8]{1,2,0:T(8,128)S(1)}, s32[2,16,8]{1,2,0:T(8,128)}, u32[]{:S(2)}) copy-start(s32[2,16,8]{1,2,0:T(8,128)} %param.8) | copy-start | bytes 3076
  12.1 29.7 %copy-start.5 = (s32[128]{0:T(128)S(1)}, s32[128]{0:T(128)}, u32[]{:S(2)}) copy-start(s32[128]{0:T(128)} %param.12) | copy-start | bytes 1540
  12.1 32.0 %copy-start.6 = (s32[128]{0:T(128)S(1)}, s32[128]{0:T(128)}, u32[]{:S(2)}) copy-start(s32[128]{0:T(128)} %param.13) | copy-start | bytes 1540
  12.1 65.0 %all-to-all-start = ((bf16[128,2,3584]{2,1,0:T(2,128)(2,1)}), bf16[128,2,3584]{2,1,0:T(2,128)(2,1)S(1)}, u32[]{:S(2)}, u32[]{:S(2)}) async-start(bf16[128,2,3584]{2,1,0:T(2,128)(2,1)} %reshape_squeeze.4), calls=%async_computation | async-start | bytes 3670016 | tf_op jit(solution)/shard_map/all_to_all | solution.py:56
  30.9 22.0 %collective-permute-start = (bf16[2,4,896]{2,1,0:T(4,128)(2,1)S(1)}, bf16[2,4,896]{2,1,0:T(4,128)(2,1)S(1)}, u32[]{:S(2)}, u32[]{:S(2)}) collective-permute-start(bf16[2,4,896]{2,1,0:T(4,128)(2,1)S(1)} %bitcast.73), channel_id=1, source_target_pairs={{0,1},{1,2},{2,3},{3,0},{4,5},{5,6},{6,7},{7,4},{8,9},{9,10},{10,1... | collective-permute-start | bytes 43016 | tf_op jit(solution)/shard_map/ppermute | solution.py:36
  34.0 18.9 %collective-permute-start.1 = (bf16[2,4,896]{2,1,0:T(4,128)(2,1)S(1)}, bf16[2,4,896]{2,1,0:T(4,128)(2,1)S(1)}, u32[]{:S(2)}, u32[]{:S(2)}) collective-permute-start(bf16[2,4,896]{2,1,0:T(4,128)(2,1)S(1)} %bitcast.74), channel_id=1, source_target_pairs={{0,2},{1,3},{2,0},{3,1},{4,6},{5,7},{6,4},{7,5},{8,10},{9,11},{10,... | collective-permute-start | bytes 43016 | tf_op jit(solution)/shard_map/ppermute | solution.py:36
  38.4 14.5 %collective-permute-start.2 = (bf16[2,4,896]{2,1,0:T(4,128)(2,1)S(1)}, bf16[2,4,896]{2,1,0:T(4,128)(2,1)S(1)}, u32[]{:S(2)}, u32[]{:S(2)}) collective-permute-start(bf16[2,4,896]{2,1,0:T(4,128)(2,1)S(1)} %bitcast.75), channel_id=1, source_target_pairs={{0,3},{1,0},{2,1},{3,2},{4,7},{5,4},{6,5},{7,6},{8,11},{9,8},{10,9... | collective-permute-start | bytes 43016 | tf_op jit(solution)/shard_map/ppermute | solution.py:36
  77.1 35.6 %all-to-all-start.1 = ((bf16[128,4,896]{2,1,0:T(4,128)(2,1)}), bf16[128,4,896]{2,1,0:T(4,128)(2,1)S(1)}, u32[]{:S(2)}, u32[]{:S(2)}) async-start(bf16[128,4,896]{2,1,0:T(4,128)(2,1)} %reshape.197), calls=%async_computation.1 | async-start | bytes 1835008 | tf_op jit(solution)/shard_map/all_to_all | solution.py:79
  84.9 71.9 %all-gather.2.cloned.1.call-start = ((), (), s32[]{:S(2)}) async-start(), calls=%async_computation.4 | async-start | bytes 4587520 | tf_op jit(solution)/shard_map/all_gather | solution.py:85
  113.9 53.6 %all-to-all-start.2 = ((bf16[128,2,3584]{2,1,0:T(2,128)(2,1)}), bf16[128,2,3584]{2,1,0:T(2,128)(2,1)S(1)}, u32[]{:S(2)}, u32[]{:S(2)}) async-start(bf16[128,2,3584]{2,1,0:T(2,128)(2,1)} %broadcast_select_fusion), calls=%async_computation.2 | async-start | bytes 3670016 | tf_op jit(solution)/shard_map/all_to_all | solution.py:82
  156.8 3.9 %copy-start.1 = (bf16[3584,256]{1,0:T(8,128)(2,1)S(1)}, bf16[3584,256]{1,0:T(8,128)(2,1)}, u32[]{:S(2)}) copy-start(bf16[3584,256]{1,0:T(8,128)(2,1)} %get-tuple-element.14) | copy-start | bytes 5505028
  156.8 4.2 %copy-start.7 = (bf16[512,3584]{1,0:T(8,128)(2,1)S(1)}, bf16[512,3584]{1,0:T(8,128)(2,1)}, u32[]{:S(2)}) copy-start(bf16[512,3584]{1,0:T(8,128)(2,1)} %all-gather.2.cloned.1.call-done) | copy-start | bytes 11010052
  161.0 16.4 %copy-start.4 = (f32[2,16,8]{1,2,0:T(8,128)S(1)}, f32[2,16,8]{1,2,0:T(8,128)}, u32[]{:S(2)}) copy-start(f32[2,16,8]{1,2,0:T(8,128)} %param.9) | copy-start | bytes 3076
  167.5 24.1 %all-to-all-start.3 = ((bf16[128,4,256]{2,1,0:T(4,128)(2,1)}), bf16[128,4,256]{2,1,0:T(4,128)(2,1)S(1)}, u32[]{:S(2)}, u32[]{:S(2)}) async-start(bf16[128,4,256]{2,1,0:T(4,128)(2,1)} %reshape.199), calls=%async_computation.3 | async-start | bytes 524288 | tf_op jit(solution)/shard_map/all_to_all | solution.py:92
Sparse Core Ops, SparseCore 0:
  114.0 42.6 all-gather.1
